TPU v7x, 256 devices: a whole 4x4x8 slice. The times are simulated.
256 devices in a mesh: row: 8 (over z), col: 32 (over y, x, core).
Axes of the slice: x: 4, y: 4, z: 8, core: 2. Of those that a mesh axis runs over, the one named last changes fastest.
Arguments:
- tokens: bfloat16 [512, 8192], P('col', 'row'), may hold values from -6 to 6
- cotangent: bfloat16 [512, 8192], P('col', 'row'), may hold values from -6 to 6
- w_gate: bfloat16 [8192, 16384], P('row', 'col'), may hold values from -0.09375 to 0.09375
- w_up: bfloat16 [8192, 16384], P('row', 'col'), may hold values from -0.09375 to 0.09375
- w_down: bfloat16 [16384, 8192], P('col', 'row'), may hold values from -0.0625 to 0.0625
- order_gate: int32 [2048], replicated, may hold values from 0 to 2047, each once
- order_up: int32 [2048], replicated, may hold values from 0 to 2047, each once
- order_down: int32 [2048], replicated, may hold values from 0 to 2047, each once
Outputs:
- output: bfloat16 [512, 8192], P('col', 'row')
- input_grad: bfloat16 [512, 8192], P('col', 'row')
- gate_weight_grad: float32 [8192, 16384], P('row', 'col')
- up_weight_grad: float32 [8192, 16384], P('row', 'col')
- down_weight_grad: float32 [16384, 8192], P('col', 'row')
Inputs may be any that keep to these rules, and one draw needn't show every extreme that they name: `order_gate`: each of the 2048 block numbers appears exactly once. `order_up`: each of the 2048 block numbers appears exactly once. `order_down`: each of the 2048 block numbers appears exactly once.
All inputs are finite; a program needn't handle non-finite values.
Results may differ from a plain program's by a relative error of at most 0.0049.
Values may be sent and summed in bfloat16 or wider, within the bound.
No kernel may reach another device: no remote copies, remote signals or barrier semaphores. Data moves between devices by JAX's collectives and lax.ppermute only.
A program may use at most 64 MiB of HBM per device.

v0:
```python
import jax
import jax.numpy as jnp
from jax import lax
from jax.sharding import PartitionSpec as P

BLOCK = 256


def kept_table(order, row_first, col_first, row_count, col_count, stride):
    kept_count = order.shape[0] // 2
    row_ids = row_first + jnp.arange(row_count, dtype=jnp.int32)
    col_ids = col_first + jnp.arange(col_count, dtype=jnp.int32)
    block_ids = row_ids[:, None] * stride + col_ids[None, :]
    return jnp.any(block_ids[:, :, None] == order[:kept_count][None, None, :], axis=2)


def expand_mask(kept_mask):
    row_count, col_count = kept_mask.shape
    spread = jnp.broadcast_to(kept_mask[:, None, :, None], (row_count, BLOCK, col_count, BLOCK))
    return spread.reshape(row_count * BLOCK, col_count * BLOCK)


def dense_apply(left_operand, right_operand, kept_mask, product_kind):
    full_mask = expand_mask(kept_mask)
    if product_kind == "forward":
        masked = right_operand * full_mask.astype(right_operand.dtype)
        return jnp.dot(left_operand, masked, preferred_element_type=jnp.float32)
    if product_kind == "transposed":
        masked = right_operand * full_mask.astype(right_operand.dtype)
        return lax.dot_general(
            left_operand, masked, (((1,), (1,)), ((), ())), preferred_element_type=jnp.float32
        )
    product = lax.dot_general(
        left_operand, right_operand, (((0,), (0,)), ((), ())), preferred_element_type=jnp.float32
    )
    return product * full_mask.astype(jnp.float32)


def apply_blocks(left_operand, right_operand, kept_mask, product_kind):
    return dense_apply(left_operand, right_operand, kept_mask, product_kind)


def on_device(tokens, cotangent, w_gate, w_up, w_down, order_gate, order_up, order_down):
    rows_here = w_gate.shape[0] // BLOCK
    cols_here = w_gate.shape[1] // BLOCK
    row_start = lax.axis_index("row") * rows_here
    col_start = lax.axis_index("col") * cols_here
    width_blocks = rows_here * lax.axis_size("row")
    hidden_blocks = cols_here * lax.axis_size("col")
    keep_gate = kept_table(order_gate, row_start, col_start, rows_here, cols_here, hidden_blocks)
    keep_up = kept_table(order_up, row_start, col_start, rows_here, cols_here, hidden_blocks)
    keep_down = kept_table(order_down, col_start, row_start, cols_here, rows_here, width_blocks)
    tokens_all = lax.all_gather(tokens, "col", axis=0, tiled=True)
    gate_term = apply_blocks(tokens_all, w_gate, keep_gate, "forward")
    up_term = apply_blocks(tokens_all, w_up, keep_up, "forward")
    gate, up = (
        lax.psum_scatter(gate_term, "row", scatter_dimension=0, tiled=True),
        lax.psum_scatter(up_term, "row", scatter_dimension=0, tiled=True),
    )
    sigmoid_gate = jax.nn.sigmoid(gate)
    activation = gate * sigmoid_gate
    hidden = (activation * up).astype(jnp.bfloat16)
    hidden_all = lax.all_gather(hidden, "row", axis=0, tiled=True)
    output_term = apply_blocks(hidden_all, w_down, keep_down, "forward")
    output = lax.psum_scatter(output_term, "col", scatter_dimension=0, tiled=True).astype(
        jnp.bfloat16
    )
    cotangent_all = lax.all_gather(cotangent, "col", axis=0, tiled=True)
    hidden_term = apply_blocks(cotangent_all, w_down, keep_down, "transposed")
    hidden_grad = lax.psum_scatter(hidden_term, "row", scatter_dimension=0, tiled=True)
    gate_grad = (hidden_grad * up * sigmoid_gate * (1.0 + gate * (1.0 - sigmoid_gate))).astype(
        jnp.bfloat16
    )
    up_grad = (hidden_grad * activation).astype(jnp.bfloat16)
    gate_grad_all, up_grad_all = (
        lax.all_gather(gate_grad, "row", axis=0, tiled=True),
        lax.all_gather(up_grad, "row", axis=0, tiled=True),
    )
    down_weight_grad = apply_blocks(hidden_all, cotangent_all, keep_down, "weights")
    gate_weight_grad = apply_blocks(tokens_all, gate_grad_all, keep_gate, "weights")
    up_weight_grad = apply_blocks(tokens_all, up_grad_all, keep_up, "weights")
    through_gate = apply_blocks(gate_grad_all, w_gate, keep_gate, "transposed")
    through_up = apply_blocks(up_grad_all, w_up, keep_up, "transposed")
    gate_share = lax.psum_scatter(through_gate, "col", scatter_dimension=0, tiled=True)
    up_share = lax.psum_scatter(through_up, "col", scatter_dimension=0, tiled=True)
    input_grad = gate_share + up_share
    return (
        output,
        input_grad.astype(jnp.bfloat16),
        gate_weight_grad,
        up_weight_grad,
        down_weight_grad,
    )


def solution(mesh):
    placed = (
        P("col", "row"),
        P("col", "row"),
        P("row", "col"),
        P("row", "col"),
        P("col", "row"),
        P(),
        P(),
        P(),
    )
    return jax.shard_map(
        on_device,
        mesh=mesh,
        in_specs=placed,
        out_specs=(
            P("col", "row"),
            P("col", "row"),
            P("row", "col"),
            P("row", "col"),
            P("col", "row"),
        ),
        check_vma=False,
    )
```

profile of v0, /device:TPU:1, one launch (start us, length us, event | category | flops | bytes accessed | tf_op | source)
XLA Modules:
  0.0 445.2 jit_solution(2200922386354329133)
XLA Ops:
  10.3 51.9 %all-gather.5.cloned.1.call-done = bf16[512,1024]{1,0:T(8,128)(2,1)} async-done(((bf16[16,1024]{1,0:T(8,128)(2,1)}), bf16[512,1024]{1,0:T(8,128)(2,1)}) %all-gather.5.cloned.1.call-update) | async-done | bytes 1048592 | tf_op jit(solution)/shard_map/all_gather | solution.py:68
  62.3 2.3 convolution_bitcast_fusion
  67.5 44.4 %all-gather.3.cloned.1.call-done = bf16[512,1024]{1,0:T(8,128)(2,1)} async-done(((bf16[16,1024]{1,0:T(8,128)(2,1)}), bf16[512,1024]{1,0:T(8,128)(2,1)}) %all-gather.3.cloned.1.call-update) | async-done | bytes 1048592 | tf_op jit(solution)/shard_map/all_gather | solution.py:53
  111.8 2.0 convolution_bitcast_fusion.2
  115.8 1.7 copy.34
  117.5 2.9 convolution_bitcast_fusion.1
  120.5 2.5 copy.44
  123.1 25.0 %reduce-scatter.20.cloned.1.call-done = f32[64,512]{1,0:T(8,128)} async-done(((f32[512,512]{1,0:T(8,128)}), f32[64,512]{1,0:T(8,128)}) %reduce-scatter.20.cloned.1.call-update) | async-done | bytes 131088 | tf_op jit(solution)/shard_map/reduce_scatter | solution.py:70
  148.1 40.6 %reduce-scatter.16.cloned.1.call-done = f32[64,512]{1,0:T(8,128)} async-done(((f32[512,512]{1,0:T(8,128)}), f32[64,512]{1,0:T(8,128)}) %reduce-scatter.16.cloned.1.call-update) | async-done | bytes 131088 | tf_op jit(solution)/shard_map/reduce_scatter | solution.py:57
  188.7 40.0 %reduce-scatter.18.cloned.1.call-done = f32[64,512]{1,0:T(8,128)} async-done(((f32[512,512]{1,0:T(8,128)}), f32[64,512]{1,0:T(8,128)}) %reduce-scatter.18.cloned.1.call-update) | async-done | bytes 131088 | tf_op jit(solution)/shard_map/reduce_scatter | solution.py:58
  229.9 19.4 %all_gather.16 = bf16[512,512]{1,0:T(8,128)(2,1)S(1)} all-gather(bf16[64,512]{1,0:T(8,128)(2,1)S(1)} %get-tuple-element.29), channel_id=1, replica_groups=mesh['row'=8,'col'=32] {'row'}, dimensions={0}, use_global_device_ids=true | all-gather | bytes 589824 | tf_op jit(solution)/shard_map/all_gather | solution.py:63
  249.2 3.3 fusion.1
  252.6 19.8 %all_gather.18 = bf16[512,512]{1,0:T(8,128)(2,1)S(1)} all-gather(bf16[64,512]{1,0:T(8,128)(2,1)S(1)} %get-tuple-element.28), channel_id=1, replica_groups=mesh['row'=8,'col'=32] {'row'}, dimensions={0}, use_global_device_ids=true | all-gather | bytes 589824 | tf_op jit(solution)/shard_map/all_gather | solution.py:76
  272.3 19.8 %all_gather.19 = bf16[512,512]{1,0:T(8,128)(2,1)S(1)} all-gather(bf16[64,512]{1,0:T(8,128)(2,1)S(1)} %get-tuple-element.27), channel_id=1, replica_groups=mesh['row'=8,'col'=32] {'row'}, dimensions={0}, use_global_device_ids=true | all-gather | bytes 589824 | tf_op jit(solution)/shard_map/all_gather | solution.py:77
  292.2 2.0 fusion.9
  294.2 2.1 convolution_add_fusion
  297.7 2.0 bitcast_select_fusion.1
  299.7 3.0 copy.40
  302.7 2.0 bitcast_select_fusion
  304.8 3.0 copy.41
  307.8 2.0 convolution_select_fusion
  309.8 37.3 %reduce-scatter.12.cloned.1.call-done = f32[16,1024]{1,0:T(8,128)} async-done(((f32[512,1024]{1,0:T(8,128)}), f32[16,1024]{1,0:T(8,128)}) %reduce-scatter.12.cloned.1.call-update) | async-done | bytes 65552 | tf_op jit(solution)/shard_map/reduce_scatter | solution.py:65
  348.5 88.4 %reduce-scatter.14.cloned.1.call-done = f32[16,1024]{1,0:T(8,128)} async-done(((f32[512,1024]{1,0:T(8,128)}), f32[16,1024]{1,0:T(8,128)}) %reduce-scatter.14.cloned.1.call-update) | async-done | bytes 65552 | tf_op jit(solution)/shard_map/reduce_scatter | solution.py:84
  436.9 1.5 convert_element_type.28
  (60 shorter events, 12.0 us)
Async XLA Ops:
  7.2 55.1 %all-gather.5.cloned.1.call-start = ((), (), s32[]{:S(2)}) async-start(), calls=%async_computation.7 | async-start | bytes 1081344 | tf_op jit(solution)/shard_map/all_gather | solution.py:68
  7.9 103.9 %all-gather.3.cloned.1.call-start = ((), (), s32[]{:S(2)}) async-start(), calls=%async_computation.5 | async-start | bytes 1081344 | tf_op jit(solution)/shard_map/all_gather | solution.py:53
  8.6 139.4 %reduce-scatter.20.cloned.1.call-start = ((), (), s32[]{:S(2)}) async-start(), calls=%async_computation.11 | async-start | bytes 1179648 | tf_op jit(solution)/shard_map/reduce_scatter | solution.py:70
  10.3 238.9 %copy-start.5 = (pred[64,8,4,256]{3,1,2,0:T(8,128)(4,1)}, pred[64,8,4,256]{3,1,2,0:T(8,128)(4,1)S(1)}, u32[]{:S(2)}) copy-start(pred[64,8,4,256]{3,1,2,0:T(8,128)(4,1)S(1)} %copy.50) | copy-start | bytes 1572868
  64.6 1.5 slice-start
  64.6 1.5 slice-start.1
  64.6 2.3 copy-start.9
  65.9 122.8 %reduce-scatter.16.cloned.1.call-start = ((), (), s32[]{:S(2)}) async-start(), calls=%async_computation.9 | async-start | bytes 1179648 | tf_op jit(solution)/shard_map/reduce_scatter | solution.py:57
  66.9 46.9 %copy-start.7 = (pred[64,8,4,256]{3,1,2,0:T(8,128)(4,1)}, pred[64,8,4,256]{3,1,2,0:T(8,128)(4,1)S(1)}, u32[]{:S(2)}) copy-start(pred[64,8,4,256]{3,1,2,0:T(8,128)(4,1)S(1)} %copy.48) | copy-start | bytes 1572868
  115.2 113.6 %reduce-scatter.18.cloned.1.call-start = ((), (), s32[]{:S(2)}) async-start(), calls=%async_computation.10 | async-start | bytes 1179648 | tf_op jit(solution)/shard_map/reduce_scatter | solution.py:58
  115.8 4.6 %copy-start = (pred[64,8,4,256]{3,1,2,0:T(8,128)(4,1)}, pred[64,8,4,256]{3,1,2,0:T(8,128)(4,1)S(1)}, u32[]{:S(2)}) copy-start(pred[64,8,4,256]{3,1,2,0:T(8,128)(4,1)S(1)} %copy.49) | copy-start | bytes 1572868
  123.0 224.1 %reduce-scatter.12.cloned.1.call-start = ((), (), s32[]{:S(2)}) async-start(), calls=%async_computation.6 | async-start | bytes 2162688 | tf_op jit(solution)/shard_map/reduce_scatter | solution.py:65
  252.5 184.4 %reduce-scatter.14.cloned.1.call-start = ((), (), s32[]{:S(2)}) async-start(), calls=%async_computation.8 | async-start | bytes 2162688 | tf_op jit(solution)/shard_map/reduce_scatter | solution.py:84
  292.2 2.0 copy-start.3
  292.2 2.0 copy-start.1
  296.3 1.0 copy-start.8
  296.3 1.4 copy-start.11
  299.7 3.0 copy-start.2
  299.7 3.0 copy-start.4
  304.8 3.0 copy-start.6
  304.8 3.0 copy-start.10
Sparse Core Ops, SparseCore 0:
  10.5 51.7 all-gather.4
  64.8 46.9 all-gather.2
  114.9 33.0 reduce-scatter.19
  151.0 37.6 reduce-scatter.15
  191.1 37.6 reduce-scatter.17
  252.7 94.3 reduce-scatter.11
  350.9 85.9 reduce-scatter.13
where the time goes:
time: 446 us; the launch traced here: 445 us
  waiting for transfers between devices  329 us (74%)
  blocking collectives  58.9 us (13%)
  matrix products  20.7 us (5%)
  local copies, waits for them, and re-layouts  17.3 us (4%)
  between operations  14.3 us (3%)
  other arithmetic  4.62 us (1%)
    reduce_scatter x1, waiting for transfers between devices, on_device(): lax.psum_scatter(through_gate, 'col', scatter_dimension=0, tiled=True)  88.4 us
    all_gather x1, waiting for transfers between devices, on_device(): cotangent_all = lax.all_gather(cotangent, 'col', axis=0, tiled=True)  51.9 us
    all_gather x1, waiting for transfers between devices, on_device(): tokens_all = lax.all_gather(tokens, 'col', axis=0, tiled=True)  44.4 us
    reduce_scatter x1, waiting for transfers between devices, on_device(): lax.psum_scatter(gate_term, 'row', scatter_dimension=0, tiled=True)  40.6 us
    reduce_scatter x1, waiting for transfers between devices, on_device(): lax.psum_scatter(up_term, 'row', scatter_dimension=0, tiled=True)  40 us
    reduce_scatter x1, waiting for transfers between devices, on_device(): lax.psum_scatter(output_term, 'col', scatter_dimension=0, tiled=True)  37.3 us
    reduce_scatter x1, waiting for transfers between devices, on_device(): lax.psum_scatter(hidden_term, 'row', scatter_dimension=0, tiled=True)  25 us
    all_gather x1, blocking collectives, on_device(): lax.all_gather(up_grad, 'row', axis=0, tiled=True)  19.8 us
  transfers between devices with their start and end apart: 7, of which 7 were waited for; matrix products, arithmetic and copies ran while one was open for 8% of the time, Pallas kernels for 0%

commit v1 on v0

--- a/solution.py
+++ b/solution.py
@@ -40,6 +40,19 @@
     return dense_apply(left_operand, right_operand, kept_mask, product_kind)
 
 
+def a2a_scatter_sum(parts, axis_name):
+    count = lax.axis_size(axis_name)
+    pieces = parts.reshape((count, parts.shape[0] // count) + parts.shape[1:])
+    return lax.all_to_all(pieces, axis_name, 0, 0, tiled=True).sum(axis=0)
+
+
+def a2a_gather(block, axis_name):
+    count = lax.axis_size(axis_name)
+    spread = jnp.broadcast_to(block[None], (count,) + block.shape)
+    gathered = lax.all_to_all(spread, axis_name, 0, 0, tiled=True)
+    return gathered.reshape((count * block.shape[0],) + block.shape[1:])
+
+
 def on_device(tokens, cotangent, w_gate, w_up, w_down, order_gate, order_up, order_down):
     rows_here = w_gate.shape[0] // BLOCK
     cols_here = w_gate.shape[1] // BLOCK
@@ -47,43 +60,38 @@
     col_start = lax.axis_index("col") * cols_here
     width_blocks = rows_here * lax.axis_size("row")
     hidden_blocks = cols_here * lax.axis_size("col")
+    hidden_here = w_gate.shape[1]
     keep_gate = kept_table(order_gate, row_start, col_start, rows_here, cols_here, hidden_blocks)
     keep_up = kept_table(order_up, row_start, col_start, rows_here, cols_here, hidden_blocks)
     keep_down = kept_table(order_down, col_start, row_start, cols_here, rows_here, width_blocks)
-    tokens_all = lax.all_gather(tokens, "col", axis=0, tiled=True)
+    cotangent_all = lax.all_gather(cotangent, "col", axis=0, tiled=True)
+    tokens_all = a2a_gather(tokens, "col")
     gate_term = apply_blocks(tokens_all, w_gate, keep_gate, "forward")
     up_term = apply_blocks(tokens_all, w_up, keep_up, "forward")
-    gate, up = (
-        lax.psum_scatter(gate_term, "row", scatter_dimension=0, tiled=True),
-        lax.psum_scatter(up_term, "row", scatter_dimension=0, tiled=True),
-    )
+    both = a2a_scatter_sum(jnp.concatenate([gate_term, up_term], axis=1), "row")
+    gate, up = both[:, :hidden_here], both[:, hidden_here:]
+    hidden_term = apply_blocks(cotangent_all, w_down, keep_down, "transposed")
+    hidden_grad = a2a_scatter_sum(hidden_term, "row")
     sigmoid_gate = jax.nn.sigmoid(gate)
     activation = gate * sigmoid_gate
     hidden = (activation * up).astype(jnp.bfloat16)
-    hidden_all = lax.all_gather(hidden, "row", axis=0, tiled=True)
+    hidden_all = a2a_gather(hidden, "row")
     output_term = apply_blocks(hidden_all, w_down, keep_down, "forward")
     output = lax.psum_scatter(output_term, "col", scatter_dimension=0, tiled=True).astype(
         jnp.bfloat16
     )
-    cotangent_all = lax.all_gather(cotangent, "col", axis=0, tiled=True)
-    hidden_term = apply_blocks(cotangent_all, w_down, keep_down, "transposed")
-    hidden_grad = lax.psum_scatter(hidden_term, "row", scatter_dimension=0, tiled=True)
     gate_grad = (hidden_grad * up * sigmoid_gate * (1.0 + gate * (1.0 - sigmoid_gate))).astype(
         jnp.bfloat16
     )
     up_grad = (hidden_grad * activation).astype(jnp.bfloat16)
-    gate_grad_all, up_grad_all = (
-        lax.all_gather(gate_grad, "row", axis=0, tiled=True),
-        lax.all_gather(up_grad, "row", axis=0, tiled=True),
-    )
+    grads_all = a2a_gather(jnp.concatenate([gate_grad, up_grad], axis=1), "row")
+    gate_grad_all, up_grad_all = grads_all[:, :hidden_here], grads_all[:, hidden_here:]
     down_weight_grad = apply_blocks(hidden_all, cotangent_all, keep_down, "weights")
     gate_weight_grad = apply_blocks(tokens_all, gate_grad_all, keep_gate, "weights")
     up_weight_grad = apply_blocks(tokens_all, up_grad_all, keep_up, "weights")
     through_gate = apply_blocks(gate_grad_all, w_gate, keep_gate, "transposed")
     through_up = apply_blocks(up_grad_all, w_up, keep_up, "transposed")
-    gate_share = lax.psum_scatter(through_gate, "col", scatter_dimension=0, tiled=True)
-    up_share = lax.psum_scatter(through_up, "col", scatter_dimension=0, tiled=True)
-    input_grad = gate_share + up_share
+    input_grad = a2a_scatter_sum(through_gate + through_up, "col")
     return (
         output,
         input_grad.astype(jnp.bfloat16),

time: 446 us -> 283 us (0.63)
  waiting for transfers between devices: 329 us -> 189 us
  blocking collectives: 58.9 us -> 0 us
  starting transfers between devices: 0.28 us -> 35.7 us
    reduce_scatter x4 -> x0, waiting for transfers between devices: 194 us -> none  [the longest x1 88.4 us: on_device(): lax.psum_scatter(through_gate, 'col', scatter_dimension=0, tiled=True)]
    all_to_all x0 -> x6, waiting for transfers between devices: none -> 120 us  [the longest x3 80.2 us: a2a_scatter_sum(): return lax.all_to_all(pieces, axis_name, 0, 0, tiled=True).sum(axis=0)]
    all_gather x3 -> x0, blocking collectives: 58.9 us -> none  [the longest x1 19.8 us: on_device(): lax.all_gather(up_grad, 'row', axis=0, tiled=True)]
    all_gather x1 -> x0, waiting for transfers between devices: 44.4 us -> none  [on_device(): tokens_all = lax.all_gather(tokens, 'col', axis=0, tiled=True)]
    all_to_all x0 -> x6, starting transfers between devices: none -> 35.6 us  [the longest x3 18.3 us: a2a_scatter_sum(): return lax.all_to_all(pieces, axis_name, 0, 0, tiled=True).sum(axis=0)]
    reduce_scatter x1, waiting for transfers between devices: 37.3 us -> 23.5 us  [on_device(): lax.psum_scatter(output_term, 'col', scatter_dimension=0, tiled=True)]
    all_gather x1, waiting for transfers between devices: 51.9 us -> 44.6 us  [on_device(): cotangent_all = lax.all_gather(cotangent, 'col', axis=0, tiled=True)]
    unnamed x34 -> x43, local copies, waits for them, and re-layouts: 15.5 us -> 11.4 us
  transfers between devices with their start and end apart: 7 -> 8, of which waited for: 7 -> 7; matrix products, arithmetic and copies ran while one was open for 8% -> 14% of each run, Pallas kernels for 0% -> 0%
where the time goes in v1:
time: 283 us; the launch traced here: 281 us
  waiting for transfers between devices  189 us (67%)
  starting transfers between devices  35.7 us (13%)
  matrix products  21.3 us (8%)
  local copies, waits for them, and re-layouts  18.1 us (6%)
  between operations  14.4 us (5%)
  other arithmetic  3.27 us (1%)
    all_to_all x3, waiting for transfers between devices, a2a_scatter_sum(): return lax.all_to_all(pieces, axis_name, 0, 0, tiled=True).sum(axis=0)  80.2 us
    all_gather x1, waiting for transfers between devices, on_device(): cotangent_all = lax.all_gather(cotangent, 'col', axis=0, tiled=True)  44.6 us
    all_to_all x3, waiting for transfers between devices, a2a_gather(): gathered = lax.all_to_all(spread, axis_name, 0, 0, tiled=True)  39.7 us
    reduce_scatter x1, waiting for transfers between devices, on_device(): lax.psum_scatter(output_term, 'col', scatter_dimension=0, tiled=True)  23.5 us
    all_to_all x3, starting transfers between devices, a2a_scatter_sum(): return lax.all_to_all(pieces, axis_name, 0, 0, tiled=True).sum(axis=0)  18.3 us
    all_to_all x3, starting transfers between devices, a2a_gather(): gathered = lax.all_to_all(spread, axis_name, 0, 0, tiled=True)  17.3 us
    unnamed x43, local copies, waits for them, and re-layouts  11.4 us
    dot_general x3, matrix products, dense_apply(): lax.dot_general(left_operand, right_operand, (((0,), (0,)), ((), ())), pr...  8.97 us
  transfers between devices with their start and end apart: 8, of which 7 were waited for; matrix products, arithmetic and copies ran while one was open for 14% of the time, Pallas kernels for 0%

profile of v1, /device:TPU:1, one launch (start us, length us, event | category | flops | bytes accessed | tf_op | source)
XLA Modules:
  0.0 281.4 jit_solution(4696219631229832951)
XLA Ops:
  9.8 8.7 %all-to-all-start = ((bf16[32,16,1024]{2,1,0:T(8,128)(2,1)}), bf16[32,16,1024]{2,1,0:T(8,128)(2,1)S(1)}, u32[]{:S(2)}, u32[]{:S(2)}) async-start(bf16[32,16,1024]{2,1,0:T(8,128)(2,1)} %broadcast_in_dim.13), calls=%async_computation | async-start | bytes 2097152 | tf_op jit(solution)/shard_map/all_to_all | solution.py:52
  19.4 44.6 %all-gather.2.cloned.1.call-done = bf16[512,1024]{1,0:T(8,128)(2,1)} async-done(((bf16[16,1024]{1,0:T(8,128)(2,1)}), bf16[512,1024]{1,0:T(8,128)(2,1)}) %all-gather.2.cloned.1.call-update) | async-done | bytes 1048592 | tf_op jit(solution)/shard_map/all_gather | solution.py:67
  64.1 2.9 %fusion = f32[512,512]{0,1:T(8,128)} fusion(bf16[512,1024]{1,0:T(8,128)(2,1)} %all-gather.2.cloned.1.call-done, pred[512,1024]{1,0:T(8,128)(4,1)S(1)} %bitcast.50, bf16[512,1024]{1,0:T(8,128)(2,1)S(1)} %copy-done.13), kind=kOutput, calls=%fused_computation.7 | convolution fusion | flops 537395200 | bytes 3670016 | tf_op jit(solution)/shard_map/dot_general | solution.py:30
  67.0 6.7 %all-to-all-start.3 = ((f32[8,64,512]{2,1,0:T(8,128)}), f32[8,64,512]{2,1,0:T(8,128)S(1)}, u32[]{:S(2)}, u32[]{:S(2)}) async-start(f32[8,64,512]{2,1,0:T(8,128)} %bitcast.57), calls=%async_computation.4 | async-start | bytes 2097152 | tf_op jit(solution)/shard_map/all_to_all | solution.py:46
  77.8 2.3 copy.22
  80.1 2.1 convolution_bitcast_fusion
  85.0 18.0 %all-to-all-done.3 = f32[8,64,512]{2,1,0:T(8,128)S(1)} async-done(((f32[8,64,512]{2,1,0:T(8,128)}), f32[8,64,512]{2,1,0:T(8,128)S(1)}, u32[]{:S(2)}, u32[]{:S(2)}) %all-to-all-start.3) | async-done | bytes 1048608 | tf_op jit(solution)/shard_map/all_to_all | solution.py:46
  103.0 3.6 %all-to-all-start.1 = ((f32[8,64,1024]{2,1,0:T(8,128)}), f32[8,64,1024]{2,1,0:T(8,128)S(1)}, u32[]{:S(2)}, u32[]{:S(2)}) async-start(f32[8,64,1024]{2,1,0:T(8,128)} %bitcast.37), calls=%async_computation.1 | async-start | bytes 4194304 | tf_op jit(solution)/shard_map/all_to_all | solution.py:46
  106.7 48.0 %all-to-all-done.1 = f32[8,64,1024]{2,1,0:T(8,128)S(1)} async-done(((f32[8,64,1024]{2,1,0:T(8,128)}), f32[8,64,1024]{2,1,0:T(8,128)S(1)}, u32[]{:S(2)}, u32[]{:S(2)}) %all-to-all-start.1) | async-done | bytes 2097184 | tf_op jit(solution)/shard_map/all_to_all | solution.py:46
  155.8 5.1 %all-to-all-start.2 = ((bf16[8,64,512]{2,1,0:T(8,128)(2,1)}), bf16[8,64,512]{2,1,0:T(8,128)(2,1)S(1)}, u32[]{:S(2)}, u32[]{:S(2)}) async-start(bf16[8,64,512]{2,1,0:T(8,128)(2,1)} %broadcast_in_dim.15), calls=%async_computation.2 | async-start | bytes 1048576 | tf_op jit(solution)/shard_map/all_to_all | solution.py:52
  160.9 15.1 %all-to-all-done.2 = bf16[8,64,512]{2,1,0:T(8,128)(2,1)S(1)} async-done(((bf16[8,64,512]{2,1,0:T(8,128)(2,1)}), bf16[8,64,512]{2,1,0:T(8,128)(2,1)S(1)}, u32[]{:S(2)}, u32[]{:S(2)}) %all-to-all-start.2) | async-done | bytes 524320 | tf_op jit(solution)/shard_map/all_to_all | solution.py:52
  177.1 3.6 %all-to-all-start.4 = ((bf16[8,64,1024]{2,1,0:T(8,128)(2,1)}), bf16[8,64,1024]{2,1,0:T(8,128)(2,1)S(1)}, u32[]{:S(2)}, u32[]{:S(2)}) async-start(bf16[8,64,1024]{2,1,0:T(8,128)(2,1)} %broadcast_in_dim.17), calls=%async_computation.5 | async-start | bytes 2097152 | tf_op jit(solution)/shard_map/all_to_all | solution.py:52
  180.7 2.0 fusion.2
  182.8 24.5 %all-to-all-done.4 = bf16[8,64,1024]{2,1,0:T(8,128)(2,1)S(1)} async-done(((bf16[8,64,1024]{2,1,0:T(8,128)(2,1)}), bf16[8,64,1024]{2,1,0:T(8,128)(2,1)S(1)}, u32[]{:S(2)}, u32[]{:S(2)}) %all-to-all-start.4) | async-done | bytes 1048608 | tf_op jit(solution)/shard_map/all_to_all | solution.py:52
  207.3 2.4 fusion.6
  209.7 2.1 convolution_add_fusion
  211.8 8.0 %all-to-all-start.5 = ((f32[32,16,1024]{2,1,0:T(8,128)}), f32[32,16,1024]{2,1,0:T(8,128)S(1)}, u32[]{:S(2)}, u32[]{:S(2)}) async-start(f32[32,16,1024]{2,1,0:T(8,128)} %bitcast.8), calls=%async_computation.6 | async-start | bytes 4194304 | tf_op jit(solution)/shard_map/all_to_all | solution.py:46
  219.8 3.4 %convolution_select_fusion = f32[512,1024]{1,0:T(8,128)} fusion(pred[512,1024]{1,0:T(8,128)(4,1)S(1)} %bitcast.52, bf16[512,512]{1,0:T(8,128)(2,1)S(1)} %bitcast.39, bf16[512,1024]{1,0:T(8,128)(2,1)} %all-gather.2.cloned.1.call-done), kind=kOutput, calls=%fused_computation.3 | convolution fusion | flops 537395200 | bytes 4194304 | tf_op jit(solution)/shard_map/dot_general | solution.py:33
  223.3 2.1 bitcast_select_fusion.1
  225.3 3.0 %copy.25 = f32[1024,512]{1,0:T(8,128)} copy(f32[1024,512]{0,1:T(8,128)} %bitcast_select_fusion.1) | data formatting | bytes 4194304
  228.3 3.5 %bitcast_select_fusion = f32[1024,512]{0,1:T(8,128)} fusion(pred[1024,512]{0,1:T(8,128)(4,1)} %bitcast.45, bf16[512,1024]{1,0:T(8,128)(2,1)} %bitcast.54, bf16[512,1024]{1,0:T(8,128)(2,1)S(1)} %bitcast.43), kind=kOutput, calls=%fused_computation.1 | convolution fusion | flops 537395200 | bytes 4194304 | tf_op jit(solution)/shard_map/dot_general | solution.py:33
  231.8 2.9 %copy.26 = f32[1024,512]{1,0:T(8,128)} copy(f32[1024,512]{0,1:T(8,128)} %bitcast_select_fusion) | data formatting | bytes 4194304
  234.7 14.2 %all-to-all-done.5 = f32[32,16,1024]{2,1,0:T(8,128)S(1)} async-done(((f32[32,16,1024]{2,1,0:T(8,128)}), f32[32,16,1024]{2,1,0:T(8,128)S(1)}, u32[]{:S(2)}, u32[]{:S(2)}) %all-to-all-start.5) | async-done | bytes 2097184 | tf_op jit(solution)/shard_map/all_to_all | solution.py:46
  249.6 23.5 %reduce-scatter.2.cloned.1.call-done = f32[16,1024]{1,0:T(8,128)} async-done(((f32[512,1024]{1,0:T(8,128)}), f32[16,1024]{1,0:T(8,128)}) %reduce-scatter.2.cloned.1.call-update) | async-done | bytes 65552 | tf_op jit(solution)/shard_map/reduce_scatter | solution.py:80
  (72 shorter events, 14.8 us)
Async XLA Ops:
  7.2 11.4 %slice-start = ((s32[2048]{0:T(1024)}), s32[1024]{0:T(1024)S(1)}, s32[]{:S(2)}) async-start(s32[2048]{0:T(1024)} %param.15), calls=%async_computation.9 | async-start | bytes 8192 | tf_op jit(solution)/shard_map/slice | solution.py:14
  7.2 56.9 %all-gather.2.cloned.1.call-start = ((), (), s32[]{:S(2)}) async-start(), calls=%async_computation.8 | async-start | bytes 1081344 | tf_op jit(solution)/shard_map/all_gather | solution.py:67
  9.8 54.3 %copy-start.13 = (bf16[512,1024]{1,0:T(8,128)(2,1)S(1)}, bf16[512,1024]{1,0:T(8,128)(2,1)}, u32[]{:S(2)}) copy-start(bf16[512,1024]{1,0:T(8,128)(2,1)} %param.12) | copy-start | bytes 3145732
  9.8 57.3 %all-to-all-start = ((bf16[32,16,1024]{2,1,0:T(8,128)(2,1)}), bf16[32,16,1024]{2,1,0:T(8,128)(2,1)S(1)}, u32[]{:S(2)}, u32[]{:S(2)}) async-start(bf16[32,16,1024]{2,1,0:T(8,128)(2,1)} %broadcast_in_dim.13), calls=%async_computation | async-start | bytes 2097152 | tf_op jit(solution)/shard_map/all_to_all | solution.py:52
  19.4 47.6 %copy-start.7 = (pred[64,8,4,256]{3,1,2,0:T(8,128)(4,1)}, pred[64,8,4,256]{3,1,2,0:T(8,128)(4,1)S(1)}, u32[]{:S(2)}) copy-start(pred[64,8,4,256]{3,1,2,0:T(8,128)(4,1)S(1)} %copy.29) | copy-start | bytes 1572868
  67.0 6.8 %slice-start.1 = ((s32[2048]{0:T(1024)}), s32[1024]{0:T(1024)S(1)}, s32[]{:S(2)}) async-start(s32[2048]{0:T(1024)} %param.13), calls=%async_computation.10 | async-start | bytes 8192 | tf_op jit(solution)/shard_map/slice | solution.py:14
  67.0 6.8 %slice-start.2 = ((s32[2048]{0:T(1024)}), s32[1024]{0:T(1024)S(1)}, s32[]{:S(2)}) async-start(s32[2048]{0:T(1024)} %param.14), calls=%async_computation.11 | async-start | bytes 8192 | tf_op jit(solution)/shard_map/slice | solution.py:14
  67.0 7.4 %copy-start.9 = (bf16[32,16,1024]{2,1,0:T(8,128)(2,1)}, bf16[32,16,1024]{2,1,0:T(8,128)(2,1)S(1)}, u32[]{:S(2)}) copy-start(bf16[32,16,1024]{2,1,0:T(8,128)(2,1)S(1)} %all-to-all-done) | copy-start | bytes 3145732
  67.0 36.0 %all-to-all-start.3 = ((f32[8,64,512]{2,1,0:T(8,128)}), f32[8,64,512]{2,1,0:T(8,128)S(1)}, u32[]{:S(2)}, u32[]{:S(2)}) async-start(f32[8,64,512]{2,1,0:T(8,128)} %bitcast.57), calls=%async_computation.4 | async-start | bytes 2097152 | tf_op jit(solution)/shard_map/all_to_all | solution.py:46
  74.7 7.5 %copy-start.5 = (pred[64,8,4,256]{3,1,2,0:T(8,128)(4,1)}, pred[64,8,4,256]{3,1,2,0:T(8,128)(4,1)S(1)}, u32[]{:S(2)}) copy-start(pred[64,8,4,256]{3,1,2,0:T(8,128)(4,1)S(1)} %copy.28) | copy-start | bytes 1572868
  76.4 5.8 %copy-start = (bf16[1024,512]{0,1:T(8,128)(2,1)}, bf16[1024,512]{0,1:T(8,128)(2,1)S(1)}, u32[]{:S(2)}) copy-start(bf16[1024,512]{0,1:T(8,128)(2,1)S(1)} %copy.23) | copy-start | bytes 3145732
  103.0 51.7 %all-to-all-start.1 = ((f32[8,64,1024]{2,1,0:T(8,128)}), f32[8,64,1024]{2,1,0:T(8,128)S(1)}, u32[]{:S(2)}, u32[]{:S(2)}) async-start(f32[8,64,1024]{2,1,0:T(8,128)} %bitcast.37), calls=%async_computation.1 | async-start | bytes 4194304 | tf_op jit(solution)/shard_map/all_to_all | solution.py:46
  155.8 24.9 %copy-start.8 = (pred[64,8,4,256]{3,1,2,0:T(8,128)(4,1)S(1)}, pred[64,8,4,256]{3,1,2,0:T(8,128)(4,1)}, u32[]{:S(2)}) copy-start(pred[64,8,4,256]{3,1,2,0:T(8,128)(4,1)} %copy-done.7) | copy-start | bytes 1572868
  155.8 24.9 %copy-start.14 = (bf16[512,1024]{1,0:T(8,128)(2,1)S(1)}, bf16[512,1024]{1,0:T(8,128)(2,1)}, u32[]{:S(2)}) copy-start(bf16[512,1024]{1,0:T(8,128)(2,1)} %param.12) | copy-start | bytes 3145732
  155.8 20.2 %all-to-all-start.2 = ((bf16[8,64,512]{2,1,0:T(8,128)(2,1)}), bf16[8,64,512]{2,1,0:T(8,128)(2,1)S(1)}, u32[]{:S(2)}, u32[]{:S(2)}) async-start(bf16[8,64,512]{2,1,0:T(8,128)(2,1)} %broadcast_in_dim.15), calls=%async_computation.2 | async-start | bytes 1048576 | tf_op jit(solution)/shard_map/all_to_all | solution.py:52
  177.1 30.2 %all-to-all-start.4 = ((bf16[8,64,1024]{2,1,0:T(8,128)(2,1)}), bf16[8,64,1024]{2,1,0:T(8,128)(2,1)S(1)}, u32[]{:S(2)}, u32[]{:S(2)}) async-start(bf16[8,64,1024]{2,1,0:T(8,128)(2,1)} %broadcast_in_dim.17), calls=%async_computation.5 | async-start | bytes 2097152 | tf_op jit(solution)/shard_map/all_to_all | solution.py:52
  180.6 92.5 %reduce-scatter.2.cloned.1.call-start = ((), (), s32[]{:S(2)}) async-start(), calls=%async_computation.7 | async-start | bytes 2162688 | tf_op jit(solution)/shard_map/reduce_scatter | solution.py:80
  182.7 24.6 %copy-start.16 = (pred[64,8,4,256]{3,1,2,0:T(8,128)(4,1)S(1)}, pred[64,8,4,256]{3,1,2,0:T(8,128)(4,1)}, u32[]{:S(2)}) copy-start(pred[64,8,4,256]{3,1,2,0:T(8,128)(4,1)} %copy.27) | copy-start | bytes 1572868
  207.3 2.4 copy-start.6
  211.8 37.1 %all-to-all-start.5 = ((f32[32,16,1024]{2,1,0:T(8,128)}), f32[32,16,1024]{2,1,0:T(8,128)S(1)}, u32[]{:S(2)}, u32[]{:S(2)}) async-start(f32[32,16,1024]{2,1,0:T(8,128)} %bitcast.8), calls=%async_computation.6 | async-start | bytes 4194304 | tf_op jit(solution)/shard_map/all_to_all | solution.py:46
  219.8 3.5 %copy-start.3 = (bf16[8,64,1024]{2,1,0:T(8,128)(2,1)S(1)}, bf16[8,64,1024]{2,1,0:T(8,128)(2,1)}, u32[]{:S(2)}) copy-start(bf16[8,64,1024]{2,1,0:T(8,128)(2,1)} %copy-done.2) | copy-start | bytes 3145732
  219.8 3.5 %copy-start.11 = (bf16[32,16,1024]{2,1,0:T(8,128)(2,1)S(1)}, bf16[32,16,1024]{2,1,0:T(8,128)(2,1)}, u32[]{:S(2)}) copy-start(bf16[32,16,1024]{2,1,0:T(8,128)(2,1)} %copy-done.9) | copy-start | bytes 3145732
  219.8 3.5 %copy-start.17 = (pred[64,8,4,256]{3,1,2,0:T(8,128)(4,1)S(1)}, pred[64,8,4,256]{3,1,2,0:T(8,128)(4,1)}, u32[]{:S(2)}) copy-start(pred[64,8,4,256]{3,1,2,0:T(8,128)(4,1)} %copy.27) | copy-start | bytes 1572868
  225.3 3.0 %copy-start.4 = (bf16[8,64,1024]{2,1,0:T(8,128)(2,1)S(1)}, bf16[8,64,1024]{2,1,0:T(8,128)(2,1)}, u32[]{:S(2)}) copy-start(bf16[8,64,1024]{2,1,0:T(8,128)(2,1)} %copy-done.2) | copy-start | bytes 3145732
  (5 other events, 11.3 us)
Sparse Core Ops, SparseCore 0:
  10.5 53.4 all-gather.1
  185.3 87.8 reduce-scatter.1

commit v2 on v1

--- a/solution.py
+++ b/solution.py
@@ -64,34 +64,36 @@
     keep_gate = kept_table(order_gate, row_start, col_start, rows_here, cols_here, hidden_blocks)
     keep_up = kept_table(order_up, row_start, col_start, rows_here, cols_here, hidden_blocks)
     keep_down = kept_table(order_down, col_start, row_start, cols_here, rows_here, width_blocks)
-    cotangent_all = lax.all_gather(cotangent, "col", axis=0, tiled=True)
-    tokens_all = a2a_gather(tokens, "col")
+    width_here = tokens.shape[1]
+    inputs_all = a2a_gather(jnp.concatenate([tokens, cotangent], axis=1), "col")
+    tokens_all, cotangent_all = inputs_all[:, :width_here], inputs_all[:, width_here:]
     gate_term = apply_blocks(tokens_all, w_gate, keep_gate, "forward")
     up_term = apply_blocks(tokens_all, w_up, keep_up, "forward")
-    both = a2a_scatter_sum(jnp.concatenate([gate_term, up_term], axis=1), "row")
-    gate, up = both[:, :hidden_here], both[:, hidden_here:]
     hidden_term = apply_blocks(cotangent_all, w_down, keep_down, "transposed")
-    hidden_grad = a2a_scatter_sum(hidden_term, "row")
+    sums = a2a_scatter_sum(jnp.concatenate([gate_term, up_term, hidden_term], axis=1), "row")
+    gate = sums[:, :hidden_here]
+    up = sums[:, hidden_here : 2 * hidden_here]
+    hidden_grad = sums[:, 2 * hidden_here :]
     sigmoid_gate = jax.nn.sigmoid(gate)
     activation = gate * sigmoid_gate
     hidden = (activation * up).astype(jnp.bfloat16)
-    hidden_all = a2a_gather(hidden, "row")
-    output_term = apply_blocks(hidden_all, w_down, keep_down, "forward")
-    output = lax.psum_scatter(output_term, "col", scatter_dimension=0, tiled=True).astype(
-        jnp.bfloat16
-    )
     gate_grad = (hidden_grad * up * sigmoid_gate * (1.0 + gate * (1.0 - sigmoid_gate))).astype(
         jnp.bfloat16
     )
     up_grad = (hidden_grad * activation).astype(jnp.bfloat16)
-    grads_all = a2a_gather(jnp.concatenate([gate_grad, up_grad], axis=1), "row")
-    gate_grad_all, up_grad_all = grads_all[:, :hidden_here], grads_all[:, hidden_here:]
+    acts_all = a2a_gather(jnp.concatenate([hidden, gate_grad, up_grad], axis=1), "row")
+    hidden_all = acts_all[:, :hidden_here]
+    gate_grad_all = acts_all[:, hidden_here : 2 * hidden_here]
+    up_grad_all = acts_all[:, 2 * hidden_here :]
+    output_term = apply_blocks(hidden_all, w_down, keep_down, "forward")
     down_weight_grad = apply_blocks(hidden_all, cotangent_all, keep_down, "weights")
     gate_weight_grad = apply_blocks(tokens_all, gate_grad_all, keep_gate, "weights")
     up_weight_grad = apply_blocks(tokens_all, up_grad_all, keep_up, "weights")
     through_gate = apply_blocks(gate_grad_all, w_gate, keep_gate, "transposed")
     through_up = apply_blocks(up_grad_all, w_up, keep_up, "transposed")
-    input_grad = a2a_scatter_sum(through_gate + through_up, "col")
+    outs = a2a_scatter_sum(jnp.concatenate([output_term, through_gate + through_up], axis=1), "col")
+    output = outs[:, :width_here].astype(jnp.bfloat16)
+    input_grad = outs[:, width_here:]
     return (
         output,
         input_grad.astype(jnp.bfloat16),

time: 283 us -> 241 us (0.85)
  waiting for transfers between devices: 189 us -> 62.9 us
  blocking collectives: 0 us -> 119 us
  starting transfers between devices: 35.7 us -> 19.8 us
  between operations: 14.4 us -> 0.93 us
  local copies, waits for them, and re-layouts: 18.1 us -> 11.9 us
  other arithmetic: 3.27 us -> 6.84 us
  matrix products: 21.3 us -> 18.1 us
    all_to_all x0 -> x2, blocking collectives: none -> 119 us  [the longest x1 79 us: a2a_scatter_sum(): return lax.all_to_all(pieces, axis_name, 0, 0, tiled=True).sum(axis=0)]
    all_gather x1 -> x0, waiting for transfers between devices: 44.6 us -> none  [on_device(): cotangent_all = lax.all_gather(cotangent, 'col', axis=0, tiled=True)]
    all_to_all x3 -> x1, waiting for transfers between devices: 80.2 us -> 39.6 us  [a2a_scatter_sum(): return lax.all_to_all(pieces, axis_name, 0, 0, tiled=True).sum(axis=0)]
    reduce_scatter x1 -> x0, waiting for transfers between devices: 23.5 us -> none  [on_device(): lax.psum_scatter(output_term, 'col', scatter_dimension=0, tiled=True)]
    all_to_all x3 -> x1, waiting for transfers between devices: 39.7 us -> 23.4 us  [a2a_gather(): gathered = lax.all_to_all(spread, axis_name, 0, 0, tiled=True)]
    all_to_all x3 -> x1, starting transfers between devices: 17.3 us -> 8.76 us  [a2a_gather(): gathered = lax.all_to_all(spread, axis_name, 0, 0, tiled=True)]
    all_to_all x3 -> x1, starting transfers between devices: 18.3 us -> 11 us  [a2a_scatter_sum(): return lax.all_to_all(pieces, axis_name, 0, 0, tiled=True).sum(axis=0)]
    unnamed x43 -> x33, local copies, waits for them, and re-layouts: 11.4 us -> 4.94 us
  transfers between devices with their start and end apart: 8 -> 2, of which waited for: 7 -> 2; matrix products, arithmetic and copies ran while one was open for 14% -> 6% of each run, Pallas kernels for 0% -> 0%
where the time goes in v2:
time: 241 us; the launch traced here: 240 us
  blocking collectives  119 us (49%)
  waiting for transfers between devices  62.9 us (26%)
  starting transfers between devices  19.8 us (8%)
  matrix products  18.1 us (8%)
  local copies, waits for them, and re-layouts  11.9 us (5%)
  other arithmetic  6.84 us (3%)
    all_to_all x1, blocking collectives, a2a_scatter_sum(): return lax.all_to_all(pieces, axis_name, 0, 0, tiled=True).sum(axis=0)  79 us
    all_to_all x1, blocking collectives, a2a_gather(): gathered = lax.all_to_all(spread, axis_name, 0, 0, tiled=True)  40.3 us
    all_to_all x1, waiting for transfers between devices, a2a_scatter_sum(): return lax.all_to_all(pieces, axis_name, 0, 0, tiled=True).sum(axis=0)  39.6 us
    all_to_all x1, waiting for transfers between devices, a2a_gather(): gathered = lax.all_to_all(spread, axis_name, 0, 0, tiled=True)  23.4 us
    all_to_all x1, starting transfers between devices, a2a_scatter_sum(): return lax.all_to_all(pieces, axis_name, 0, 0, tiled=True).sum(axis=0)  11 us
    dot_general x3, matrix products, dense_apply(): lax.dot_general(left_operand, right_operand, (((0,), (0,)), ((), ())), pr...  9.84 us
    all_to_all x1, starting transfers between devices, a2a_gather(): gathered = lax.all_to_all(spread, axis_name, 0, 0, tiled=True)  8.76 us
    unnamed x33, local copies, waits for them, and re-layouts  4.94 us
  transfers between devices with their start and end apart: 2, of which 2 were waited for; matrix products, arithmetic and copies ran while one was open for 6% of the time, Pallas kernels for 0%

profile of v2, /device:TPU:1, one launch (start us, length us, event | category | flops | bytes accessed | tf_op | source)
XLA Modules:
  0.0 239.9 jit_solution(12858135818607556724)
XLA Ops:
  0.6 0.8 pad_maximum_fusion.3
  1.4 1.6 broadcast_in_dim.10
  3.0 8.8 %all-to-all-start = ((bf16[32,16,2048]{2,1,0:T(8,128)(2,1)}), bf16[32,16,2048]{2,1,0:T(8,128)(2,1)}, u32[]{:S(2)}, u32[]{:S(2)}) async-start(bf16[32,16,2048]{2,1,0:T(8,128)(2,1)} %broadcast_in_dim.10), calls=%async_computation | async-start | bytes 4194304 | tf_op jit(solution)/shard_map/all_to_all | solution.py:52
  13.9 1.0 copy-done.7
  14.9 1.3 copy.18
  17.1 23.4 %all-to-all-done = bf16[32,16,2048]{2,1,0:T(8,128)(2,1)} async-done(((bf16[32,16,2048]{2,1,0:T(8,128)(2,1)}), bf16[32,16,2048]{2,1,0:T(8,128)(2,1)}, u32[]{:S(2)}, u32[]{:S(2)}) %all-to-all-start) | async-done | bytes 2097184 | tf_op jit(solution)/shard_map/all_to_all | solution.py:52
  40.5 2.1 fusion.5
  42.6 2.1 fusion.7
  44.7 2.0 fusion.1
  47.0 2.3 copy.20
  49.3 79.0 %all_to_all.20 = f32[8,64,1536]{2,1,0:T(8,128)S(1)} all-to-all(f32[8,64,1536]{2,1,0:T(8,128)} %bitcast.18), channel_id=1, replica_groups=mesh['row'=8,'col'=32] {'row'}, dimensions={0} | all-to-all | bytes 6291456 | tf_op jit(solution)/shard_map/all_to_all | solution.py:46
  128.8 40.3 %all_to_all.21 = bf16[8,64,1536]{2,1,0:T(8,128)(2,1)S(1)} all-to-all(bf16[8,64,1536]{2,1,0:T(8,128)(2,1)S(1)} %broadcast_in_dim.14), channel_id=1, replica_groups=mesh['row'=8,'col'=32] {'row'}, dimensions={0} | all-to-all | bytes 3145728 | tf_op jit(solution)/shard_map/all_to_all | solution.py:52
  169.2 0.7 fusion.10
  170.5 0.7 fusion.9
  171.9 0.8 convolution_add_fusion
  172.7 2.5 %pad_maximum_fusion = f32[512,2048]{1,0:T(8,128)} fusion(f32[512,1024]{1,0:T(8,128)S(1)} %convolution_add_fusion, f32[512,1024]{1,0:T(8,128)S(1)} %fusion.9), kind=kLoop, calls=%fused_computation | loop fusion | flops 1048576 | bytes 8388608 | tf_op jit(solution)/shard_map/concatenate | solution.py:94
  175.2 11.0 %all-to-all-start.3 = ((f32[32,16,2048]{2,1,0:T(8,128)}), f32[32,16,2048]{2,1,0:T(8,128)}, u32[]{:S(2)}, u32[]{:S(2)}) async-start(f32[32,16,2048]{2,1,0:T(8,128)} %bitcast.17), calls=%async_computation.3 | async-start | bytes 8388608 | tf_op jit(solution)/shard_map/all_to_all | solution.py:46
  186.2 0.6 copy.22
  187.4 3.3 %convolution_select_fusion.1 = f32[1024,512]{1,0:T(8,128)} fusion(pred[1024,512]{1,0:T(32,128)(4,1)S(1)} %copy.22, bf16[512,2048]{1,0:T(8,128)(2,1)} %bitcast, bf16[512,1536]{1,0:T(8,128)(2,1)S(1)} %bitcast.25), kind=kOutput, calls=%fused_computation.3 | convolution fusion | flops 537395200 | bytes 4194304 | tf_op jit(solution)/shard_map/dot_general | solution.py:33
  190.7 3.3 %convolution_select_fusion.2 = f32[1024,512]{1,0:T(8,128)} fusion(pred[1024,512]{1,0:T(32,128)(4,1)S(1)} %copy.21, bf16[512,2048]{1,0:T(8,128)(2,1)} %bitcast, bf16[512,1536]{1,0:T(8,128)(2,1)S(1)} %bitcast.26), kind=kOutput, calls=%fused_computation.4 | convolution fusion | flops 537395200 | bytes 4194304 | tf_op jit(solution)/shard_map/dot_general | solution.py:33
  194.0 3.3 %convolution_select_fusion = f32[512,1024]{1,0:T(8,128)} fusion(pred[512,1024]{1,0:T(8,128)(4,1)S(1)} %bitcast.36, bf16[512,2048]{1,0:T(8,128)(2,1)} %bitcast, bf16[512,1536]{1,0:T(8,128)(2,1)S(1)} %bitcast.27), kind=kOutput, calls=%fused_computation.2 | convolution fusion | flops 537395200 | bytes 4194304 | tf_op jit(solution)/shard_map/dot_general | solution.py:33
  197.3 39.6 %all-to-all-done.3 = f32[32,16,2048]{2,1,0:T(8,128)} async-done(((f32[32,16,2048]{2,1,0:T(8,128)}), f32[32,16,2048]{2,1,0:T(8,128)}, u32[]{:S(2)}, u32[]{:S(2)}) %all-to-all-start.3) | async-done | bytes 4194336 | tf_op jit(solution)/shard_map/all_to_all | solution.py:46
  236.8 2.4 reduce_sum.19
  239.2 0.6 fusion.24
  (52 shorter events, 5.7 us)
Async XLA Ops:
  3.0 8.9 %slice-start = ((s32[2048]{0:T(1024)}), s32[1024]{0:T(1024)S(1)}, s32[]{:S(2)}) async-start(s32[2048]{0:T(1024)} %param.13), calls=%async_computation.4 | async-start | bytes 8192 | tf_op jit(solution)/shard_map/slice | solution.py:14
  3.0 8.9 %slice-start.1 = ((s32[2048]{0:T(1024)}), s32[1024]{0:T(1024)S(1)}, s32[]{:S(2)}) async-start(s32[2048]{0:T(1024)} %param.14), calls=%async_computation.5 | async-start | bytes 8192 | tf_op jit(solution)/shard_map/slice | solution.py:14
  3.0 9.7 %copy-start.6 = (bf16[1024,512]{1,0:T(8,128)(2,1)S(1)}, bf16[1024,512]{1,0:T(8,128)(2,1)}, u32[]{:S(2)}) copy-start(bf16[1024,512]{1,0:T(8,128)(2,1)} %param.11) | copy-start | bytes 3145732
  3.0 37.5 %all-to-all-start = ((bf16[32,16,2048]{2,1,0:T(8,128)(2,1)}), bf16[32,16,2048]{2,1,0:T(8,128)(2,1)}, u32[]{:S(2)}, u32[]{:S(2)}) async-start(bf16[32,16,2048]{2,1,0:T(8,128)(2,1)} %broadcast_in_dim.10), calls=%async_computation | async-start | bytes 4194304 | tf_op jit(solution)/shard_map/all_to_all | solution.py:52
  12.7 27.8 %copy-start = (pred[64,8,4,256]{3,1,2,0:T(8,128)(4,1)}, pred[64,8,4,256]{3,1,2,0:T(8,128)(4,1)S(1)}, u32[]{:S(2)}) copy-start(pred[64,8,4,256]{3,1,2,0:T(8,128)(4,1)S(1)} %copy.24) | copy-start | bytes 1572868
  13.3 27.2 %copy-start.2 = (bf16[1024,512]{0,1:T(8,128)(2,1)}, bf16[1024,512]{0,1:T(8,128)(2,1)S(1)}, u32[]{:S(2)}) copy-start(bf16[1024,512]{0,1:T(8,128)(2,1)S(1)} %copy.19) | copy-start | bytes 3145732
  13.3 1.6 copy-start.7
  13.3 3.0 %slice-start.2 = ((s32[2048]{0:T(1024)}), s32[1024]{0:T(1024)S(1)}, s32[]{:S(2)}) async-start(s32[2048]{0:T(1024)} %param.15), calls=%async_computation.6 | async-start | bytes 8192 | tf_op jit(solution)/shard_map/slice | solution.py:14
  14.9 27.7 %copy-start.4 = (pred[64,8,4,256]{3,1,2,0:T(8,128)(4,1)}, pred[64,8,4,256]{3,1,2,0:T(8,128)(4,1)S(1)}, u32[]{:S(2)}) copy-start(pred[64,8,4,256]{3,1,2,0:T(8,128)(4,1)S(1)} %copy.23) | copy-start | bytes 1572868
  17.1 27.5 %copy-start.10 = (pred[64,8,4,256]{3,1,2,0:T(8,128)(4,1)}, pred[64,8,4,256]{3,1,2,0:T(8,128)(4,1)S(1)}, u32[]{:S(2)}) copy-start(pred[64,8,4,256]{3,1,2,0:T(8,128)(4,1)S(1)} %copy.25) | copy-start | bytes 1572868
  40.5 2.1 copy-start.8
  42.6 2.1 copy-start.12
  128.7 40.5 %copy-start.5 = (pred[64,8,4,256]{3,1,2,0:T(8,128)(4,1)S(1)}, pred[64,8,4,256]{3,1,2,0:T(8,128)(4,1)}, u32[]{:S(2)}) copy-start(pred[64,8,4,256]{3,1,2,0:T(8,128)(4,1)} %copy-done.4) | copy-start | bytes 1572868
  128.7 40.5 %copy-start.9 = (bf16[1024,512]{0,1:T(8,128)(2,1)S(1)}, bf16[1024,512]{0,1:T(8,128)(2,1)}, u32[]{:S(2)}) copy-start(bf16[1024,512]{0,1:T(8,128)(2,1)} %copy.18) | copy-start | bytes 3145732
  169.1 1.0 copy-start.11
  169.1 1.4 copy-start.13
  170.5 1.0 copy-start.1
  170.5 1.4 copy-start.3
  175.2 61.7 %all-to-all-start.3 = ((f32[32,16,2048]{2,1,0:T(8,128)}), f32[32,16,2048]{2,1,0:T(8,128)}, u32[]{:S(2)}, u32[]{:S(2)}) async-start(f32[32,16,2048]{2,1,0:T(8,128)} %bitcast.17), calls=%async_computation.3 | async-start | bytes 8388608 | tf_op jit(solution)/shard_map/all_to_all | solution.py:46

commit v3 on v2

--- a/solution.py
+++ b/solution.py
@@ -53,6 +53,26 @@
     return gathered.reshape((count * block.shape[0],) + block.shape[1:])
 
 
+def ring_scatter_sum(parts, axis_name):
+    count = lax.axis_size(axis_name)
+    here = lax.axis_index(axis_name)
+    pieces = parts.reshape((count, parts.shape[0] // count) + parts.shape[1:])
+    half = parts.shape[1] // 2
+    ahead, behind = pieces[:, :, :half], pieces[:, :, half:]
+    forward = [(i, (i + 1) % count) for i in range(count)]
+    backward = [(i, (i - 1) % count) for i in range(count)]
+    carry_ahead = lax.dynamic_index_in_dim(ahead, (here - 1) % count, 0, keepdims=False)
+    carry_behind = lax.dynamic_index_in_dim(behind, (here + 1) % count, 0, keepdims=False)
+    for step in range(1, count):
+        carry_ahead = lax.ppermute(carry_ahead, axis_name, forward) + lax.dynamic_index_in_dim(
+            ahead, (here - 1 - step) % count, 0, keepdims=False
+        )
+        carry_behind = lax.ppermute(carry_behind, axis_name, backward) + lax.dynamic_index_in_dim(
+            behind, (here + 1 + step) % count, 0, keepdims=False
+        )
+    return jnp.concatenate([carry_ahead, carry_behind], axis=1)
+
+
 def on_device(tokens, cotangent, w_gate, w_up, w_down, order_gate, order_up, order_down):
     rows_here = w_gate.shape[0] // BLOCK
     cols_here = w_gate.shape[1] // BLOCK
@@ -70,7 +90,7 @@
     gate_term = apply_blocks(tokens_all, w_gate, keep_gate, "forward")
     up_term = apply_blocks(tokens_all, w_up, keep_up, "forward")
     hidden_term = apply_blocks(cotangent_all, w_down, keep_down, "transposed")
-    sums = a2a_scatter_sum(jnp.concatenate([gate_term, up_term, hidden_term], axis=1), "row")
+    sums = ring_scatter_sum(jnp.concatenate([gate_term, up_term, hidden_term], axis=1), "row")
     gate = sums[:, :hidden_here]
     up = sums[:, hidden_here : 2 * hidden_here]
     hidden_grad = sums[:, 2 * hidden_here :]

time: 241 us -> 213 us (0.88)
  blocking collectives: 119 us -> 31.7 us
  starting transfers between devices: 19.8 us -> 51.8 us
  waiting for transfers between devices: 62.9 us -> 88 us
    all_to_all x1 -> x0, blocking collectives: 79 us -> none  [a2a_scatter_sum(): return lax.all_to_all(pieces, axis_name, 0, 0, tiled=True).sum(axis=0)]
    ppermute x0 -> x14, starting transfers between devices: none -> 26.2 us  [the longest x7 25.6 us: ring_scatter_sum(): lax.ppermute(carry_behind, axis_name, backward)]
    ppermute x0 -> x14, waiting for transfers between devices: none -> 25.1 us  [the longest x7 20.4 us: ring_scatter_sum(): lax.ppermute(carry_behind, axis_name, backward)]
    all_to_all x1, blocking collectives: 40.3 us -> 31.7 us  [a2a_gather(): gathered = lax.all_to_all(spread, axis_name, 0, 0, tiled=True)]
    all_to_all x1, starting transfers between devices: 11 us -> 16.8 us  [a2a_scatter_sum(): return lax.all_to_all(pieces, axis_name, 0, 0, tiled=True).sum(axis=0)]
  transfers between devices with their start and end apart: 2 -> 16, of which waited for: 2 -> 13; matrix products, arithmetic and copies ran while one was open for 6% -> 7% of each run, Pallas kernels for 0% -> 0%
where the time goes in v3:
time: 213 us; the launch traced here: 212 us
  waiting for transfers between devices  88 us (41%)
  starting transfers between devices  51.8 us (24%)
  blocking collectives  31.7 us (15%)
  matrix products  18.1 us (8%)
  local copies, waits for them, and re-layouts  14.1 us (7%)
  other arithmetic  7.05 us (3%)
    all_to_all x1, waiting for transfers between devices, a2a_scatter_sum(): return lax.all_to_all(pieces, axis_name, 0, 0, tiled=True).sum(axis=0)  39.6 us
    all_to_all x1, blocking collectives, a2a_gather(): gathered = lax.all_to_all(spread, axis_name, 0, 0, tiled=True)  31.7 us
    ppermute x7, starting transfers between devices, ring_scatter_sum(): lax.ppermute(carry_behind, axis_name, backward)  25.6 us
    all_to_all x1, waiting for transfers between devices, a2a_gather(): gathered = lax.all_to_all(spread, axis_name, 0, 0, tiled=True)  23.3 us
    ppermute x7, waiting for transfers between devices, ring_scatter_sum(): lax.ppermute(carry_behind, axis_name, backward)  20.4 us
    all_to_all x1, starting transfers between devices, a2a_scatter_sum(): return lax.all_to_all(pieces, axis_name, 0, 0, tiled=True).sum(axis=0)  16.8 us
    dot_general x3, matrix products, dense_apply(): lax.dot_general(left_operand, right_operand, (((0,), (0,)), ((), ())), pr...  9.84 us
    all_to_all x1, starting transfers between devices, a2a_gather(): gathered = lax.all_to_all(spread, axis_name, 0, 0, tiled=True)  8.76 us
  transfers between devices with their start and end apart: 16, of which 13 were waited for; matrix products, arithmetic and copies ran while one was open for 7% of the time, Pallas kernels for 0%

profile of v3, /device:TPU:1, one launch (start us, length us, event | category | flops | bytes accessed | tf_op | source)
XLA Modules:
  0.0 211.8 jit_solution(9413351803578352394)
XLA Ops:
  3.0 8.8 %all-to-all-start = ((bf16[32,16,2048]{2,1,0:T(8,128)(2,1)}), bf16[32,16,2048]{2,1,0:T(8,128)(2,1)}, u32[]{:S(2)}, u32[]{:S(2)}) async-start(bf16[32,16,2048]{2,1,0:T(8,128)(2,1)} %broadcast_in_dim.10), calls=%async_computation | async-start | bytes 4194304 | tf_op jit(solution)/shard_map/all_to_all | solution.py:52
  17.2 23.3 %all-to-all-done = bf16[32,16,2048]{2,1,0:T(8,128)(2,1)} async-done(((bf16[32,16,2048]{2,1,0:T(8,128)(2,1)}), bf16[32,16,2048]{2,1,0:T(8,128)(2,1)}, u32[]{:S(2)}, u32[]{:S(2)}) %all-to-all-start) | async-done | bytes 2097184 | tf_op jit(solution)/shard_map/all_to_all | solution.py:52
  51.5 5.7 %collective-permute-start.7 = (f32[64,768]{1,0:T(8,128)S(1)}, f32[64,768]{1,0:T(8,128)S(1)}, u32[]{:S(2)}, u32[]{:S(2)}) collective-permute-start(f32[64,768]{1,0:T(8,128)S(1)} %dynamic-slice_bitcast_fusion), channel_id=1, source_target_pairs={{0,224},{32,0},{64,32},{96,64},{128,96},{160,128},{192,160},{224,1... | collective-permute-start | bytes 589832 | tf_op jit(solution)/shard_map/ppermute | solution.py:70
  57.3 2.5 %collective-permute-done.7 = f32[64,768]{1,0:T(8,128)S(1)} collective-permute-done((f32[64,768]{1,0:T(8,128)S(1)}, f32[64,768]{1,0:T(8,128)S(1)}, u32[]{:S(2)}, u32[]{:S(2)}) %collective-permute-start.7) | collective-permute-done | bytes 196640 | tf_op jit(solution)/shard_map/ppermute | solution.py:70
  59.8 3.5 %collective-permute-start.8 = (f32[64,768]{1,0:T(8,128)S(1)}, f32[64,768]{1,0:T(8,128)S(1)}, u32[]{:S(2)}, u32[]{:S(2)}) collective-permute-start(f32[64,768]{1,0:T(8,128)S(1)} %bitcast_add_fusion.6), channel_id=1, source_target_pairs={{0,224},{32,0},{64,32},{96,64},{128,96},{160,128},{192,160},{224,1... | collective-permute-start | bytes 589832 | tf_op jit(solution)/shard_map/ppermute | solution.py:70
  63.5 2.5 %collective-permute-done.8 = f32[64,768]{1,0:T(8,128)S(1)} collective-permute-done((f32[64,768]{1,0:T(8,128)S(1)}, f32[64,768]{1,0:T(8,128)S(1)}, u32[]{:S(2)}, u32[]{:S(2)}) %collective-permute-start.8) | collective-permute-done | bytes 196640 | tf_op jit(solution)/shard_map/ppermute | solution.py:70
  66.0 3.2 %collective-permute-start.9 = (f32[64,768]{1,0:T(8,128)S(1)}, f32[64,768]{1,0:T(8,128)S(1)}, u32[]{:S(2)}, u32[]{:S(2)}) collective-permute-start(f32[64,768]{1,0:T(8,128)S(1)} %bitcast_add_fusion.5), channel_id=1, source_target_pairs={{0,224},{32,0},{64,32},{96,64},{128,96},{160,128},{192,160},{224,1... | collective-permute-start | bytes 589832 | tf_op jit(solution)/shard_map/ppermute | solution.py:70
  69.3 2.5 %collective-permute-done.9 = f32[64,768]{1,0:T(8,128)S(1)} collective-permute-done((f32[64,768]{1,0:T(8,128)S(1)}, f32[64,768]{1,0:T(8,128)S(1)}, u32[]{:S(2)}, u32[]{:S(2)}) %collective-permute-start.9) | collective-permute-done | bytes 196640 | tf_op jit(solution)/shard_map/ppermute | solution.py:70
  71.8 3.4 %collective-permute-start.10 = (f32[64,768]{1,0:T(8,128)S(1)}, f32[64,768]{1,0:T(8,128)S(1)}, u32[]{:S(2)}, u32[]{:S(2)}) collective-permute-start(f32[64,768]{1,0:T(8,128)S(1)} %bitcast_add_fusion.4), channel_id=1, source_target_pairs={{0,224},{32,0},{64,32},{96,64},{128,96},{160,128},{192,160},{224,1... | collective-permute-start | bytes 589832 | tf_op jit(solution)/shard_map/ppermute | solution.py:70
  75.3 2.7 %collective-permute-done.10 = f32[64,768]{1,0:T(8,128)S(1)} collective-permute-done((f32[64,768]{1,0:T(8,128)S(1)}, f32[64,768]{1,0:T(8,128)S(1)}, u32[]{:S(2)}, u32[]{:S(2)}) %collective-permute-start.10) | collective-permute-done | bytes 196640 | tf_op jit(solution)/shard_map/ppermute | solution.py:70
  78.0 3.2 %collective-permute-start.11 = (f32[64,768]{1,0:T(8,128)S(1)}, f32[64,768]{1,0:T(8,128)S(1)}, u32[]{:S(2)}, u32[]{:S(2)}) collective-permute-start(f32[64,768]{1,0:T(8,128)S(1)} %bitcast_add_fusion.3), channel_id=1, source_target_pairs={{0,224},{32,0},{64,32},{96,64},{128,96},{160,128},{192,160},{224,1... | collective-permute-start | bytes 589832 | tf_op jit(solution)/shard_map/ppermute | solution.py:70
  81.6 3.7 %collective-permute-done.11 = f32[64,768]{1,0:T(8,128)S(1)} collective-permute-done((f32[64,768]{1,0:T(8,128)S(1)}, f32[64,768]{1,0:T(8,128)S(1)}, u32[]{:S(2)}, u32[]{:S(2)}) %collective-permute-start.11) | collective-permute-done | bytes 196640 | tf_op jit(solution)/shard_map/ppermute | solution.py:70
  85.4 3.2 %collective-permute-start.12 = (f32[64,768]{1,0:T(8,128)S(1)}, f32[64,768]{1,0:T(8,128)S(1)}, u32[]{:S(2)}, u32[]{:S(2)}) collective-permute-start(f32[64,768]{1,0:T(8,128)S(1)} %bitcast_add_fusion.2), channel_id=1, source_target_pairs={{0,224},{32,0},{64,32},{96,64},{128,96},{160,128},{192,160},{224,1... | collective-permute-start | bytes 589832 | tf_op jit(solution)/shard_map/ppermute | solution.py:70
  89.1 3.7 %collective-permute-done.12 = f32[64,768]{1,0:T(8,128)S(1)} collective-permute-done((f32[64,768]{1,0:T(8,128)S(1)}, f32[64,768]{1,0:T(8,128)S(1)}, u32[]{:S(2)}, u32[]{:S(2)}) %collective-permute-start.12) | collective-permute-done | bytes 196640 | tf_op jit(solution)/shard_map/ppermute | solution.py:70
  92.8 3.5 %collective-permute-start.13 = (f32[64,768]{1,0:T(8,128)S(1)}, f32[64,768]{1,0:T(8,128)S(1)}, u32[]{:S(2)}, u32[]{:S(2)}) collective-permute-start(f32[64,768]{1,0:T(8,128)S(1)} %bitcast_add_fusion.1), channel_id=1, source_target_pairs={{0,224},{32,0},{64,32},{96,64},{128,96},{160,128},{192,160},{224,1... | collective-permute-start | bytes 589832 | tf_op jit(solution)/shard_map/ppermute | solution.py:70
  96.7 2.9 %collective-permute-done.13 = f32[64,768]{1,0:T(8,128)S(1)} collective-permute-done((f32[64,768]{1,0:T(8,128)S(1)}, f32[64,768]{1,0:T(8,128)S(1)}, u32[]{:S(2)}, u32[]{:S(2)}) %collective-permute-start.13) | collective-permute-done | bytes 196640 | tf_op jit(solution)/shard_map/ppermute | solution.py:70
  99.6 3.7 %collective-permute-done.6 = f32[64,768]{1,0:T(8,128)S(1)} collective-permute-done((f32[64,768]{1,0:T(8,128)S(1)}, f32[64,768]{1,0:T(8,128)S(1)}, u32[]{:S(2)}, u32[]{:S(2)}) %collective-permute-start.6) | collective-permute-done | bytes 196640 | tf_op jit(solution)/shard_map/ppermute | solution.py:67
  103.6 31.7 %all_to_all.15 = bf16[8,64,1536]{2,1,0:T(8,128)(2,1)S(1)} all-to-all(bf16[8,64,1536]{2,1,0:T(8,128)(2,1)S(1)} %broadcast_in_dim.14), channel_id=1, replica_groups=mesh['row'=8,'col'=32] {'row'}, dimensions={0} | all-to-all | bytes 3145728 | tf_op jit(solution)/shard_map/all_to_all | solution.py:52
  138.8 2.5 %pad_maximum_fusion = f32[512,2048]{1,0:T(8,128)} fusion(f32[512,1024]{1,0:T(8,128)S(1)} %convolution_add_fusion, f32[512,1024]{1,0:T(8,128)S(1)} %fusion.9), kind=kLoop, calls=%fused_computation | loop fusion | flops 1048576 | bytes 8388608 | tf_op jit(solution)/shard_map/concatenate | solution.py:114
  141.3 16.8 %all-to-all-start.2 = ((f32[32,16,2048]{2,1,0:T(8,128)}), f32[32,16,2048]{2,1,0:T(8,128)}, u32[]{:S(2)}, u32[]{:S(2)}) async-start(f32[32,16,2048]{2,1,0:T(8,128)} %bitcast.49), calls=%async_computation.2 | async-start | bytes 8388608 | tf_op jit(solution)/shard_map/all_to_all | solution.py:46
  159.4 3.3 %convolution_select_fusion.1 = f32[1024,512]{1,0:T(8,128)} fusion(pred[1024,512]{1,0:T(32,128)(4,1)S(1)} %copy.28, bf16[512,2048]{1,0:T(8,128)(2,1)} %bitcast, bf16[512,1536]{1,0:T(8,128)(2,1)S(1)} %bitcast.57), kind=kOutput, calls=%fused_computation.3 | convolution fusion | flops 537395200 | bytes 4194304 | tf_op jit(solution)/shard_map/dot_general | solution.py:33
  162.7 3.3 %convolution_select_fusion.2 = f32[1024,512]{1,0:T(8,128)} fusion(pred[1024,512]{1,0:T(32,128)(4,1)S(1)} %copy.27, bf16[512,2048]{1,0:T(8,128)(2,1)} %bitcast, bf16[512,1536]{1,0:T(8,128)(2,1)S(1)} %bitcast.58), kind=kOutput, calls=%fused_computation.4 | convolution fusion | flops 537395200 | bytes 4194304 | tf_op jit(solution)/shard_map/dot_general | solution.py:33
  166.0 3.3 %convolution_select_fusion = f32[512,1024]{1,0:T(8,128)} fusion(pred[512,1024]{1,0:T(8,128)(4,1)S(1)} %bitcast.68, bf16[512,2048]{1,0:T(8,128)(2,1)} %bitcast, bf16[512,1536]{1,0:T(8,128)(2,1)S(1)} %bitcast.59), kind=kOutput, calls=%fused_computation.2 | convolution fusion | flops 537395200 | bytes 4194304 | tf_op jit(solution)/shard_map/dot_general | solution.py:33
  169.2 39.6 %all-to-all-done.2 = f32[32,16,2048]{2,1,0:T(8,128)} async-done(((f32[32,16,2048]{2,1,0:T(8,128)}), f32[32,16,2048]{2,1,0:T(8,128)}, u32[]{:S(2)}, u32[]{:S(2)}) %all-to-all-start.2) | async-done | bytes 4194336 | tf_op jit(solution)/shard_map/all_to_all | solution.py:46
  (95 shorter events, 28.5 us)
Async XLA Ops:
  3.0 8.9 %slice-start.1 = ((s32[2048]{0:T(1024)}), s32[1024]{0:T(1024)S(1)}, s32[]{:S(2)}) async-start(s32[2048]{0:T(1024)} %param.14), calls=%async_computation.4 | async-start | bytes 8192 | tf_op jit(solution)/shard_map/slice | solution.py:14
  3.0 9.7 %copy-start.6 = (bf16[1024,512]{1,0:T(8,128)(2,1)S(1)}, bf16[1024,512]{1,0:T(8,128)(2,1)}, u32[]{:S(2)}) copy-start(bf16[1024,512]{1,0:T(8,128)(2,1)} %param.11) | copy-start | bytes 3145732
  3.0 37.5 %all-to-all-start = ((bf16[32,16,2048]{2,1,0:T(8,128)(2,1)}), bf16[32,16,2048]{2,1,0:T(8,128)(2,1)}, u32[]{:S(2)}, u32[]{:S(2)}) async-start(bf16[32,16,2048]{2,1,0:T(8,128)(2,1)} %broadcast_in_dim.10), calls=%async_computation | async-start | bytes 4194304 | tf_op jit(solution)/shard_map/all_to_all | solution.py:52
  12.7 27.8 %copy-start = (pred[64,8,4,256]{3,1,2,0:T(8,128)(4,1)}, pred[64,8,4,256]{3,1,2,0:T(8,128)(4,1)S(1)}, u32[]{:S(2)}) copy-start(pred[64,8,4,256]{3,1,2,0:T(8,128)(4,1)S(1)} %copy.30) | copy-start | bytes 1572868
  13.3 27.2 %copy-start.2 = (bf16[1024,512]{0,1:T(8,128)(2,1)}, bf16[1024,512]{0,1:T(8,128)(2,1)S(1)}, u32[]{:S(2)}) copy-start(bf16[1024,512]{0,1:T(8,128)(2,1)S(1)} %copy.25) | copy-start | bytes 3145732
  14.9 27.6 %copy-start.4 = (pred[64,8,4,256]{3,1,2,0:T(8,128)(4,1)}, pred[64,8,4,256]{3,1,2,0:T(8,128)(4,1)S(1)}, u32[]{:S(2)}) copy-start(pred[64,8,4,256]{3,1,2,0:T(8,128)(4,1)S(1)} %copy.29) | copy-start | bytes 1572868
  17.1 27.5 %copy-start.10 = (pred[64,8,4,256]{3,1,2,0:T(8,128)(4,1)}, pred[64,8,4,256]{3,1,2,0:T(8,128)(4,1)S(1)}, u32[]{:S(2)}) copy-start(pred[64,8,4,256]{3,1,2,0:T(8,128)(4,1)S(1)} %copy.31) | copy-start | bytes 1572868
  51.5 8.3 %collective-permute-start.7 = (f32[64,768]{1,0:T(8,128)S(1)}, f32[64,768]{1,0:T(8,128)S(1)}, u32[]{:S(2)}, u32[]{:S(2)}) collective-permute-start(f32[64,768]{1,0:T(8,128)S(1)} %dynamic-slice_bitcast_fusion), channel_id=1, source_target_pairs={{0,224},{32,0},{64,32},{96,64},{128,96},{160,128},{192,160},{224,1... | collective-permute-start | bytes 589832 | tf_op jit(solution)/shard_map/ppermute | solution.py:70
  57.2 6.1 %collective-permute-start = (f32[64,768]{1,0:T(8,128)S(1)}, f32[64,768]{1,0:T(8,128)S(1)}, u32[]{:S(2)}, u32[]{:S(2)}) collective-permute-start(f32[64,768]{1,0:T(8,128)S(1)} %dynamic-slice_bitcast_fusion.1), channel_id=1, source_target_pairs={{0,32},{32,64},{64,96},{96,128},{128,160},{160,192},{192,224},{224... | collective-permute-start | bytes 589832 | tf_op jit(solution)/shard_map/ppermute | solution.py:67
  59.8 6.1 %collective-permute-start.8 = (f32[64,768]{1,0:T(8,128)S(1)}, f32[64,768]{1,0:T(8,128)S(1)}, u32[]{:S(2)}, u32[]{:S(2)}) collective-permute-start(f32[64,768]{1,0:T(8,128)S(1)} %bitcast_add_fusion.6), channel_id=1, source_target_pairs={{0,224},{32,0},{64,32},{96,64},{128,96},{160,128},{192,160},{224,1... | collective-permute-start | bytes 589832 | tf_op jit(solution)/shard_map/ppermute | solution.py:70
  63.4 5.8 %collective-permute-start.1 = (f32[64,768]{1,0:T(8,128)S(1)}, f32[64,768]{1,0:T(8,128)S(1)}, u32[]{:S(2)}, u32[]{:S(2)}) collective-permute-start(f32[64,768]{1,0:T(8,128)S(1)} %bitcast_add_fusion.13), channel_id=1, source_target_pairs={{0,32},{32,64},{64,96},{96,128},{128,160},{160,192},{192,224},{224... | collective-permute-start | bytes 589832 | tf_op jit(solution)/shard_map/ppermute | solution.py:67
  66.0 5.8 %collective-permute-start.9 = (f32[64,768]{1,0:T(8,128)S(1)}, f32[64,768]{1,0:T(8,128)S(1)}, u32[]{:S(2)}, u32[]{:S(2)}) collective-permute-start(f32[64,768]{1,0:T(8,128)S(1)} %bitcast_add_fusion.5), channel_id=1, source_target_pairs={{0,224},{32,0},{64,32},{96,64},{128,96},{160,128},{192,160},{224,1... | collective-permute-start | bytes 589832 | tf_op jit(solution)/shard_map/ppermute | solution.py:70
  69.2 6.0 %collective-permute-start.2 = (f32[64,768]{1,0:T(8,128)S(1)}, f32[64,768]{1,0:T(8,128)S(1)}, u32[]{:S(2)}, u32[]{:S(2)}) collective-permute-start(f32[64,768]{1,0:T(8,128)S(1)} %bitcast_add_fusion.12), channel_id=1, source_target_pairs={{0,32},{32,64},{64,96},{96,128},{128,160},{160,192},{192,224},{224... | collective-permute-start | bytes 589832 | tf_op jit(solution)/shard_map/ppermute | solution.py:67
  71.8 6.2 %collective-permute-start.10 = (f32[64,768]{1,0:T(8,128)S(1)}, f32[64,768]{1,0:T(8,128)S(1)}, u32[]{:S(2)}, u32[]{:S(2)}) collective-permute-start(f32[64,768]{1,0:T(8,128)S(1)} %bitcast_add_fusion.4), channel_id=1, source_target_pairs={{0,224},{32,0},{64,32},{96,64},{128,96},{160,128},{192,160},{224,1... | collective-permute-start | bytes 589832 | tf_op jit(solution)/shard_map/ppermute | solution.py:70
  75.2 6.3 %collective-permute-start.3 = (f32[64,768]{1,0:T(8,128)S(1)}, f32[64,768]{1,0:T(8,128)S(1)}, u32[]{:S(2)}, u32[]{:S(2)}) collective-permute-start(f32[64,768]{1,0:T(8,128)S(1)} %bitcast_add_fusion.11), channel_id=1, source_target_pairs={{0,32},{32,64},{64,96},{96,128},{128,160},{160,192},{192,224},{224... | collective-permute-start | bytes 589832 | tf_op jit(solution)/shard_map/ppermute | solution.py:67
  78.0 7.3 %collective-permute-start.11 = (f32[64,768]{1,0:T(8,128)S(1)}, f32[64,768]{1,0:T(8,128)S(1)}, u32[]{:S(2)}, u32[]{:S(2)}) collective-permute-start(f32[64,768]{1,0:T(8,128)S(1)} %bitcast_add_fusion.3), channel_id=1, source_target_pairs={{0,224},{32,0},{64,32},{96,64},{128,96},{160,128},{192,160},{224,1... | collective-permute-start | bytes 589832 | tf_op jit(solution)/shard_map/ppermute | solution.py:70
  81.5 7.4 %collective-permute-start.4 = (f32[64,768]{1,0:T(8,128)S(1)}, f32[64,768]{1,0:T(8,128)S(1)}, u32[]{:S(2)}, u32[]{:S(2)}) collective-permute-start(f32[64,768]{1,0:T(8,128)S(1)} %bitcast_add_fusion.10), channel_id=1, source_target_pairs={{0,32},{32,64},{64,96},{96,128},{128,160},{160,192},{192,224},{224... | collective-permute-start | bytes 589832 | tf_op jit(solution)/shard_map/ppermute | solution.py:67
  85.4 7.4 %collective-permute-start.12 = (f32[64,768]{1,0:T(8,128)S(1)}, f32[64,768]{1,0:T(8,128)S(1)}, u32[]{:S(2)}, u32[]{:S(2)}) collective-permute-start(f32[64,768]{1,0:T(8,128)S(1)} %bitcast_add_fusion.2), channel_id=1, source_target_pairs={{0,224},{32,0},{64,32},{96,64},{128,96},{160,128},{192,160},{224,1... | collective-permute-start | bytes 589832 | tf_op jit(solution)/shard_map/ppermute | solution.py:70
  89.0 7.6 %collective-permute-start.5 = (f32[64,768]{1,0:T(8,128)S(1)}, f32[64,768]{1,0:T(8,128)S(1)}, u32[]{:S(2)}, u32[]{:S(2)}) collective-permute-start(f32[64,768]{1,0:T(8,128)S(1)} %bitcast_add_fusion.9), channel_id=1, source_target_pairs={{0,32},{32,64},{64,96},{96,128},{128,160},{160,192},{192,224},{224... | collective-permute-start | bytes 589832 | tf_op jit(solution)/shard_map/ppermute | solution.py:67
  92.8 6.8 %collective-permute-start.13 = (f32[64,768]{1,0:T(8,128)S(1)}, f32[64,768]{1,0:T(8,128)S(1)}, u32[]{:S(2)}, u32[]{:S(2)}) collective-permute-start(f32[64,768]{1,0:T(8,128)S(1)} %bitcast_add_fusion.1), channel_id=1, source_target_pairs={{0,224},{32,0},{64,32},{96,64},{128,96},{160,128},{192,160},{224,1... | collective-permute-start | bytes 589832 | tf_op jit(solution)/shard_map/ppermute | solution.py:70
  96.6 6.7 %collective-permute-start.6 = (f32[64,768]{1,0:T(8,128)S(1)}, f32[64,768]{1,0:T(8,128)S(1)}, u32[]{:S(2)}, u32[]{:S(2)}) collective-permute-start(f32[64,768]{1,0:T(8,128)S(1)} %bitcast_add_fusion.8), channel_id=1, source_target_pairs={{0,32},{32,64},{64,96},{96,128},{128,160},{160,192},{192,224},{224... | collective-permute-start | bytes 589832 | tf_op jit(solution)/shard_map/ppermute | solution.py:67
  103.4 31.8 %copy-start.5 = (pred[64,8,4,256]{3,1,2,0:T(8,128)(4,1)S(1)}, pred[64,8,4,256]{3,1,2,0:T(8,128)(4,1)}, u32[]{:S(2)}) copy-start(pred[64,8,4,256]{3,1,2,0:T(8,128)(4,1)} %copy-done.4) | copy-start | bytes 1572868
  103.4 31.8 %copy-start.9 = (bf16[1024,512]{0,1:T(8,128)(2,1)S(1)}, bf16[1024,512]{0,1:T(8,128)(2,1)}, u32[]{:S(2)}) copy-start(bf16[1024,512]{0,1:T(8,128)(2,1)} %copy.24) | copy-start | bytes 3145732
  141.3 67.5 %all-to-all-start.2 = ((f32[32,16,2048]{2,1,0:T(8,128)}), f32[32,16,2048]{2,1,0:T(8,128)}, u32[]{:S(2)}, u32[]{:S(2)}) async-start(f32[32,16,2048]{2,1,0:T(8,128)} %bitcast.49), calls=%async_computation.2 | async-start | bytes 8388608 | tf_op jit(solution)/shard_map/all_to_all | solution.py:46
  (9 other events, 22.5 us)

commit v4 on v3

--- a/solution.py
+++ b/solution.py
@@ -1,7 +1,7 @@
 import jax
 import jax.numpy as jnp
 from jax import lax
-from jax.sharding import PartitionSpec as P
+from jax.sharding import Mesh, PartitionSpec as P
 
 BLOCK = 256
 
@@ -73,19 +73,39 @@
     return jnp.concatenate([carry_ahead, carry_behind], axis=1)
 
 
+def col_gather(block):
+    chips = lax.axis_size("chip")
+    core = lax.axis_index("core")
+    spread = jnp.broadcast_to(block[None], (chips,) + block.shape)
+    mine = lax.all_to_all(spread, "chip", 0, 0, tiled=True)
+    other = lax.ppermute(mine, "core", [(0, 1), (1, 0)])
+    paired = jnp.where(core == 0, jnp.stack([mine, other], 1), jnp.stack([other, mine], 1))
+    return paired.reshape((chips * 2 * block.shape[0],) + block.shape[1:])
+
+
+def col_scatter_sum(parts):
+    chips = lax.axis_size("chip")
+    core = lax.axis_index("core")
+    pieces = parts.reshape((chips, 2, parts.shape[0] // (2 * chips)) + parts.shape[1:])
+    mine = lax.dynamic_index_in_dim(pieces, core, 1, keepdims=False)
+    other = lax.dynamic_index_in_dim(pieces, 1 - core, 1, keepdims=False)
+    pair_sum = mine + lax.ppermute(other, "core", [(0, 1), (1, 0)])
+    return lax.all_to_all(pair_sum, "chip", 0, 0, tiled=True).sum(axis=0)
+
+
 def on_device(tokens, cotangent, w_gate, w_up, w_down, order_gate, order_up, order_down):
     rows_here = w_gate.shape[0] // BLOCK
     cols_here = w_gate.shape[1] // BLOCK
     row_start = lax.axis_index("row") * rows_here
-    col_start = lax.axis_index("col") * cols_here
+    col_start = (lax.axis_index("chip") * 2 + lax.axis_index("core")) * cols_here
     width_blocks = rows_here * lax.axis_size("row")
-    hidden_blocks = cols_here * lax.axis_size("col")
+    hidden_blocks = cols_here * lax.axis_size("chip") * 2
     hidden_here = w_gate.shape[1]
     keep_gate = kept_table(order_gate, row_start, col_start, rows_here, cols_here, hidden_blocks)
     keep_up = kept_table(order_up, row_start, col_start, rows_here, cols_here, hidden_blocks)
     keep_down = kept_table(order_down, col_start, row_start, cols_here, rows_here, width_blocks)
     width_here = tokens.shape[1]
-    inputs_all = a2a_gather(jnp.concatenate([tokens, cotangent], axis=1), "col")
+    inputs_all = col_gather(jnp.concatenate([tokens, cotangent], axis=1))
     tokens_all, cotangent_all = inputs_all[:, :width_here], inputs_all[:, width_here:]
     gate_term = apply_blocks(tokens_all, w_gate, keep_gate, "forward")
     up_term = apply_blocks(tokens_all, w_up, keep_up, "forward")
@@ -111,7 +131,7 @@
     up_weight_grad = apply_blocks(tokens_all, up_grad_all, keep_up, "weights")
     through_gate = apply_blocks(gate_grad_all, w_gate, keep_gate, "transposed")
     through_up = apply_blocks(up_grad_all, w_up, keep_up, "transposed")
-    outs = a2a_scatter_sum(jnp.concatenate([output_term, through_gate + through_up], axis=1), "col")
+    outs = col_scatter_sum(jnp.concatenate([output_term, through_gate + through_up], axis=1))
     output = outs[:, :width_here].astype(jnp.bfloat16)
     input_grad = outs[:, width_here:]
     return (
@@ -124,26 +144,29 @@
 
 
 def solution(mesh):
+    rows, cols = mesh.devices.shape
+    split = Mesh(mesh.devices.reshape(rows, cols // 2, 2), ("row", "chip", "core"))
+    col = ("chip", "core")
     placed = (
-        P("col", "row"),
-        P("col", "row"),
-        P("row", "col"),
-        P("row", "col"),
-        P("col", "row"),
+        P(col, "row"),
+        P(col, "row"),
+        P("row", col),
+        P("row", col),
+        P(col, "row"),
         P(),
         P(),
         P(),
     )
     return jax.shard_map(
         on_device,
-        mesh=mesh,
+        mesh=split,
         in_specs=placed,
         out_specs=(
-            P("col", "row"),
-            P("col", "row"),
-            P("row", "col"),
-            P("row", "col"),
-            P("col", "row"),
+            P(col, "row"),
+            P(col, "row"),
+            P("row", col),
+            P("row", col),
+            P(col, "row"),
         ),
         check_vma=False,
     )

time: 213 us -> 197 us (0.925)
  starting transfers between devices: 51.8 us -> 42 us
  blocking collectives: 31.7 us -> 23.4 us
  local copies, waits for them, and re-layouts: 14.1 us -> 21.1 us
  matrix products: 18.1 us -> 11.9 us
    all_to_all x1, waiting for transfers between devices: 39.6 us -> 23.8 us  [col_scatter_sum(): return lax.all_to_all(pair_sum, 'chip', 0, 0, tiled=True).sum(axis=0)]
    all_to_all x1, starting transfers between devices: 16.8 us -> 4.07 us  [col_scatter_sum(): return lax.all_to_all(pair_sum, 'chip', 0, 0, tiled=True).sum(axis=0)]
    all_to_all x1, waiting for transfers between devices: 23.3 us -> 34.8 us  [a2a_gather(): gathered = lax.all_to_all(spread, axis_name, 0, 0, tiled=True)]
    all_to_all x1, blocking collectives: 31.7 us -> 23.4 us  [col_gather(): mine = lax.all_to_all(spread, 'chip', 0, 0, tiled=True)]
    ppermute x0 -> x2, starting transfers between devices: none -> 8.15 us  [the longest x1 6.08 us: col_scatter_sum(): pair_sum = mine + lax.ppermute(other, 'core', [(0, 1), (1, 0)])]
    unnamed x33 -> x43, local copies, waits for them, and re-layouts: 4.94 us -> 10.5 us
    all_to_all x1, starting transfers between devices: 8.76 us -> 3.58 us  [a2a_gather(): gathered = lax.all_to_all(spread, axis_name, 0, 0, tiled=True)]
    ppermute x0 -> x2, waiting for transfers between devices: none -> 4 us  [the longest x1 4 us: col_scatter_sum(): pair_sum = mine + lax.ppermute(other, 'core', [(0, 1), (1, 0)])]
  transfers between devices with their start and end apart: 16 -> 18, of which waited for: 13 -> 12; matrix products, arithmetic and copies ran while one was open for 7% -> 8% of each run, Pallas kernels for 0% -> 0%
where the time goes in v4:
time: 197 us; the launch traced here: 196 us
  waiting for transfers between devices  89.1 us (45%)
  starting transfers between devices  42 us (21%)
  blocking collectives  23.4 us (12%)
  local copies, waits for them, and re-layouts  21.1 us (11%)
  matrix products  11.9 us (6%)
  other arithmetic  7.87 us (4%)
    all_to_all x1, waiting for transfers between devices, a2a_gather(): gathered = lax.all_to_all(spread, axis_name, 0, 0, tiled=True)  34.8 us
    ppermute x7, starting transfers between devices, ring_scatter_sum(): lax.ppermute(carry_behind, axis_name, backward)  25.6 us
    all_to_all x1, waiting for transfers between devices, col_scatter_sum(): return lax.all_to_all(pair_sum, 'chip', 0, 0, tiled=True).sum(axis=0)  23.8 us
    all_to_all x1, blocking collectives, col_gather(): mine = lax.all_to_all(spread, 'chip', 0, 0, tiled=True)  23.4 us
    ppermute x7, waiting for transfers between devices, ring_scatter_sum(): lax.ppermute(carry_behind, axis_name, backward)  22.2 us
    unnamed x43, local copies, waits for them, and re-layouts  10.5 us
    dot_general x3, matrix products, dense_apply(): lax.dot_general(left_operand, right_operand, (((0,), (0,)), ((), ())), pr...  7.55 us
    ppermute x1, starting transfers between devices, col_scatter_sum(): pair_sum = mine + lax.ppermute(other, 'core', [(0, 1), (1, 0)])  6.08 us
  transfers between devices with their start and end apart: 18, of which 12 were waited for; matrix products, arithmetic and copies ran while one was open for 8% of the time, Pallas kernels for 0%

profile of v4, /device:TPU:1, one launch (start us, length us, event | category | flops | bytes accessed | tf_op | source)
XLA Modules:
  0.0 196.4 jit_solution(17170802709656790718)
XLA Ops:
  1.6 23.4 %all_to_all.15 = bf16[16,16,2048]{2,1,0:T(8,128)(2,1)S(1)} all-to-all(bf16[16,16,2048]{2,1,0:T(8,128)(2,1)S(1)} %broadcast_in_dim.10), channel_id=1, replica_groups=mesh['row'=8,'chip'=16,'core'=2] {'chip'}, dimensions={0} | all-to-all | bytes 2097152 | tf_op jit(solution)/shard_map/all_to_all | solution.py:80
  45.3 5.7 %collective-permute-start.8 = (f32[64,768]{1,0:T(8,128)S(1)}, f32[64,768]{1,0:T(8,128)S(1)}, u32[]{:S(2)}, u32[]{:S(2)}) collective-permute-start(f32[64,768]{1,0:T(8,128)S(1)} %dynamic-slice_bitcast_fusion.1), channel_id=1, source_target_pairs={{0,224},{32,0},{64,32},{96,64},{128,96},{160,128},{192,160},{224,1... | collective-permute-start | bytes 589832 | tf_op jit(solution)/shard_map/ppermute | solution.py:70
  51.1 4.1 %collective-permute-done.8 = f32[64,768]{1,0:T(8,128)S(1)} collective-permute-done((f32[64,768]{1,0:T(8,128)S(1)}, f32[64,768]{1,0:T(8,128)S(1)}, u32[]{:S(2)}, u32[]{:S(2)}) %collective-permute-start.8) | collective-permute-done | bytes 196640 | tf_op jit(solution)/shard_map/ppermute | solution.py:70
  55.2 3.5 %collective-permute-start.9 = (f32[64,768]{1,0:T(8,128)S(1)}, f32[64,768]{1,0:T(8,128)S(1)}, u32[]{:S(2)}, u32[]{:S(2)}) collective-permute-start(f32[64,768]{1,0:T(8,128)S(1)} %bitcast_add_fusion.7), channel_id=1, source_target_pairs={{0,224},{32,0},{64,32},{96,64},{128,96},{160,128},{192,160},{224,1... | collective-permute-start | bytes 589832 | tf_op jit(solution)/shard_map/ppermute | solution.py:70
  58.8 3.3 %collective-permute-done.9 = f32[64,768]{1,0:T(8,128)S(1)} collective-permute-done((f32[64,768]{1,0:T(8,128)S(1)}, f32[64,768]{1,0:T(8,128)S(1)}, u32[]{:S(2)}, u32[]{:S(2)}) %collective-permute-start.9) | collective-permute-done | bytes 196640 | tf_op jit(solution)/shard_map/ppermute | solution.py:70
  62.2 3.5 %collective-permute-start.10 = (f32[64,768]{1,0:T(8,128)S(1)}, f32[64,768]{1,0:T(8,128)S(1)}, u32[]{:S(2)}, u32[]{:S(2)}) collective-permute-start(f32[64,768]{1,0:T(8,128)S(1)} %bitcast_add_fusion.6), channel_id=1, source_target_pairs={{0,224},{32,0},{64,32},{96,64},{128,96},{160,128},{192,160},{224,1... | collective-permute-start | bytes 589832 | tf_op jit(solution)/shard_map/ppermute | solution.py:70
  65.8 2.5 %collective-permute-done.10 = f32[64,768]{1,0:T(8,128)S(1)} collective-permute-done((f32[64,768]{1,0:T(8,128)S(1)}, f32[64,768]{1,0:T(8,128)S(1)}, u32[]{:S(2)}, u32[]{:S(2)}) %collective-permute-start.10) | collective-permute-done | bytes 196640 | tf_op jit(solution)/shard_map/ppermute | solution.py:70
  68.3 3.4 %collective-permute-start.11 = (f32[64,768]{1,0:T(8,128)S(1)}, f32[64,768]{1,0:T(8,128)S(1)}, u32[]{:S(2)}, u32[]{:S(2)}) collective-permute-start(f32[64,768]{1,0:T(8,128)S(1)} %bitcast_add_fusion.5), channel_id=1, source_target_pairs={{0,224},{32,0},{64,32},{96,64},{128,96},{160,128},{192,160},{224,1... | collective-permute-start | bytes 589832 | tf_op jit(solution)/shard_map/ppermute | solution.py:70
  71.8 2.5 %collective-permute-done.11 = f32[64,768]{1,0:T(8,128)S(1)} collective-permute-done((f32[64,768]{1,0:T(8,128)S(1)}, f32[64,768]{1,0:T(8,128)S(1)}, u32[]{:S(2)}, u32[]{:S(2)}) %collective-permute-start.11) | collective-permute-done | bytes 196640 | tf_op jit(solution)/shard_map/ppermute | solution.py:70
  74.3 3.2 %collective-permute-start.12 = (f32[64,768]{1,0:T(8,128)S(1)}, f32[64,768]{1,0:T(8,128)S(1)}, u32[]{:S(2)}, u32[]{:S(2)}) collective-permute-start(f32[64,768]{1,0:T(8,128)S(1)} %bitcast_add_fusion.4), channel_id=1, source_target_pairs={{0,224},{32,0},{64,32},{96,64},{128,96},{160,128},{192,160},{224,1... | collective-permute-start | bytes 589832 | tf_op jit(solution)/shard_map/ppermute | solution.py:70
  77.6 2.5 %collective-permute-done.12 = f32[64,768]{1,0:T(8,128)S(1)} collective-permute-done((f32[64,768]{1,0:T(8,128)S(1)}, f32[64,768]{1,0:T(8,128)S(1)}, u32[]{:S(2)}, u32[]{:S(2)}) %collective-permute-start.12) | collective-permute-done | bytes 196640 | tf_op jit(solution)/shard_map/ppermute | solution.py:70
  80.1 3.2 %collective-permute-start.13 = (f32[64,768]{1,0:T(8,128)S(1)}, f32[64,768]{1,0:T(8,128)S(1)}, u32[]{:S(2)}, u32[]{:S(2)}) collective-permute-start(f32[64,768]{1,0:T(8,128)S(1)} %bitcast_add_fusion.3), channel_id=1, source_target_pairs={{0,224},{32,0},{64,32},{96,64},{128,96},{160,128},{192,160},{224,1... | collective-permute-start | bytes 589832 | tf_op jit(solution)/shard_map/ppermute | solution.py:70
  83.5 3.2 %collective-permute-done.13 = f32[64,768]{1,0:T(8,128)S(1)} collective-permute-done((f32[64,768]{1,0:T(8,128)S(1)}, f32[64,768]{1,0:T(8,128)S(1)}, u32[]{:S(2)}, u32[]{:S(2)}) %collective-permute-start.13) | collective-permute-done | bytes 196640 | tf_op jit(solution)/shard_map/ppermute | solution.py:70
  86.7 3.2 %collective-permute-start.14 = (f32[64,768]{1,0:T(8,128)S(1)}, f32[64,768]{1,0:T(8,128)S(1)}, u32[]{:S(2)}, u32[]{:S(2)}) collective-permute-start(f32[64,768]{1,0:T(8,128)S(1)} %bitcast_add_fusion.2), channel_id=1, source_target_pairs={{0,224},{32,0},{64,32},{96,64},{128,96},{160,128},{192,160},{224,1... | collective-permute-start | bytes 589832 | tf_op jit(solution)/shard_map/ppermute | solution.py:70
  90.3 4.1 %collective-permute-done.14 = f32[64,768]{1,0:T(8,128)S(1)} collective-permute-done((f32[64,768]{1,0:T(8,128)S(1)}, f32[64,768]{1,0:T(8,128)S(1)}, u32[]{:S(2)}, u32[]{:S(2)}) %collective-permute-start.14) | collective-permute-done | bytes 196640 | tf_op jit(solution)/shard_map/ppermute | solution.py:70
  94.5 3.9 %collective-permute-done.7 = f32[64,768]{1,0:T(8,128)S(1)} collective-permute-done((f32[64,768]{1,0:T(8,128)S(1)}, f32[64,768]{1,0:T(8,128)S(1)}, u32[]{:S(2)}, u32[]{:S(2)}) %collective-permute-start.7) | collective-permute-done | bytes 196640 | tf_op jit(solution)/shard_map/ppermute | solution.py:67
  99.8 3.6 %all-to-all-start.1 = ((bf16[8,64,1536]{2,1,0:T(8,128)(2,1)}), bf16[8,64,1536]{2,1,0:T(8,128)(2,1)S(1)}, u32[]{:S(2)}, u32[]{:S(2)}) async-start(bf16[8,64,1536]{2,1,0:T(8,128)(2,1)} %broadcast_in_dim.14), calls=%async_computation.1 | async-start | bytes 3145728 | tf_op jit(solution)/shard_map/all_to_all | solution.py:52
  103.4 34.8 %all-to-all-done.1 = bf16[8,64,1536]{2,1,0:T(8,128)(2,1)S(1)} async-done(((bf16[8,64,1536]{2,1,0:T(8,128)(2,1)}), bf16[8,64,1536]{2,1,0:T(8,128)(2,1)S(1)}, u32[]{:S(2)}, u32[]{:S(2)}) %all-to-all-start.1) | async-done | bytes 1572896 | tf_op jit(solution)/shard_map/all_to_all | solution.py:52
  145.5 6.1 %collective-permute-start.15 = (f32[16,16,2048]{2,1,0:T(8,128)}, f32[16,16,2048]{2,1,0:T(8,128)S(1)}, u32[]{:S(2)}, u32[]{:S(2)}) collective-permute-start(f32[16,16,2048]{2,1,0:T(8,128)} %dynamic-slice_bitcast_fusion), channel_id=1, source_target_pairs={{0,1},{1,0},{2,3},{3,2},{4,5},{5,4},{6,7},{7,6},{8,9},{9,8},{10,11... | collective-permute-start | bytes 6291464 | tf_op jit(solution)/shard_map/ppermute | solution.py:92
  151.6 4.0 %collective-permute-done.15 = f32[16,16,2048]{2,1,0:T(8,128)S(1)} collective-permute-done((f32[16,16,2048]{2,1,0:T(8,128)}, f32[16,16,2048]{2,1,0:T(8,128)S(1)}, u32[]{:S(2)}, u32[]{:S(2)}) %collective-permute-start.15) | collective-permute-done | bytes 2097184 | tf_op jit(solution)/shard_map/ppermute | solution.py:92
  155.6 3.3 %bitcast_add_fusion = f32[16,16,2048]{2,1,0:T(8,128)} fusion(f32[16,16,2048]{2,1,0:T(8,128)S(1)} %collective-permute-done.15, f32[16,2,16,2048]{3,2,1,0:T(8,128)} %bitcast.56, s32[]{:T(128)S(6)} %select_n.170), kind=kLoop, calls=%fused_computation.3 | loop fusion | flops 524288 | bytes 6291460 | tf_op jit(solution)/shard_map/add | solution.py:92
  158.9 4.1 %all-to-all-start.2 = ((f32[16,16,2048]{2,1,0:T(8,128)}), f32[16,16,2048]{2,1,0:T(8,128)S(1)}, u32[]{:S(2)}, u32[]{:S(2)}) async-start(f32[16,16,2048]{2,1,0:T(8,128)} %bitcast_add_fusion), calls=%async_computation.2 | async-start | bytes 4194304 | tf_op jit(solution)/shard_map/all_to_all | solution.py:93
  164.4 3.4 %convolution_select_fusion.1 = f32[1024,512]{1,0:T(8,128)} fusion(pred[1024,512]{1,0:T(32,128)(4,1)S(1)} %copy.28, bf16[512,2048]{1,0:T(8,128)(2,1)} %bitcast.71, bf16[512,1536]{1,0:T(8,128)(2,1)S(1)} %bitcast.65), kind=kOutput, calls=%fused_computation.6 | convolution fusion | flops 537395200 | bytes 4194304 | tf_op jit(solution)/shard_map/dot_general | solution.py:33
  171.9 23.8 %all-to-all-done.2 = f32[16,16,2048]{2,1,0:T(8,128)S(1)} async-done(((f32[16,16,2048]{2,1,0:T(8,128)}), f32[16,16,2048]{2,1,0:T(8,128)S(1)}, u32[]{:S(2)}, u32[]{:S(2)}) %all-to-all-start.2) | async-done | bytes 2097184 | tf_op jit(solution)/shard_map/all_to_all | solution.py:93
  (112 shorter events, 37.1 us)
Async XLA Ops:
  0.6 26.5 %slice-start = ((s32[2048]{0:T(1024)}), s32[1024]{0:T(1024)S(1)}, s32[]{:S(2)}) async-start(s32[2048]{0:T(1024)} %param.13), calls=%async_computation.3 | async-start | bytes 8192 | tf_op jit(solution)/shard_map/slice | solution.py:14
  0.6 26.5 %slice-start.1 = ((s32[2048]{0:T(1024)}), s32[1024]{0:T(1024)S(1)}, s32[]{:S(2)}) async-start(s32[2048]{0:T(1024)} %param.14), calls=%async_computation.4 | async-start | bytes 8192 | tf_op jit(solution)/shard_map/slice | solution.py:14
  25.0 9.5 %collective-permute-start = (bf16[16,16,2048]{2,1,0:T(8,128)(2,1)S(1)}, bf16[16,16,2048]{2,1,0:T(8,128)(2,1)}, u32[]{:S(2)}, u32[]{:S(2)}) collective-permute-start(bf16[16,16,2048]{2,1,0:T(8,128)(2,1)S(1)} %all_to_all.15), channel_id=1, source_target_pairs={{0,1},{1,0},{2,3},{3,2},{4,5},{5,4},{6,7},{7,6},{8,9},{9,8},{10,11... | collective-permute-start | bytes 3145736 | tf_op jit(solution)/shard_map/ppermute | solution.py:81
  28.0 8.3 %copy-start.1 = (pred[64,8,4,256]{3,1,2,0:T(8,128)(4,1)}, pred[64,8,4,256]{3,1,2,0:T(8,128)(4,1)S(1)}, u32[]{:S(2)}) copy-start(pred[64,8,4,256]{3,1,2,0:T(8,128)(4,1)S(1)} %copy.30) | copy-start | bytes 1572868
  30.3 6.8 %copy-start.9 = (pred[64,8,4,256]{3,1,2,0:T(8,128)(4,1)}, pred[64,8,4,256]{3,1,2,0:T(8,128)(4,1)S(1)}, u32[]{:S(2)}) copy-start(pred[64,8,4,256]{3,1,2,0:T(8,128)(4,1)S(1)} %copy.29) | copy-start | bytes 1572868
  45.3 9.9 %collective-permute-start.8 = (f32[64,768]{1,0:T(8,128)S(1)}, f32[64,768]{1,0:T(8,128)S(1)}, u32[]{:S(2)}, u32[]{:S(2)}) collective-permute-start(f32[64,768]{1,0:T(8,128)S(1)} %dynamic-slice_bitcast_fusion.1), channel_id=1, source_target_pairs={{0,224},{32,0},{64,32},{96,64},{128,96},{160,128},{192,160},{224,1... | collective-permute-start | bytes 589832 | tf_op jit(solution)/shard_map/ppermute | solution.py:70
  51.0 7.8 %collective-permute-start.1 = (f32[64,768]{1,0:T(8,128)S(1)}, f32[64,768]{1,0:T(8,128)S(1)}, u32[]{:S(2)}, u32[]{:S(2)}) collective-permute-start(f32[64,768]{1,0:T(8,128)S(1)} %dynamic-slice_bitcast_fusion.2), channel_id=1, source_target_pairs={{0,32},{32,64},{64,96},{96,128},{128,160},{160,192},{192,224},{224... | collective-permute-start | bytes 589832 | tf_op jit(solution)/shard_map/ppermute | solution.py:67
  55.2 6.9 %collective-permute-start.9 = (f32[64,768]{1,0:T(8,128)S(1)}, f32[64,768]{1,0:T(8,128)S(1)}, u32[]{:S(2)}, u32[]{:S(2)}) collective-permute-start(f32[64,768]{1,0:T(8,128)S(1)} %bitcast_add_fusion.7), channel_id=1, source_target_pairs={{0,224},{32,0},{64,32},{96,64},{128,96},{160,128},{192,160},{224,1... | collective-permute-start | bytes 589832 | tf_op jit(solution)/shard_map/ppermute | solution.py:70
  58.8 6.9 %collective-permute-start.2 = (f32[64,768]{1,0:T(8,128)S(1)}, f32[64,768]{1,0:T(8,128)S(1)}, u32[]{:S(2)}, u32[]{:S(2)}) collective-permute-start(f32[64,768]{1,0:T(8,128)S(1)} %bitcast_add_fusion.14), channel_id=1, source_target_pairs={{0,32},{32,64},{64,96},{96,128},{128,160},{160,192},{192,224},{224... | collective-permute-start | bytes 589832 | tf_op jit(solution)/shard_map/ppermute | solution.py:67
  62.2 6.1 %collective-permute-start.10 = (f32[64,768]{1,0:T(8,128)S(1)}, f32[64,768]{1,0:T(8,128)S(1)}, u32[]{:S(2)}, u32[]{:S(2)}) collective-permute-start(f32[64,768]{1,0:T(8,128)S(1)} %bitcast_add_fusion.6), channel_id=1, source_target_pairs={{0,224},{32,0},{64,32},{96,64},{128,96},{160,128},{192,160},{224,1... | collective-permute-start | bytes 589832 | tf_op jit(solution)/shard_map/ppermute | solution.py:70
  65.7 6.0 %collective-permute-start.3 = (f32[64,768]{1,0:T(8,128)S(1)}, f32[64,768]{1,0:T(8,128)S(1)}, u32[]{:S(2)}, u32[]{:S(2)}) collective-permute-start(f32[64,768]{1,0:T(8,128)S(1)} %bitcast_add_fusion.13), channel_id=1, source_target_pairs={{0,32},{32,64},{64,96},{96,128},{128,160},{160,192},{192,224},{224... | collective-permute-start | bytes 589832 | tf_op jit(solution)/shard_map/ppermute | solution.py:67
  68.3 6.0 %collective-permute-start.11 = (f32[64,768]{1,0:T(8,128)S(1)}, f32[64,768]{1,0:T(8,128)S(1)}, u32[]{:S(2)}, u32[]{:S(2)}) collective-permute-start(f32[64,768]{1,0:T(8,128)S(1)} %bitcast_add_fusion.5), channel_id=1, source_target_pairs={{0,224},{32,0},{64,32},{96,64},{128,96},{160,128},{192,160},{224,1... | collective-permute-start | bytes 589832 | tf_op jit(solution)/shard_map/ppermute | solution.py:70
  71.7 5.8 %collective-permute-start.4 = (f32[64,768]{1,0:T(8,128)S(1)}, f32[64,768]{1,0:T(8,128)S(1)}, u32[]{:S(2)}, u32[]{:S(2)}) collective-permute-start(f32[64,768]{1,0:T(8,128)S(1)} %bitcast_add_fusion.12), channel_id=1, source_target_pairs={{0,32},{32,64},{64,96},{96,128},{128,160},{160,192},{192,224},{224... | collective-permute-start | bytes 589832 | tf_op jit(solution)/shard_map/ppermute | solution.py:67
  74.3 5.8 %collective-permute-start.12 = (f32[64,768]{1,0:T(8,128)S(1)}, f32[64,768]{1,0:T(8,128)S(1)}, u32[]{:S(2)}, u32[]{:S(2)}) collective-permute-start(f32[64,768]{1,0:T(8,128)S(1)} %bitcast_add_fusion.4), channel_id=1, source_target_pairs={{0,224},{32,0},{64,32},{96,64},{128,96},{160,128},{192,160},{224,1... | collective-permute-start | bytes 589832 | tf_op jit(solution)/shard_map/ppermute | solution.py:70
  77.5 5.8 %collective-permute-start.5 = (f32[64,768]{1,0:T(8,128)S(1)}, f32[64,768]{1,0:T(8,128)S(1)}, u32[]{:S(2)}, u32[]{:S(2)}) collective-permute-start(f32[64,768]{1,0:T(8,128)S(1)} %bitcast_add_fusion.11), channel_id=1, source_target_pairs={{0,32},{32,64},{64,96},{96,128},{128,160},{160,192},{192,224},{224... | collective-permute-start | bytes 589832 | tf_op jit(solution)/shard_map/ppermute | solution.py:67
  80.1 6.6 %collective-permute-start.13 = (f32[64,768]{1,0:T(8,128)S(1)}, f32[64,768]{1,0:T(8,128)S(1)}, u32[]{:S(2)}, u32[]{:S(2)}) collective-permute-start(f32[64,768]{1,0:T(8,128)S(1)} %bitcast_add_fusion.3), channel_id=1, source_target_pairs={{0,224},{32,0},{64,32},{96,64},{128,96},{160,128},{192,160},{224,1... | collective-permute-start | bytes 589832 | tf_op jit(solution)/shard_map/ppermute | solution.py:70
  83.4 6.8 %collective-permute-start.6 = (f32[64,768]{1,0:T(8,128)S(1)}, f32[64,768]{1,0:T(8,128)S(1)}, u32[]{:S(2)}, u32[]{:S(2)}) collective-permute-start(f32[64,768]{1,0:T(8,128)S(1)} %bitcast_add_fusion.10), channel_id=1, source_target_pairs={{0,32},{32,64},{64,96},{96,128},{128,160},{160,192},{192,224},{224... | collective-permute-start | bytes 589832 | tf_op jit(solution)/shard_map/ppermute | solution.py:67
  86.7 7.7 %collective-permute-start.14 = (f32[64,768]{1,0:T(8,128)S(1)}, f32[64,768]{1,0:T(8,128)S(1)}, u32[]{:S(2)}, u32[]{:S(2)}) collective-permute-start(f32[64,768]{1,0:T(8,128)S(1)} %bitcast_add_fusion.2), channel_id=1, source_target_pairs={{0,224},{32,0},{64,32},{96,64},{128,96},{160,128},{192,160},{224,1... | collective-permute-start | bytes 589832 | tf_op jit(solution)/shard_map/ppermute | solution.py:70
  90.2 8.1 %collective-permute-start.7 = (f32[64,768]{1,0:T(8,128)S(1)}, f32[64,768]{1,0:T(8,128)S(1)}, u32[]{:S(2)}, u32[]{:S(2)}) collective-permute-start(f32[64,768]{1,0:T(8,128)S(1)} %bitcast_add_fusion.9), channel_id=1, source_target_pairs={{0,32},{32,64},{64,96},{96,128},{128,160},{160,192},{192,224},{224... | collective-permute-start | bytes 589832 | tf_op jit(solution)/shard_map/ppermute | solution.py:67
  98.5 39.7 %copy-start.10 = (pred[64,8,4,256]{3,1,2,0:T(8,128)(4,1)S(1)}, pred[64,8,4,256]{3,1,2,0:T(8,128)(4,1)}, u32[]{:S(2)}) copy-start(pred[64,8,4,256]{3,1,2,0:T(8,128)(4,1)} %copy-done.9) | copy-start | bytes 1572868
  98.5 39.7 %copy-start.13 = (bf16[1024,512]{0,1:T(8,128)(2,1)S(1)}, bf16[1024,512]{0,1:T(8,128)(2,1)}, u32[]{:S(2)}) copy-start(bf16[1024,512]{0,1:T(8,128)(2,1)} %copy.24) | copy-start | bytes 3145732
  99.8 38.4 %all-to-all-start.1 = ((bf16[8,64,1536]{2,1,0:T(8,128)(2,1)}), bf16[8,64,1536]{2,1,0:T(8,128)(2,1)S(1)}, u32[]{:S(2)}, u32[]{:S(2)}) async-start(bf16[8,64,1536]{2,1,0:T(8,128)(2,1)} %broadcast_in_dim.14), calls=%async_computation.1 | async-start | bytes 3145728 | tf_op jit(solution)/shard_map/all_to_all | solution.py:52
  145.5 10.1 %collective-permute-start.15 = (f32[16,16,2048]{2,1,0:T(8,128)}, f32[16,16,2048]{2,1,0:T(8,128)S(1)}, u32[]{:S(2)}, u32[]{:S(2)}) collective-permute-start(f32[16,16,2048]{2,1,0:T(8,128)} %dynamic-slice_bitcast_fusion), channel_id=1, source_target_pairs={{0,1},{1,0},{2,3},{3,2},{4,5},{5,4},{6,7},{7,6},{8,9},{9,8},{10,11... | collective-permute-start | bytes 6291464 | tf_op jit(solution)/shard_map/ppermute | solution.py:92
  158.9 36.8 %all-to-all-start.2 = ((f32[16,16,2048]{2,1,0:T(8,128)}), f32[16,16,2048]{2,1,0:T(8,128)S(1)}, u32[]{:S(2)}, u32[]{:S(2)}) async-start(f32[16,16,2048]{2,1,0:T(8,128)} %bitcast_add_fusion), calls=%async_computation.2 | async-start | bytes 4194304 | tf_op jit(solution)/shard_map/all_to_all | solution.py:93
  (16 other events, 39.8 us)

commit v5 on v4

--- a/solution.py
+++ b/solution.py
@@ -71,6 +71,51 @@
             behind, (here + 1 + step) % count, 0, keepdims=False
         )
     return jnp.concatenate([carry_ahead, carry_behind], axis=1)
+
+
+def relay_scatter_sum(parts, axis_name):
+    count = lax.axis_size(axis_name)
+    here = lax.axis_index(axis_name)
+    pieces = parts.reshape((count, parts.shape[0] // count) + parts.shape[1:])
+
+    def piece_for(offset):
+        return lax.dynamic_index_in_dim(pieces, (here + offset) % count, 0, keepdims=False)
+
+    forward = [(i, (i + 1) % count) for i in range(count)]
+    backward = [(i, (i - 1) % count) for i in range(count)]
+    ahead = count // 2
+    behind = count - 1 - ahead
+    carry_ahead = piece_for(ahead)
+    carry_behind = piece_for(-behind)
+    for step in range(1, ahead + 1):
+        carry_ahead = lax.ppermute(carry_ahead, axis_name, forward)
+        if step < ahead:
+            carry_ahead = carry_ahead + piece_for(ahead - step)
+        if step <= behind:
+            carry_behind = lax.ppermute(carry_behind, axis_name, backward)
+            if step < behind:
+                carry_behind = carry_behind + piece_for(step - behind)
+    return piece_for(0) + carry_ahead + carry_behind
+
+
+def relay_gather(block, axis_name):
+    count = lax.axis_size(axis_name)
+    here = lax.axis_index(axis_name)
+    forward = [(i, (i + 1) % count) for i in range(count)]
+    backward = [(i, (i - 1) % count) for i in range(count)]
+    ahead = count // 2
+    behind = count - 1 - ahead
+    from_behind, from_ahead = [], []
+    carry_ahead, carry_behind = block, block
+    for step in range(1, ahead + 1):
+        carry_ahead = lax.ppermute(carry_ahead, axis_name, forward)
+        from_behind.append(carry_ahead)
+        if step <= behind:
+            carry_behind = lax.ppermute(carry_behind, axis_name, backward)
+            from_ahead.append(carry_behind)
+    by_offset = jnp.stack([block] + from_ahead + from_behind[::-1])
+    placed = jnp.roll(by_offset, here, axis=0)
+    return placed.reshape((count * block.shape[0],) + block.shape[1:])
 
 
 def col_gather(block):
@@ -110,7 +155,7 @@
     gate_term = apply_blocks(tokens_all, w_gate, keep_gate, "forward")
     up_term = apply_blocks(tokens_all, w_up, keep_up, "forward")
     hidden_term = apply_blocks(cotangent_all, w_down, keep_down, "transposed")
-    sums = ring_scatter_sum(jnp.concatenate([gate_term, up_term, hidden_term], axis=1), "row")
+    sums = relay_scatter_sum(jnp.concatenate([gate_term, up_term, hidden_term], axis=1), "row")
     gate = sums[:, :hidden_here]
     up = sums[:, hidden_here : 2 * hidden_here]
     hidden_grad = sums[:, 2 * hidden_here :]
@@ -121,7 +166,7 @@
         jnp.bfloat16
     )
     up_grad = (hidden_grad * activation).astype(jnp.bfloat16)
-    acts_all = a2a_gather(jnp.concatenate([hidden, gate_grad, up_grad], axis=1), "row")
+    acts_all = relay_gather(jnp.concatenate([hidden, gate_grad, up_grad], axis=1), "row")
     hidden_all = acts_all[:, :hidden_here]
     gate_grad_all = acts_all[:, hidden_here : 2 * hidden_here]
     up_grad_all = acts_all[:, 2 * hidden_here :]

time: 197 us -> 191 us (0.970)
  starting transfers between devices: 42 us -> 33.8 us
  other arithmetic: 7.87 us -> 15.8 us
  waiting for transfers between devices: 89.1 us -> 85.1 us
  local copies, waits for them, and re-layouts: 21.1 us -> 19 us
    all_to_all x1 -> x0, waiting for transfers between devices: 34.8 us -> none  [a2a_gather(): gathered = lax.all_to_all(spread, axis_name, 0, 0, tiled=True)]
    ppermute x14, waiting for transfers between devices: 26.5 us -> 57.1 us  [the longest x4 36.6 us: relay_scatter_sum(): carry_ahead = lax.ppermute(carry_ahead, axis_name, forward)]
    add x14 -> x4, other arithmetic: 0.36 us -> 6.9 us  [the longest x3 5.84 us: relay_scatter_sum(): carry_ahead = carry_ahead + piece_for(ahead - step)]
    ppermute x14, starting transfers between devices: 26.2 us -> 19.8 us  [the longest x3 9.29 us: relay_scatter_sum(): carry_behind = lax.ppermute(carry_behind, axis_name, backward)]
    all_to_all x1 -> x0, starting transfers between devices: 3.58 us -> none  [a2a_gather(): gathered = lax.all_to_all(spread, axis_name, 0, 0, tiled=True)]
    slice x1 -> x0, local copies, waits for them, and re-layouts: 2.18 us -> none  [ring_scatter_sum(): ahead, behind = (pieces[:, :, :half], pieces[:, :, half:])]
    unnamed x43 -> x54, local copies, waits for them, and re-layouts: 10.5 us -> 11.1 us
  transfers between devices with their start and end apart: 18 -> 17, of which waited for: 12 -> 11; matrix products, arithmetic and copies ran while one was open for 8% -> 9% of each run, Pallas kernels for 0% -> 0%
where the time goes in v5:
time: 191 us; the launch traced here: 190 us
  waiting for transfers between devices  85.1 us (45%)
  starting transfers between devices  33.8 us (18%)
  blocking collectives  23.4 us (12%)
  local copies, waits for them, and re-layouts  19 us (10%)
  other arithmetic  15.8 us (8%)
  matrix products  12 us (6%)
    ppermute x4, waiting for transfers between devices, relay_scatter_sum(): carry_ahead = lax.ppermute(carry_ahead, axis_name, forward)  36.6 us
    all_to_all x1, waiting for transfers between devices, col_scatter_sum(): return lax.all_to_all(pair_sum, 'chip', 0, 0, tiled=True).sum(axis=0)  24 us
    all_to_all x1, blocking collectives, col_gather(): mine = lax.all_to_all(spread, 'chip', 0, 0, tiled=True)  23.4 us
    ppermute x4, waiting for transfers between devices, relay_gather(): carry_ahead = lax.ppermute(carry_ahead, axis_name, forward)  15.1 us
    unnamed x54, local copies, waits for them, and re-layouts  11.1 us
    ppermute x3, starting transfers between devices, relay_scatter_sum(): carry_behind = lax.ppermute(carry_behind, axis_name, backward)  9.29 us
    ppermute x3, starting transfers between devices, relay_gather(): carry_behind = lax.ppermute(carry_behind, axis_name, backward)  8.81 us
    ppermute x1, starting transfers between devices, col_scatter_sum(): pair_sum = mine + lax.ppermute(other, 'core', [(0, 1), (1, 0)])  8.01 us
  transfers between devices with their start and end apart: 17, of which 11 were waited for; matrix products, arithmetic and copies ran while one was open for 9% of the time, Pallas kernels for 0%

profile of v5, /device:TPU:1, one launch (start us, length us, event | category | flops | bytes accessed | tf_op | source)
XLA Modules:
  0.0 190.3 jit_solution(17252354412196190061)
XLA Ops:
  1.6 23.4 %all_to_all.10 = bf16[16,16,2048]{2,1,0:T(8,128)(2,1)S(1)} all-to-all(bf16[16,16,2048]{2,1,0:T(8,128)(2,1)S(1)} %broadcast_in_dim.8), channel_id=1, replica_groups=mesh['row'=8,'chip'=16,'core'=2] {'chip'}, dimensions={0} | all-to-all | bytes 2097152 | tf_op jit(solution)/shard_map/all_to_all | solution.py:125
  30.3 2.5 %copy.18 = bf16[1024,512]{0,1:T(8,128)(2,1)} copy(bf16[1024,512]{1,0:T(8,128)(2,1)} %param.10) | data formatting | bytes 2097152 | tf_op args[2]
  41.8 2.4 %copy.20 = f32[512,1536]{1,0:T(8,128)S(1)} copy(f32[512,1536]{0,1:T(8,128)} %pad_maximum_fusion.1) | data formatting | bytes 6291456 | tf_op jit(solution)/shard_map/concatenate | solution.py:158
  46.7 3.9 %collective-permute-start.5 = (f32[64,1536]{1,0:T(8,128)S(1)}, f32[64,1536]{1,0:T(8,128)}, u32[]{:S(2)}, u32[]{:S(2)}) collective-permute-start(f32[64,1536]{1,0:T(8,128)S(1)} %get-tuple-element.12), channel_id=1, source_target_pairs={{0,224},{32,0},{64,32},{96,64},{128,96},{160,128},{192,160},{224,1... | collective-permute-start | bytes 1179656 | tf_op jit(solution)/shard_map/ppermute | solution.py:95
  50.6 9.8 %collective-permute-done.1 = f32[64,1536]{1,0:T(8,128)} collective-permute-done((f32[64,1536]{1,0:T(8,128)}, f32[64,1536]{1,0:T(8,128)}, u32[]{:S(2)}, u32[]{:S(2)}) %collective-permute-start.1) | collective-permute-done | bytes 393248 | tf_op jit(solution)/shard_map/ppermute | solution.py:91
  62.2 11.6 %collective-permute-done.2 = f32[64,1536]{1,0:T(8,128)} collective-permute-done((f32[64,1536]{1,0:T(8,128)}, f32[64,1536]{1,0:T(8,128)}, u32[]{:S(2)}, u32[]{:S(2)}) %collective-permute-start.2) | collective-permute-done | bytes 393248 | tf_op jit(solution)/shard_map/ppermute | solution.py:91
  75.8 2.7 %collective-permute-start.6 = (f32[64,1536]{1,0:T(8,128)S(1)}, f32[64,1536]{1,0:T(8,128)}, u32[]{:S(2)}, u32[]{:S(2)}) collective-permute-start(f32[64,1536]{1,0:T(8,128)S(1)} %get-tuple-element.10), channel_id=1, source_target_pairs={{0,224},{32,0},{64,32},{96,64},{128,96},{160,128},{192,160},{224,1... | collective-permute-start | bytes 1179656 | tf_op jit(solution)/shard_map/ppermute | solution.py:95
  78.4 8.1 %collective-permute-done.3 = f32[64,1536]{1,0:T(8,128)} collective-permute-done((f32[64,1536]{1,0:T(8,128)}, f32[64,1536]{1,0:T(8,128)}, u32[]{:S(2)}, u32[]{:S(2)}) %collective-permute-start.3) | collective-permute-done | bytes 393248 | tf_op jit(solution)/shard_map/ppermute | solution.py:91
  86.5 2.1 %bitcast_add_fusion.3 = (f32[64,1536]{1,0:T(8,128)}, f32[64,1536]{1,0:T(8,128)}) fusion(f32[64,1536]{1,0:T(8,128)} %collective-permute-done.3, f32[8,64,1536]{2,1,0:T(8,128)S(1)} %bitcast.70, s32[]{:T(128)S(6)} %select_n.101, f32[64,1536]{1,0:T(8,128)} %collective-permute-done.6, s32[]{:T(128)S(6)} %select_n.107), kind=kLoop, calls=%fused_computation.31 | loop fusion | flops 196608 | bytes 2359304 | tf_op jit(solution)/shard_map/add | solution.py:93
  88.6 2.7 %collective-permute-start.7 = (f32[64,1536]{1,0:T(8,128)}, f32[64,1536]{1,0:T(8,128)}, u32[]{:S(2)}, u32[]{:S(2)}) collective-permute-start(f32[64,1536]{1,0:T(8,128)} %get-tuple-element.8), channel_id=1, source_target_pairs={{0,224},{32,0},{64,32},{96,64},{128,96},{160,128},{192,160},{224,1... | collective-permute-start | bytes 1179656 | tf_op jit(solution)/shard_map/ppermute | solution.py:95
  91.3 7.1 %collective-permute-done.4 = f32[64,1536]{1,0:T(8,128)S(1)} collective-permute-done((f32[64,1536]{1,0:T(8,128)}, f32[64,1536]{1,0:T(8,128)S(1)}, u32[]{:S(2)}, u32[]{:S(2)}) %collective-permute-start.4) | collective-permute-done | bytes 393248 | tf_op jit(solution)/shard_map/ppermute | solution.py:91
  99.6 2.6 %collective-permute-start.8 = (bf16[64,1536]{1,0:T(8,128)(2,1)S(1)}, bf16[64,1536]{1,0:T(8,128)(2,1)S(1)}, u32[]{:S(2)}, u32[]{:S(2)}) collective-permute-start(bf16[64,1536]{1,0:T(8,128)(2,1)S(1)} %pad_maximum_fusion.2), channel_id=1, source_target_pairs={{0,224},{32,0},{64,32},{96,64},{128,96},{160,128},{192,160},{224,1... | collective-permute-start | bytes 589832 | tf_op jit(solution)/shard_map/ppermute | solution.py:114
  102.2 2.6 %collective-permute-done.8 = bf16[64,1536]{1,0:T(8,128)(2,1)S(1)} collective-permute-done((bf16[64,1536]{1,0:T(8,128)(2,1)S(1)}, bf16[64,1536]{1,0:T(8,128)(2,1)S(1)}, u32[]{:S(2)}, u32[]{:S(2)}) %collective-permute-start.8) | collective-permute-done | bytes 196640 | tf_op jit(solution)/shard_map/ppermute | solution.py:114
  104.8 3.1 %collective-permute-start.9 = (bf16[64,1536]{1,0:T(8,128)(2,1)S(1)}, bf16[64,1536]{1,0:T(8,128)(2,1)S(1)}, u32[]{:S(2)}, u32[]{:S(2)}) collective-permute-start(bf16[64,1536]{1,0:T(8,128)(2,1)S(1)} %collective-permute-done.8), channel_id=1, source_target_pairs={{0,224},{32,0},{64,32},{96,64},{128,96},{160,128},{192,160},{224,1... | collective-permute-start | bytes 589832 | tf_op jit(solution)/shard_map/ppermute | solution.py:114
  107.9 2.9 %collective-permute-done.9 = bf16[64,1536]{1,0:T(8,128)(2,1)S(1)} collective-permute-done((bf16[64,1536]{1,0:T(8,128)(2,1)S(1)}, bf16[64,1536]{1,0:T(8,128)(2,1)S(1)}, u32[]{:S(2)}, u32[]{:S(2)}) %collective-permute-start.9) | collective-permute-done | bytes 196640 | tf_op jit(solution)/shard_map/ppermute | solution.py:114
  110.8 3.1 %collective-permute-start.10 = (bf16[64,1536]{1,0:T(8,128)(2,1)S(1)}, bf16[64,1536]{1,0:T(8,128)(2,1)S(1)}, u32[]{:S(2)}, u32[]{:S(2)}) collective-permute-start(bf16[64,1536]{1,0:T(8,128)(2,1)S(1)} %collective-permute-done.9), channel_id=1, source_target_pairs={{0,224},{32,0},{64,32},{96,64},{128,96},{160,128},{192,160},{224,1... | collective-permute-start | bytes 589832 | tf_op jit(solution)/shard_map/ppermute | solution.py:114
  114.2 7.4 %collective-permute-done.13 = bf16[64,1536]{1,0:T(8,128)(2,1)S(1)} collective-permute-done((bf16[64,1536]{1,0:T(8,128)(2,1)S(1)}, bf16[64,1536]{1,0:T(8,128)(2,1)S(1)}, u32[]{:S(2)}, u32[]{:S(2)}) %collective-permute-start.13) | collective-permute-done | bytes 196640 | tf_op jit(solution)/shard_map/ppermute | solution.py:111
  121.6 7.4 %collective-permute-done.14 = bf16[64,1536]{1,0:T(8,128)(2,1)S(1)} collective-permute-done((bf16[64,1536]{1,0:T(8,128)(2,1)S(1)}, bf16[64,1536]{1,0:T(8,128)(2,1)S(1)}, u32[]{:S(2)}, u32[]{:S(2)}) %collective-permute-start.14) | collective-permute-done | bytes 196640 | tf_op jit(solution)/shard_map/ppermute | solution.py:111
  137.6 8.0 %collective-permute-start.15 = (f32[16,16,2048]{2,1,0:T(8,128)}, f32[16,16,2048]{2,1,0:T(8,128)S(1)}, u32[]{:S(2)}, u32[]{:S(2)}) collective-permute-start(f32[16,16,2048]{2,1,0:T(8,128)} %dynamic-slice_bitcast_fusion), channel_id=1, source_target_pairs={{0,1},{1,0},{2,3},{3,2},{4,5},{5,4},{6,7},{7,6},{8,9},{9,8},{10,11... | collective-permute-start | bytes 6291464 | tf_op jit(solution)/shard_map/ppermute | solution.py:137
  145.6 4.0 %collective-permute-done.15 = f32[16,16,2048]{2,1,0:T(8,128)S(1)} collective-permute-done((f32[16,16,2048]{2,1,0:T(8,128)}, f32[16,16,2048]{2,1,0:T(8,128)S(1)}, u32[]{:S(2)}, u32[]{:S(2)}) %collective-permute-start.15) | collective-permute-done | bytes 2097184 | tf_op jit(solution)/shard_map/ppermute | solution.py:137
  149.6 3.2 %bitcast_add_fusion = f32[16,16,2048]{2,1,0:T(8,128)} fusion(f32[16,16,2048]{2,1,0:T(8,128)S(1)} %collective-permute-done.15, f32[16,2,16,2048]{3,2,1,0:T(8,128)} %bitcast.66, s32[]{:T(128)S(6)} %select_n.109), kind=kLoop, calls=%fused_computation.3 | loop fusion | flops 524288 | bytes 6291460 | tf_op jit(solution)/shard_map/add | solution.py:137
  152.8 3.9 %all-to-all-start.1 = ((f32[16,16,2048]{2,1,0:T(8,128)}), f32[16,16,2048]{2,1,0:T(8,128)S(1)}, u32[]{:S(2)}, u32[]{:S(2)}) async-start(f32[16,16,2048]{2,1,0:T(8,128)} %bitcast_add_fusion), calls=%async_computation.1 | async-start | bytes 4194304 | tf_op jit(solution)/shard_map/all_to_all | solution.py:138
  158.1 3.4 %convolution_select_fusion.1 = f32[1024,512]{1,0:T(8,128)} fusion(pred[1024,512]{1,0:T(32,128)(4,1)S(1)} %copy.22, bf16[512,2048]{1,0:T(8,128)(2,1)} %bitcast.85, bf16[512,1536]{1,0:T(8,128)(2,1)} %bitcast.79), kind=kOutput, calls=%fused_computation.6 | convolution fusion | flops 537395200 | bytes 4194304 | tf_op jit(solution)/shard_map/dot_general | solution.py:33
  165.6 24.0 %all-to-all-done.1 = f32[16,16,2048]{2,1,0:T(8,128)S(1)} async-done(((f32[16,16,2048]{2,1,0:T(8,128)}), f32[16,16,2048]{2,1,0:T(8,128)S(1)}, u32[]{:S(2)}, u32[]{:S(2)}) %all-to-all-start.1) | async-done | bytes 2097184 | tf_op jit(solution)/shard_map/all_to_all | solution.py:138
  (112 shorter events, 37.3 us)
Async XLA Ops:
  0.6 26.5 %slice-start = ((s32[2048]{0:T(1024)}), s32[1024]{0:T(1024)S(1)}, s32[]{:S(2)}) async-start(s32[2048]{0:T(1024)} %param.13), calls=%async_computation.2 | async-start | bytes 8192 | tf_op jit(solution)/shard_map/slice | solution.py:14
  0.6 26.5 %slice-start.1 = ((s32[2048]{0:T(1024)}), s32[1024]{0:T(1024)S(1)}, s32[]{:S(2)}) async-start(s32[2048]{0:T(1024)} %param.14), calls=%async_computation.3 | async-start | bytes 8192 | tf_op jit(solution)/shard_map/slice | solution.py:14
  25.0 9.5 %collective-permute-start = (bf16[16,16,2048]{2,1,0:T(8,128)(2,1)S(1)}, bf16[16,16,2048]{2,1,0:T(8,128)(2,1)}, u32[]{:S(2)}, u32[]{:S(2)}) collective-permute-start(bf16[16,16,2048]{2,1,0:T(8,128)(2,1)S(1)} %all_to_all.10), channel_id=1, source_target_pairs={{0,1},{1,0},{2,3},{3,2},{4,5},{5,4},{6,7},{7,6},{8,9},{9,8},{10,11... | collective-permute-start | bytes 3145736 | tf_op jit(solution)/shard_map/ppermute | solution.py:126
  28.0 8.4 %copy-start.1 = (pred[64,8,4,256]{3,1,2,0:T(8,128)(4,1)}, pred[64,8,4,256]{3,1,2,0:T(8,128)(4,1)S(1)}, u32[]{:S(2)}) copy-start(pred[64,8,4,256]{3,1,2,0:T(8,128)(4,1)S(1)} %copy.24) | copy-start | bytes 1572868
  28.0 4.9 %slice-start.2 = ((s32[2048]{0:T(1024)}), s32[1024]{0:T(1024)S(1)}, s32[]{:S(2)}) async-start(s32[2048]{0:T(1024)} %param.15), calls=%async_computation.4 | async-start | bytes 8192 | tf_op jit(solution)/shard_map/slice | solution.py:14
  29.7 6.7 %copy-start.3 = (bf16[1024,512]{0,1:T(8,128)(2,1)}, bf16[1024,512]{0,1:T(8,128)(2,1)S(1)}, u32[]{:S(2)}) copy-start(bf16[1024,512]{0,1:T(8,128)(2,1)S(1)} %copy.19) | copy-start | bytes 3145732
  30.3 6.8 %copy-start.9 = (pred[64,8,4,256]{3,1,2,0:T(8,128)(4,1)}, pred[64,8,4,256]{3,1,2,0:T(8,128)(4,1)S(1)}, u32[]{:S(2)}) copy-start(pred[64,8,4,256]{3,1,2,0:T(8,128)(4,1)S(1)} %copy.23) | copy-start | bytes 1572868
  45.0 15.4 %collective-permute-start.1 = (f32[64,1536]{1,0:T(8,128)}, f32[64,1536]{1,0:T(8,128)}, u32[]{:S(2)}, u32[]{:S(2)}) collective-permute-start(f32[64,1536]{1,0:T(8,128)} %get-tuple-element.11), channel_id=1, source_target_pairs={{0,32},{32,64},{64,96},{96,128},{128,160},{160,192},{192,224},{224... | collective-permute-start | bytes 1179656 | tf_op jit(solution)/shard_map/ppermute | solution.py:91
  46.7 15.5 %collective-permute-start.5 = (f32[64,1536]{1,0:T(8,128)S(1)}, f32[64,1536]{1,0:T(8,128)}, u32[]{:S(2)}, u32[]{:S(2)}) collective-permute-start(f32[64,1536]{1,0:T(8,128)S(1)} %get-tuple-element.12), channel_id=1, source_target_pairs={{0,224},{32,0},{64,32},{96,64},{128,96},{160,128},{192,160},{224,1... | collective-permute-start | bytes 1179656 | tf_op jit(solution)/shard_map/ppermute | solution.py:95
  62.2 11.6 %collective-permute-start.2 = (f32[64,1536]{1,0:T(8,128)}, f32[64,1536]{1,0:T(8,128)}, u32[]{:S(2)}, u32[]{:S(2)}) collective-permute-start(f32[64,1536]{1,0:T(8,128)} %bitcast_add_fusion.5), channel_id=1, source_target_pairs={{0,32},{32,64},{64,96},{96,128},{128,160},{160,192},{192,224},{224... | collective-permute-start | bytes 1179656 | tf_op jit(solution)/shard_map/ppermute | solution.py:91
  75.8 10.8 %collective-permute-start.3 = (f32[64,1536]{1,0:T(8,128)}, f32[64,1536]{1,0:T(8,128)}, u32[]{:S(2)}, u32[]{:S(2)}) collective-permute-start(f32[64,1536]{1,0:T(8,128)} %get-tuple-element.9), channel_id=1, source_target_pairs={{0,32},{32,64},{64,96},{96,128},{128,160},{160,192},{192,224},{224... | collective-permute-start | bytes 1179656 | tf_op jit(solution)/shard_map/ppermute | solution.py:91
  75.8 10.8 %collective-permute-start.6 = (f32[64,1536]{1,0:T(8,128)S(1)}, f32[64,1536]{1,0:T(8,128)}, u32[]{:S(2)}, u32[]{:S(2)}) collective-permute-start(f32[64,1536]{1,0:T(8,128)S(1)} %get-tuple-element.10), channel_id=1, source_target_pairs={{0,224},{32,0},{64,32},{96,64},{128,96},{160,128},{192,160},{224,1... | collective-permute-start | bytes 1179656 | tf_op jit(solution)/shard_map/ppermute | solution.py:95
  88.6 9.8 %collective-permute-start.4 = (f32[64,1536]{1,0:T(8,128)}, f32[64,1536]{1,0:T(8,128)S(1)}, u32[]{:S(2)}, u32[]{:S(2)}) collective-permute-start(f32[64,1536]{1,0:T(8,128)} %get-tuple-element.7), channel_id=1, source_target_pairs={{0,32},{32,64},{64,96},{96,128},{128,160},{160,192},{192,224},{224... | collective-permute-start | bytes 1179656 | tf_op jit(solution)/shard_map/ppermute | solution.py:91
  88.6 9.8 %collective-permute-start.7 = (f32[64,1536]{1,0:T(8,128)}, f32[64,1536]{1,0:T(8,128)}, u32[]{:S(2)}, u32[]{:S(2)}) collective-permute-start(f32[64,1536]{1,0:T(8,128)} %get-tuple-element.8), channel_id=1, source_target_pairs={{0,224},{32,0},{64,32},{96,64},{128,96},{160,128},{192,160},{224,1... | collective-permute-start | bytes 1179656 | tf_op jit(solution)/shard_map/ppermute | solution.py:95
  99.6 5.2 %collective-permute-start.8 = (bf16[64,1536]{1,0:T(8,128)(2,1)S(1)}, bf16[64,1536]{1,0:T(8,128)(2,1)S(1)}, u32[]{:S(2)}, u32[]{:S(2)}) collective-permute-start(bf16[64,1536]{1,0:T(8,128)(2,1)S(1)} %pad_maximum_fusion.2), channel_id=1, source_target_pairs={{0,224},{32,0},{64,32},{96,64},{128,96},{160,128},{192,160},{224,1... | collective-permute-start | bytes 589832 | tf_op jit(solution)/shard_map/ppermute | solution.py:114
  102.2 5.7 %collective-permute-start.11 = (bf16[64,1536]{1,0:T(8,128)(2,1)S(1)}, bf16[64,1536]{1,0:T(8,128)(2,1)S(1)}, u32[]{:S(2)}, u32[]{:S(2)}) collective-permute-start(bf16[64,1536]{1,0:T(8,128)(2,1)S(1)} %pad_maximum_fusion.2), channel_id=1, source_target_pairs={{0,32},{32,64},{64,96},{96,128},{128,160},{160,192},{192,224},{224... | collective-permute-start | bytes 589832 | tf_op jit(solution)/shard_map/ppermute | solution.py:111
  104.8 6.0 %collective-permute-start.9 = (bf16[64,1536]{1,0:T(8,128)(2,1)S(1)}, bf16[64,1536]{1,0:T(8,128)(2,1)S(1)}, u32[]{:S(2)}, u32[]{:S(2)}) collective-permute-start(bf16[64,1536]{1,0:T(8,128)(2,1)S(1)} %collective-permute-done.8), channel_id=1, source_target_pairs={{0,224},{32,0},{64,32},{96,64},{128,96},{160,128},{192,160},{224,1... | collective-permute-start | bytes 589832 | tf_op jit(solution)/shard_map/ppermute | solution.py:114
  107.9 6.3 %collective-permute-start.12 = (bf16[64,1536]{1,0:T(8,128)(2,1)S(1)}, bf16[64,1536]{1,0:T(8,128)(2,1)S(1)}, u32[]{:S(2)}, u32[]{:S(2)}) collective-permute-start(bf16[64,1536]{1,0:T(8,128)(2,1)S(1)} %collective-permute-done.11), channel_id=1, source_target_pairs={{0,32},{32,64},{64,96},{96,128},{128,160},{160,192},{192,224},{224... | collective-permute-start | bytes 589832 | tf_op jit(solution)/shard_map/ppermute | solution.py:111
  110.8 10.8 %collective-permute-start.10 = (bf16[64,1536]{1,0:T(8,128)(2,1)S(1)}, bf16[64,1536]{1,0:T(8,128)(2,1)S(1)}, u32[]{:S(2)}, u32[]{:S(2)}) collective-permute-start(bf16[64,1536]{1,0:T(8,128)(2,1)S(1)} %collective-permute-done.9), channel_id=1, source_target_pairs={{0,224},{32,0},{64,32},{96,64},{128,96},{160,128},{192,160},{224,1... | collective-permute-start | bytes 589832 | tf_op jit(solution)/shard_map/ppermute | solution.py:114
  114.2 7.4 %collective-permute-start.13 = (bf16[64,1536]{1,0:T(8,128)(2,1)S(1)}, bf16[64,1536]{1,0:T(8,128)(2,1)S(1)}, u32[]{:S(2)}, u32[]{:S(2)}) collective-permute-start(bf16[64,1536]{1,0:T(8,128)(2,1)S(1)} %collective-permute-done.12), channel_id=1, source_target_pairs={{0,32},{32,64},{64,96},{96,128},{128,160},{160,192},{192,224},{224... | collective-permute-start | bytes 589832 | tf_op jit(solution)/shard_map/ppermute | solution.py:111
  121.6 7.4 %collective-permute-start.14 = (bf16[64,1536]{1,0:T(8,128)(2,1)S(1)}, bf16[64,1536]{1,0:T(8,128)(2,1)S(1)}, u32[]{:S(2)}, u32[]{:S(2)}) collective-permute-start(bf16[64,1536]{1,0:T(8,128)(2,1)S(1)} %collective-permute-done.13), channel_id=1, source_target_pairs={{0,32},{32,64},{64,96},{96,128},{128,160},{160,192},{192,224},{224... | collective-permute-start | bytes 589832 | tf_op jit(solution)/shard_map/ppermute | solution.py:111
  137.6 12.0 %collective-permute-start.15 = (f32[16,16,2048]{2,1,0:T(8,128)}, f32[16,16,2048]{2,1,0:T(8,128)S(1)}, u32[]{:S(2)}, u32[]{:S(2)}) collective-permute-start(f32[16,16,2048]{2,1,0:T(8,128)} %dynamic-slice_bitcast_fusion), channel_id=1, source_target_pairs={{0,1},{1,0},{2,3},{3,2},{4,5},{5,4},{6,7},{7,6},{8,9},{9,8},{10,11... | collective-permute-start | bytes 6291464 | tf_op jit(solution)/shard_map/ppermute | solution.py:137
  152.8 36.7 %all-to-all-start.1 = ((f32[16,16,2048]{2,1,0:T(8,128)}), f32[16,16,2048]{2,1,0:T(8,128)S(1)}, u32[]{:S(2)}, u32[]{:S(2)}) async-start(f32[16,16,2048]{2,1,0:T(8,128)} %bitcast_add_fusion), calls=%async_computation.1 | async-start | bytes 4194304 | tf_op jit(solution)/shard_map/all_to_all | solution.py:138
  156.8 4.7 %copy-start.6 = (bf16[8,64,1536]{2,1,0:T(8,128)(2,1)S(1)}, bf16[8,64,1536]{2,1,0:T(8,128)(2,1)}, u32[]{:S(2)}) copy-start(bf16[8,64,1536]{2,1,0:T(8,128)(2,1)} %copy-done.5) | copy-start | bytes 4718596
  (14 other events, 29.8 us)

commit v6 on v5

--- a/solution.py
+++ b/solution.py
@@ -77,25 +77,31 @@
     count = lax.axis_size(axis_name)
     here = lax.axis_index(axis_name)
     pieces = parts.reshape((count, parts.shape[0] // count) + parts.shape[1:])
-
-    def piece_for(offset):
-        return lax.dynamic_index_in_dim(pieces, (here + offset) % count, 0, keepdims=False)
+    half = parts.shape[1] // 2
+    spans = (slice(0, half), slice(half, parts.shape[1]))
+
+    def piece_for(offset, span):
+        return lax.dynamic_index_in_dim(pieces, (here + offset) % count, 0, keepdims=False)[:, span]
 
     forward = [(i, (i + 1) % count) for i in range(count)]
     backward = [(i, (i - 1) % count) for i in range(count)]
-    ahead = count // 2
-    behind = count - 1 - ahead
-    carry_ahead = piece_for(ahead)
-    carry_behind = piece_for(-behind)
-    for step in range(1, ahead + 1):
-        carry_ahead = lax.ppermute(carry_ahead, axis_name, forward)
-        if step < ahead:
-            carry_ahead = carry_ahead + piece_for(ahead - step)
-        if step <= behind:
-            carry_behind = lax.ppermute(carry_behind, axis_name, backward)
-            if step < behind:
-                carry_behind = carry_behind + piece_for(step - behind)
-    return piece_for(0) + carry_ahead + carry_behind
+    longer = count // 2
+    shorter = count - 1 - longer
+    reach = ((longer, shorter), (shorter, longer))
+    ahead = [piece_for(r[0], span) for r, span in zip(reach, spans)]
+    behind = [piece_for(-r[1], span) for r, span in zip(reach, spans)]
+    for step in range(1, longer + 1):
+        going = [c for c, r in enumerate(reach) if step <= r[0]]
+        coming = [c for c, r in enumerate(reach) if step <= r[1]]
+        sent_ahead = lax.ppermute(tuple(ahead[c] for c in going), axis_name, forward)
+        sent_behind = lax.ppermute(tuple(behind[c] for c in coming), axis_name, backward)
+        for c, value in zip(going, sent_ahead):
+            ahead[c] = value + piece_for(reach[c][0] - step, spans[c]) if step < reach[c][0] else value
+        for c, value in zip(coming, sent_behind):
+            behind[c] = value + piece_for(step - reach[c][1], spans[c]) if step < reach[c][1] else value
+    return jnp.concatenate(
+        [piece_for(0, span) + ahead[c] + behind[c] for c, span in enumerate(spans)], axis=1
+    )
 
 
 def relay_gather(block, axis_name):

time: 191 us -> 180 us (0.942)
  waiting for transfers between devices: 85.1 us -> 72.3 us
  starting transfers between devices: 33.8 us -> 41.3 us
  other arithmetic: 15.8 us -> 9.37 us
    ppermute x7 -> x14, waiting for transfers between devices: 36.6 us -> 23.8 us  [the longest x7 23.7 us: relay_scatter_sum(): lax.ppermute(tuple((ahead[c] for c in going)), axis_name, forward)]
    ppermute x7 -> x14, starting transfers between devices: 10.9 us -> 18.7 us  [the longest x7 16.3 us: relay_scatter_sum(): lax.ppermute(tuple((behind[c] for c in coming)), axis_name, backward)]
    add x4 -> x6, other arithmetic: 6.9 us -> 0.31 us  [the longest x3 0.14 us: relay_scatter_sum(): value + piece_for(reach[c][0] - step, spans[c])]
  transfers between devices with their start and end apart: 17 -> 24, of which waited for: 11 -> 15; matrix products, arithmetic and copies ran while one was open for 9% -> 9% of each run, Pallas kernels for 0% -> 0%
where the time goes in v6:
time: 180 us; the launch traced here: 179 us
  waiting for transfers between devices  72.3 us (40%)
  starting transfers between devices  41.3 us (23%)
  blocking collectives  23.4 us (13%)
  local copies, waits for them, and re-layouts  19.5 us (11%)
  matrix products  12 us (7%)
  other arithmetic  9.37 us (5%)
    all_to_all x1, waiting for transfers between devices, col_scatter_sum(): return lax.all_to_all(pair_sum, 'chip', 0, 0, tiled=True).sum(axis=0)  24 us
    ppermute x7, waiting for transfers between devices, relay_scatter_sum(): lax.ppermute(tuple((ahead[c] for c in going)), axis_name, forward)  23.7 us
    all_to_all x1, blocking collectives, col_gather(): mine = lax.all_to_all(spread, 'chip', 0, 0, tiled=True)  23.4 us
    ppermute x7, starting transfers between devices, relay_scatter_sum(): lax.ppermute(tuple((behind[c] for c in coming)), axis_name, backward)  16.3 us
    ppermute x4, waiting for transfers between devices, relay_gather(): carry_ahead = lax.ppermute(carry_ahead, axis_name, forward)  15.1 us
    unnamed x54, local copies, waits for them, and re-layouts  11.9 us
    ppermute x3, starting transfers between devices, relay_gather(): carry_behind = lax.ppermute(carry_behind, axis_name, backward)  8.81 us
    ppermute x1, starting transfers between devices, col_scatter_sum(): pair_sum = mine + lax.ppermute(other, 'core', [(0, 1), (1, 0)])  8 us
  transfers between devices with their start and end apart: 24, of which 15 were waited for; matrix products, arithmetic and copies ran while one was open for 9% of the time, Pallas kernels for 0%

profile of v6, /device:TPU:1, one launch (start us, length us, event | category | flops | bytes accessed | tf_op | source)
XLA Modules:
  0.0 179.2 jit_solution(2931934746724993014)
XLA Ops:
  1.6 23.4 %all_to_all.10 = bf16[16,16,2048]{2,1,0:T(8,128)(2,1)S(1)} all-to-all(bf16[16,16,2048]{2,1,0:T(8,128)(2,1)S(1)} %broadcast_in_dim.8), channel_id=1, replica_groups=mesh['row'=8,'chip'=16,'core'=2] {'chip'}, dimensions={0} | all-to-all | bytes 2097152 | tf_op jit(solution)/shard_map/all_to_all | solution.py:131
  30.3 2.5 %copy.18 = bf16[1024,512]{0,1:T(8,128)(2,1)} copy(bf16[1024,512]{1,0:T(8,128)(2,1)} %param.10) | data formatting | bytes 2097152 | tf_op args[2]
  46.9 4.0 %collective-permute-start.11 = (f32[64,768]{1,0:T(8,128)S(1)}, f32[64,768]{1,0:T(8,128)S(1)}, u32[]{:S(2)}, u32[]{:S(2)}) collective-permute-start(f32[64,768]{1,0:T(8,128)S(1)} %slice.133), channel_id=1, source_target_pairs={{0,224},{32,0},{64,32},{96,64},{128,96},{160,128},{192,160},{224,1... | collective-permute-start | bytes 589832 | tf_op jit(solution)/shard_map/ppermute | solution.py:97
  50.9 5.2 %collective-permute-done.1 = f32[64,768]{1,0:T(8,128)S(1)} collective-permute-done((f32[64,768]{1,0:T(8,128)S(1)}, f32[64,768]{1,0:T(8,128)S(1)}, u32[]{:S(2)}, u32[]{:S(2)}) %collective-permute-start.1) | collective-permute-done | bytes 196640 | tf_op jit(solution)/shard_map/ppermute | solution.py:96
  56.4 2.7 %collective-permute-start.12 = (f32[64,768]{1,0:T(8,128)S(1)}, f32[64,768]{1,0:T(8,128)S(1)}, u32[]{:S(2)}, u32[]{:S(2)}) collective-permute-start(f32[64,768]{1,0:T(8,128)S(1)} %get-tuple-element.32), channel_id=1, source_target_pairs={{0,224},{32,0},{64,32},{96,64},{128,96},{160,128},{192,160},{224,1... | collective-permute-start | bytes 589832 | tf_op jit(solution)/shard_map/ppermute | solution.py:97
  60.5 2.8 %collective-permute-done.2 = f32[64,768]{1,0:T(8,128)S(1)} collective-permute-done((f32[64,768]{1,0:T(8,128)S(1)}, f32[64,768]{1,0:T(8,128)S(1)}, u32[]{:S(2)}, u32[]{:S(2)}) %collective-permute-start.2) | collective-permute-done | bytes 196640 | tf_op jit(solution)/shard_map/ppermute | solution.py:96
  63.3 4.2 %collective-permute-done.8 = f32[64,768]{1,0:T(8,128)S(1)} collective-permute-done((f32[64,768]{1,0:T(8,128)S(1)}, f32[64,768]{1,0:T(8,128)S(1)}, u32[]{:S(2)}, u32[]{:S(2)}) %collective-permute-start.8) | collective-permute-done | bytes 196640 | tf_op jit(solution)/shard_map/ppermute | solution.py:96
  68.0 2.7 %collective-permute-start.13 = (f32[64,768]{1,0:T(8,128)S(1)}, f32[64,768]{1,0:T(8,128)S(1)}, u32[]{:S(2)}, u32[]{:S(2)}) collective-permute-start(f32[64,768]{1,0:T(8,128)S(1)} %get-tuple-element.30), channel_id=1, source_target_pairs={{0,224},{32,0},{64,32},{96,64},{128,96},{160,128},{192,160},{224,1... | collective-permute-start | bytes 589832 | tf_op jit(solution)/shard_map/ppermute | solution.py:97
  74.0 4.2 %collective-permute-done.9 = f32[64,768]{1,0:T(8,128)S(1)} collective-permute-done((f32[64,768]{1,0:T(8,128)S(1)}, f32[64,768]{1,0:T(8,128)S(1)}, u32[]{:S(2)}, u32[]{:S(2)}) %collective-permute-start.9) | collective-permute-done | bytes 196640 | tf_op jit(solution)/shard_map/ppermute | solution.py:96
  78.6 2.7 %collective-permute-start.14 = (f32[64,768]{1,0:T(8,128)S(1)}, f32[64,768]{1,0:T(8,128)S(1)}, u32[]{:S(2)}, u32[]{:S(2)}) collective-permute-start(f32[64,768]{1,0:T(8,128)S(1)} %get-tuple-element.28), channel_id=1, source_target_pairs={{0,224},{32,0},{64,32},{96,64},{128,96},{160,128},{192,160},{224,1... | collective-permute-start | bytes 589832 | tf_op jit(solution)/shard_map/ppermute | solution.py:97
  84.1 3.9 %collective-permute-done.4 = f32[64,768]{1,0:T(8,128)S(1)} collective-permute-done((f32[64,768]{1,0:T(8,128)S(1)}, f32[64,768]{1,0:T(8,128)S(1)}, u32[]{:S(2)}, u32[]{:S(2)}) %collective-permute-start.4) | collective-permute-done | bytes 196640 | tf_op jit(solution)/shard_map/ppermute | solution.py:96
  88.3 2.6 %collective-permute-start.15 = (bf16[64,1536]{1,0:T(8,128)(2,1)S(1)}, bf16[64,1536]{1,0:T(8,128)(2,1)S(1)}, u32[]{:S(2)}, u32[]{:S(2)}) collective-permute-start(bf16[64,1536]{1,0:T(8,128)(2,1)S(1)} %pad_maximum_fusion.2), channel_id=1, source_target_pairs={{0,224},{32,0},{64,32},{96,64},{128,96},{160,128},{192,160},{224,1... | collective-permute-start | bytes 589832 | tf_op jit(solution)/shard_map/ppermute | solution.py:120
  90.9 2.6 %collective-permute-done.15 = bf16[64,1536]{1,0:T(8,128)(2,1)S(1)} collective-permute-done((bf16[64,1536]{1,0:T(8,128)(2,1)S(1)}, bf16[64,1536]{1,0:T(8,128)(2,1)S(1)}, u32[]{:S(2)}, u32[]{:S(2)}) %collective-permute-start.15) | collective-permute-done | bytes 196640 | tf_op jit(solution)/shard_map/ppermute | solution.py:120
  93.5 3.1 %collective-permute-start.16 = (bf16[64,1536]{1,0:T(8,128)(2,1)S(1)}, bf16[64,1536]{1,0:T(8,128)(2,1)S(1)}, u32[]{:S(2)}, u32[]{:S(2)}) collective-permute-start(bf16[64,1536]{1,0:T(8,128)(2,1)S(1)} %collective-permute-done.15), channel_id=1, source_target_pairs={{0,224},{32,0},{64,32},{96,64},{128,96},{160,128},{192,160},{224,1... | collective-permute-start | bytes 589832 | tf_op jit(solution)/shard_map/ppermute | solution.py:120
  96.6 2.9 %collective-permute-done.16 = bf16[64,1536]{1,0:T(8,128)(2,1)S(1)} collective-permute-done((bf16[64,1536]{1,0:T(8,128)(2,1)S(1)}, bf16[64,1536]{1,0:T(8,128)(2,1)S(1)}, u32[]{:S(2)}, u32[]{:S(2)}) %collective-permute-start.16) | collective-permute-done | bytes 196640 | tf_op jit(solution)/shard_map/ppermute | solution.py:120
  99.5 3.1 %collective-permute-start.17 = (bf16[64,1536]{1,0:T(8,128)(2,1)S(1)}, bf16[64,1536]{1,0:T(8,128)(2,1)S(1)}, u32[]{:S(2)}, u32[]{:S(2)}) collective-permute-start(bf16[64,1536]{1,0:T(8,128)(2,1)S(1)} %collective-permute-done.16), channel_id=1, source_target_pairs={{0,224},{32,0},{64,32},{96,64},{128,96},{160,128},{192,160},{224,1... | collective-permute-start | bytes 589832 | tf_op jit(solution)/shard_map/ppermute | solution.py:120
  102.9 7.4 %collective-permute-done.20 = bf16[64,1536]{1,0:T(8,128)(2,1)S(1)} collective-permute-done((bf16[64,1536]{1,0:T(8,128)(2,1)S(1)}, bf16[64,1536]{1,0:T(8,128)(2,1)S(1)}, u32[]{:S(2)}, u32[]{:S(2)}) %collective-permute-start.20) | collective-permute-done | bytes 196640 | tf_op jit(solution)/shard_map/ppermute | solution.py:117
  110.3 7.4 %collective-permute-done.21 = bf16[64,1536]{1,0:T(8,128)(2,1)S(1)} collective-permute-done((bf16[64,1536]{1,0:T(8,128)(2,1)S(1)}, bf16[64,1536]{1,0:T(8,128)(2,1)S(1)}, u32[]{:S(2)}, u32[]{:S(2)}) %collective-permute-start.21) | collective-permute-done | bytes 196640 | tf_op jit(solution)/shard_map/ppermute | solution.py:117
  126.5 8.0 %collective-permute-start.22 = (f32[16,16,2048]{2,1,0:T(8,128)}, f32[16,16,2048]{2,1,0:T(8,128)S(1)}, u32[]{:S(2)}, u32[]{:S(2)}) collective-permute-start(f32[16,16,2048]{2,1,0:T(8,128)} %dynamic-slice_bitcast_fusion), channel_id=1, source_target_pairs={{0,1},{1,0},{2,3},{3,2},{4,5},{5,4},{6,7},{7,6},{8,9},{9,8},{10,11... | collective-permute-start | bytes 6291464 | tf_op jit(solution)/shard_map/ppermute | solution.py:143
  134.5 4.0 %collective-permute-done.22 = f32[16,16,2048]{2,1,0:T(8,128)S(1)} collective-permute-done((f32[16,16,2048]{2,1,0:T(8,128)}, f32[16,16,2048]{2,1,0:T(8,128)S(1)}, u32[]{:S(2)}, u32[]{:S(2)}) %collective-permute-start.22) | collective-permute-done | bytes 2097184 | tf_op jit(solution)/shard_map/ppermute | solution.py:143
  138.5 3.2 %bitcast_add_fusion = f32[16,16,2048]{2,1,0:T(8,128)} fusion(f32[16,16,2048]{2,1,0:T(8,128)S(1)} %collective-permute-done.22, f32[16,2,16,2048]{3,2,1,0:T(8,128)} %bitcast.66, s32[]{:T(128)S(6)} %select_n.139), kind=kLoop, calls=%fused_computation.3 | loop fusion | flops 524288 | bytes 6291460 | tf_op jit(solution)/shard_map/add | solution.py:143
  141.7 3.7 %all-to-all-start.1 = ((f32[16,16,2048]{2,1,0:T(8,128)}), f32[16,16,2048]{2,1,0:T(8,128)S(1)}, u32[]{:S(2)}, u32[]{:S(2)}) async-start(f32[16,16,2048]{2,1,0:T(8,128)} %bitcast_add_fusion), calls=%async_computation.1 | async-start | bytes 4194304 | tf_op jit(solution)/shard_map/all_to_all | solution.py:144
  146.9 3.4 %convolution_select_fusion.1 = f32[1024,512]{1,0:T(8,128)} fusion(pred[1024,512]{1,0:T(32,128)(4,1)S(1)} %copy.22, bf16[512,2048]{1,0:T(8,128)(2,1)} %bitcast.81, bf16[512,1536]{1,0:T(8,128)(2,1)S(1)} %bitcast.75), kind=kOutput, calls=%fused_computation.6 | convolution fusion | flops 537395200 | bytes 4194304 | tf_op jit(solution)/shard_map/dot_general | solution.py:33
  154.4 24.0 %all-to-all-done.1 = f32[16,16,2048]{2,1,0:T(8,128)S(1)} async-done(((f32[16,16,2048]{2,1,0:T(8,128)}), f32[16,16,2048]{2,1,0:T(8,128)S(1)}, u32[]{:S(2)}, u32[]{:S(2)}) %all-to-all-start.1) | async-done | bytes 2097184 | tf_op jit(solution)/shard_map/all_to_all | solution.py:144
  (131 shorter events, 44.2 us)
Async XLA Ops:
  25.0 9.5 %collective-permute-start = (bf16[16,16,2048]{2,1,0:T(8,128)(2,1)S(1)}, bf16[16,16,2048]{2,1,0:T(8,128)(2,1)}, u32[]{:S(2)}, u32[]{:S(2)}) collective-permute-start(bf16[16,16,2048]{2,1,0:T(8,128)(2,1)S(1)} %all_to_all.10), channel_id=1, source_target_pairs={{0,1},{1,0},{2,3},{3,2},{4,5},{5,4},{6,7},{7,6},{8,9},{9,8},{10,11... | collective-permute-start | bytes 3145736 | tf_op jit(solution)/shard_map/ppermute | solution.py:132
  45.1 10.9 %collective-permute-start.1 = (f32[64,768]{1,0:T(8,128)S(1)}, f32[64,768]{1,0:T(8,128)S(1)}, u32[]{:S(2)}, u32[]{:S(2)}) collective-permute-start(f32[64,768]{1,0:T(8,128)S(1)} %slice.121), channel_id=1, source_target_pairs={{0,32},{32,64},{64,96},{96,128},{128,160},{160,192},{192,224},{224... | collective-permute-start | bytes 589832 | tf_op jit(solution)/shard_map/ppermute | solution.py:96
  46.9 9.4 %collective-permute-start.11 = (f32[64,768]{1,0:T(8,128)S(1)}, f32[64,768]{1,0:T(8,128)S(1)}, u32[]{:S(2)}, u32[]{:S(2)}) collective-permute-start(f32[64,768]{1,0:T(8,128)S(1)} %slice.133), channel_id=1, source_target_pairs={{0,224},{32,0},{64,32},{96,64},{128,96},{160,128},{192,160},{224,1... | collective-permute-start | bytes 589832 | tf_op jit(solution)/shard_map/ppermute | solution.py:97
  56.1 7.2 %collective-permute-start.2 = (f32[64,768]{1,0:T(8,128)S(1)}, f32[64,768]{1,0:T(8,128)S(1)}, u32[]{:S(2)}, u32[]{:S(2)}) collective-permute-start(f32[64,768]{1,0:T(8,128)S(1)} %get-tuple-element.25), channel_id=1, source_target_pairs={{0,32},{32,64},{64,96},{96,128},{128,160},{160,192},{192,224},{224... | collective-permute-start | bytes 589832 | tf_op jit(solution)/shard_map/ppermute | solution.py:96
  56.2 11.3 %collective-permute-start.8 = (f32[64,768]{1,0:T(8,128)S(1)}, f32[64,768]{1,0:T(8,128)S(1)}, u32[]{:S(2)}, u32[]{:S(2)}) collective-permute-start(f32[64,768]{1,0:T(8,128)S(1)} %get-tuple-element.26), channel_id=1, source_target_pairs={{0,32},{32,64},{64,96},{96,128},{128,160},{160,192},{192,224},{224... | collective-permute-start | bytes 589832 | tf_op jit(solution)/shard_map/ppermute | solution.py:96
  56.4 11.6 %collective-permute-start.12 = (f32[64,768]{1,0:T(8,128)S(1)}, f32[64,768]{1,0:T(8,128)S(1)}, u32[]{:S(2)}, u32[]{:S(2)}) collective-permute-start(f32[64,768]{1,0:T(8,128)S(1)} %get-tuple-element.32), channel_id=1, source_target_pairs={{0,224},{32,0},{64,32},{96,64},{128,96},{160,128},{192,160},{224,1... | collective-permute-start | bytes 589832 | tf_op jit(solution)/shard_map/ppermute | solution.py:97
  59.1 8.8 %collective-permute-start.5 = (f32[64,768]{1,0:T(8,128)S(1)}, f32[64,768]{1,0:T(8,128)S(1)}, u32[]{:S(2)}, u32[]{:S(2)}) collective-permute-start(f32[64,768]{1,0:T(8,128)S(1)} %get-tuple-element.31), channel_id=1, source_target_pairs={{0,224},{32,0},{64,32},{96,64},{128,96},{160,128},{192,160},{224,1... | collective-permute-start | bytes 589832 | tf_op jit(solution)/shard_map/ppermute | solution.py:97
  67.6 6.5 %collective-permute-start.3 = (f32[64,768]{1,0:T(8,128)S(1)}, f32[64,768]{1,0:T(8,128)S(1)}, u32[]{:S(2)}, u32[]{:S(2)}) collective-permute-start(f32[64,768]{1,0:T(8,128)S(1)} %get-tuple-element.23), channel_id=1, source_target_pairs={{0,32},{32,64},{64,96},{96,128},{128,160},{160,192},{192,224},{224... | collective-permute-start | bytes 589832 | tf_op jit(solution)/shard_map/ppermute | solution.py:96
  67.8 10.4 %collective-permute-start.9 = (f32[64,768]{1,0:T(8,128)S(1)}, f32[64,768]{1,0:T(8,128)S(1)}, u32[]{:S(2)}, u32[]{:S(2)}) collective-permute-start(f32[64,768]{1,0:T(8,128)S(1)} %get-tuple-element.24), channel_id=1, source_target_pairs={{0,32},{32,64},{64,96},{96,128},{128,160},{160,192},{192,224},{224... | collective-permute-start | bytes 589832 | tf_op jit(solution)/shard_map/ppermute | solution.py:96
  68.0 10.5 %collective-permute-start.13 = (f32[64,768]{1,0:T(8,128)S(1)}, f32[64,768]{1,0:T(8,128)S(1)}, u32[]{:S(2)}, u32[]{:S(2)}) collective-permute-start(f32[64,768]{1,0:T(8,128)S(1)} %get-tuple-element.30), channel_id=1, source_target_pairs={{0,224},{32,0},{64,32},{96,64},{128,96},{160,128},{192,160},{224,1... | collective-permute-start | bytes 589832 | tf_op jit(solution)/shard_map/ppermute | solution.py:97
  70.7 7.8 %collective-permute-start.6 = (f32[64,768]{1,0:T(8,128)S(1)}, f32[64,768]{1,0:T(8,128)S(1)}, u32[]{:S(2)}, u32[]{:S(2)}) collective-permute-start(f32[64,768]{1,0:T(8,128)S(1)} %get-tuple-element.29), channel_id=1, source_target_pairs={{0,224},{32,0},{64,32},{96,64},{128,96},{160,128},{192,160},{224,1... | collective-permute-start | bytes 589832 | tf_op jit(solution)/shard_map/ppermute | solution.py:97
  78.3 5.8 %collective-permute-start.10 = (f32[64,768]{1,0:T(8,128)S(1)}, f32[64,768]{1,0:T(8,128)S(1)}, u32[]{:S(2)}, u32[]{:S(2)}) collective-permute-start(f32[64,768]{1,0:T(8,128)S(1)} %get-tuple-element.22), channel_id=1, source_target_pairs={{0,32},{32,64},{64,96},{96,128},{128,160},{160,192},{192,224},{224... | collective-permute-start | bytes 589832 | tf_op jit(solution)/shard_map/ppermute | solution.py:96
  78.4 9.6 %collective-permute-start.4 = (f32[64,768]{1,0:T(8,128)S(1)}, f32[64,768]{1,0:T(8,128)S(1)}, u32[]{:S(2)}, u32[]{:S(2)}) collective-permute-start(f32[64,768]{1,0:T(8,128)S(1)} %get-tuple-element.21), channel_id=1, source_target_pairs={{0,32},{32,64},{64,96},{96,128},{128,160},{160,192},{192,224},{224... | collective-permute-start | bytes 589832 | tf_op jit(solution)/shard_map/ppermute | solution.py:96
  78.6 9.4 %collective-permute-start.14 = (f32[64,768]{1,0:T(8,128)S(1)}, f32[64,768]{1,0:T(8,128)S(1)}, u32[]{:S(2)}, u32[]{:S(2)}) collective-permute-start(f32[64,768]{1,0:T(8,128)S(1)} %get-tuple-element.28), channel_id=1, source_target_pairs={{0,224},{32,0},{64,32},{96,64},{128,96},{160,128},{192,160},{224,1... | collective-permute-start | bytes 589832 | tf_op jit(solution)/shard_map/ppermute | solution.py:97
  81.3 6.8 %collective-permute-start.7 = (f32[64,768]{1,0:T(8,128)S(1)}, f32[64,768]{1,0:T(8,128)S(1)}, u32[]{:S(2)}, u32[]{:S(2)}) collective-permute-start(f32[64,768]{1,0:T(8,128)S(1)} %get-tuple-element.27), channel_id=1, source_target_pairs={{0,224},{32,0},{64,32},{96,64},{128,96},{160,128},{192,160},{224,1... | collective-permute-start | bytes 589832 | tf_op jit(solution)/shard_map/ppermute | solution.py:97
  88.3 5.2 %collective-permute-start.15 = (bf16[64,1536]{1,0:T(8,128)(2,1)S(1)}, bf16[64,1536]{1,0:T(8,128)(2,1)S(1)}, u32[]{:S(2)}, u32[]{:S(2)}) collective-permute-start(bf16[64,1536]{1,0:T(8,128)(2,1)S(1)} %pad_maximum_fusion.2), channel_id=1, source_target_pairs={{0,224},{32,0},{64,32},{96,64},{128,96},{160,128},{192,160},{224,1... | collective-permute-start | bytes 589832 | tf_op jit(solution)/shard_map/ppermute | solution.py:120
  90.9 5.7 %collective-permute-start.18 = (bf16[64,1536]{1,0:T(8,128)(2,1)S(1)}, bf16[64,1536]{1,0:T(8,128)(2,1)S(1)}, u32[]{:S(2)}, u32[]{:S(2)}) collective-permute-start(bf16[64,1536]{1,0:T(8,128)(2,1)S(1)} %pad_maximum_fusion.2), channel_id=1, source_target_pairs={{0,32},{32,64},{64,96},{96,128},{128,160},{160,192},{192,224},{224... | collective-permute-start | bytes 589832 | tf_op jit(solution)/shard_map/ppermute | solution.py:117
  93.5 6.0 %collective-permute-start.16 = (bf16[64,1536]{1,0:T(8,128)(2,1)S(1)}, bf16[64,1536]{1,0:T(8,128)(2,1)S(1)}, u32[]{:S(2)}, u32[]{:S(2)}) collective-permute-start(bf16[64,1536]{1,0:T(8,128)(2,1)S(1)} %collective-permute-done.15), channel_id=1, source_target_pairs={{0,224},{32,0},{64,32},{96,64},{128,96},{160,128},{192,160},{224,1... | collective-permute-start | bytes 589832 | tf_op jit(solution)/shard_map/ppermute | solution.py:120
  96.6 6.3 %collective-permute-start.19 = (bf16[64,1536]{1,0:T(8,128)(2,1)S(1)}, bf16[64,1536]{1,0:T(8,128)(2,1)S(1)}, u32[]{:S(2)}, u32[]{:S(2)}) collective-permute-start(bf16[64,1536]{1,0:T(8,128)(2,1)S(1)} %collective-permute-done.18), channel_id=1, source_target_pairs={{0,32},{32,64},{64,96},{96,128},{128,160},{160,192},{192,224},{224... | collective-permute-start | bytes 589832 | tf_op jit(solution)/shard_map/ppermute | solution.py:117
  99.5 10.8 %collective-permute-start.17 = (bf16[64,1536]{1,0:T(8,128)(2,1)S(1)}, bf16[64,1536]{1,0:T(8,128)(2,1)S(1)}, u32[]{:S(2)}, u32[]{:S(2)}) collective-permute-start(bf16[64,1536]{1,0:T(8,128)(2,1)S(1)} %collective-permute-done.16), channel_id=1, source_target_pairs={{0,224},{32,0},{64,32},{96,64},{128,96},{160,128},{192,160},{224,1... | collective-permute-start | bytes 589832 | tf_op jit(solution)/shard_map/ppermute | solution.py:120
  102.9 7.4 %collective-permute-start.20 = (bf16[64,1536]{1,0:T(8,128)(2,1)S(1)}, bf16[64,1536]{1,0:T(8,128)(2,1)S(1)}, u32[]{:S(2)}, u32[]{:S(2)}) collective-permute-start(bf16[64,1536]{1,0:T(8,128)(2,1)S(1)} %collective-permute-done.19), channel_id=1, source_target_pairs={{0,32},{32,64},{64,96},{96,128},{128,160},{160,192},{192,224},{224... | collective-permute-start | bytes 589832 | tf_op jit(solution)/shard_map/ppermute | solution.py:117
  110.3 7.4 %collective-permute-start.21 = (bf16[64,1536]{1,0:T(8,128)(2,1)S(1)}, bf16[64,1536]{1,0:T(8,128)(2,1)S(1)}, u32[]{:S(2)}, u32[]{:S(2)}) collective-permute-start(bf16[64,1536]{1,0:T(8,128)(2,1)S(1)} %collective-permute-done.20), channel_id=1, source_target_pairs={{0,32},{32,64},{64,96},{96,128},{128,160},{160,192},{192,224},{224... | collective-permute-start | bytes 589832 | tf_op jit(solution)/shard_map/ppermute | solution.py:117
  126.5 12.0 %collective-permute-start.22 = (f32[16,16,2048]{2,1,0:T(8,128)}, f32[16,16,2048]{2,1,0:T(8,128)S(1)}, u32[]{:S(2)}, u32[]{:S(2)}) collective-permute-start(f32[16,16,2048]{2,1,0:T(8,128)} %dynamic-slice_bitcast_fusion), channel_id=1, source_target_pairs={{0,1},{1,0},{2,3},{3,2},{4,5},{5,4},{6,7},{7,6},{8,9},{9,8},{10,11... | collective-permute-start | bytes 6291464 | tf_op jit(solution)/shard_map/ppermute | solution.py:143
  141.7 36.7 %all-to-all-start.1 = ((f32[16,16,2048]{2,1,0:T(8,128)}), f32[16,16,2048]{2,1,0:T(8,128)S(1)}, u32[]{:S(2)}, u32[]{:S(2)}) async-start(f32[16,16,2048]{2,1,0:T(8,128)} %bitcast_add_fusion), calls=%async_computation.1 | async-start | bytes 4194304 | tf_op jit(solution)/shard_map/all_to_all | solution.py:144
  (21 other events, 106.3 us)

commit v7 on v6

--- a/solution.py
+++ b/solution.py
@@ -73,6 +73,15 @@
     return jnp.concatenate([carry_ahead, carry_behind], axis=1)
 
 
+def joint_permute(values, axis_name, pairs):
+    if len(values) == 1:
+        return [lax.ppermute(values[0], axis_name, pairs)]
+    widths = [v.shape[1] for v in values]
+    moved = lax.ppermute(jnp.concatenate(values, axis=1), axis_name, pairs)
+    edges = [sum(widths[:k]) for k in range(len(widths) + 1)]
+    return [moved[:, edges[k] : edges[k + 1]] for k in range(len(values))]
+
+
 def relay_scatter_sum(parts, axis_name):
     count = lax.axis_size(axis_name)
     here = lax.axis_index(axis_name)
@@ -93,8 +102,8 @@
     for step in range(1, longer + 1):
         going = [c for c, r in enumerate(reach) if step <= r[0]]
         coming = [c for c, r in enumerate(reach) if step <= r[1]]
-        sent_ahead = lax.ppermute(tuple(ahead[c] for c in going), axis_name, forward)
-        sent_behind = lax.ppermute(tuple(behind[c] for c in coming), axis_name, backward)
+        sent_ahead = joint_permute([ahead[c] for c in going], axis_name, forward)
+        sent_behind = joint_permute([behind[c] for c in coming], axis_name, backward)
         for c, value in zip(going, sent_ahead):
             ahead[c] = value + piece_for(reach[c][0] - step, spans[c]) if step < reach[c][0] else value
         for c, value in zip(coming, sent_behind):
@@ -109,17 +118,28 @@
     here = lax.axis_index(axis_name)
     forward = [(i, (i + 1) % count) for i in range(count)]
     backward = [(i, (i - 1) % count) for i in range(count)]
-    ahead = count // 2
-    behind = count - 1 - ahead
+    rounds = count // 2
+    half = block.shape[1] // 2
     from_behind, from_ahead = [], []
     carry_ahead, carry_behind = block, block
-    for step in range(1, ahead + 1):
+    for step in range(1, rounds):
         carry_ahead = lax.ppermute(carry_ahead, axis_name, forward)
+        carry_behind = lax.ppermute(carry_behind, axis_name, backward)
         from_behind.append(carry_ahead)
-        if step <= behind:
-            carry_behind = lax.ppermute(carry_behind, axis_name, backward)
-            from_ahead.append(carry_behind)
-    by_offset = jnp.stack([block] + from_ahead + from_behind[::-1])
+        from_ahead.append(carry_behind)
+    if count % 2 == 0:
+        opposite = jnp.concatenate(
+            [
+                lax.ppermute(carry_ahead[:, :half], axis_name, forward),
+                lax.ppermute(carry_behind[:, half:], axis_name, backward),
+            ],
+            axis=1,
+        )
+        middle = [opposite]
+    else:
+        middle = [lax.ppermute(carry_ahead, axis_name, forward)]
+        from_ahead.append(lax.ppermute(carry_behind, axis_name, backward))
+    by_offset = jnp.stack([block] + from_ahead + middle + from_behind[::-1])
     placed = jnp.roll(by_offset, here, axis=0)
     return placed.reshape((count * block.shape[0],) + block.shape[1:])
 

time: 180 us -> 179 us (level)
  starting transfers between devices: 41.3 us -> 38.1 us
    ppermute x4 -> x3, waiting for transfers between devices: 15.1 us -> 7.66 us  [relay_gather(): carry_ahead = lax.ppermute(carry_ahead, axis_name, forward)]
    ppermute x3, starting transfers between devices: 8.81 us -> 1.94 us  [relay_gather(): carry_behind = lax.ppermute(carry_behind, axis_name, backward)]
    ppermute x14 -> x10, waiting for transfers between devices: 23.8 us -> 30.5 us  [the longest x6 22.3 us: joint_permute(): moved = lax.ppermute(jnp.concatenate(values, axis=1), axis_name, pairs)]
    ppermute x3, waiting for transfers between devices: 5.45 us -> 8.13 us  [relay_gather(): carry_behind = lax.ppermute(carry_behind, axis_name, backward)]
    ppermute x4 -> x3, starting transfers between devices: 0.01 us -> 2.58 us  [relay_gather(): carry_ahead = lax.ppermute(carry_ahead, axis_name, forward)]
    ppermute x14 -> x10, starting transfers between devices: 18.7 us -> 19.4 us  [the longest x6 12.9 us: joint_permute(): moved = lax.ppermute(jnp.concatenate(values, axis=1), axis_name, pairs)]
    unnamed x54 -> x52, local copies, waits for them, and re-layouts: 11.9 us -> 11.8 us
  transfers between devices with their start and end apart: 24 -> 19, of which waited for: 15 -> 13; matrix products, arithmetic and copies ran while one was open for 9% -> 9% of each run, Pallas kernels for 0% -> 0%
where the time goes in v7:
time: 179 us; the launch traced here: 178 us
  waiting for transfers between devices  74.1 us (41%)
  starting transfers between devices  38.1 us (21%)
  blocking collectives  23.4 us (13%)
  local copies, waits for them, and re-layouts  19.5 us (11%)
  matrix products  12 us (7%)
  other arithmetic  9.61 us (5%)
    all_to_all x1, waiting for transfers between devices, col_scatter_sum(): return lax.all_to_all(pair_sum, 'chip', 0, 0, tiled=True).sum(axis=0)  23.8 us
    all_to_all x1, blocking collectives, col_gather(): mine = lax.all_to_all(spread, 'chip', 0, 0, tiled=True)  23.4 us
    ppermute x6, waiting for transfers between devices, joint_permute(): moved = lax.ppermute(jnp.concatenate(values, axis=1), axis_name, pairs)  22.3 us
    ppermute x6, starting transfers between devices, joint_permute(): moved = lax.ppermute(jnp.concatenate(values, axis=1), axis_name, pairs)  12.9 us
    unnamed x52, local copies, waits for them, and re-layouts  11.8 us
    ppermute x1, starting transfers between devices, col_scatter_sum(): pair_sum = mine + lax.ppermute(other, 'core', [(0, 1), (1, 0)])  8.13 us
    ppermute x3, waiting for transfers between devices, relay_gather(): carry_behind = lax.ppermute(carry_behind, axis_name, backward)  8.13 us
    ppermute x3, waiting for transfers between devices, relay_gather(): carry_ahead = lax.ppermute(carry_ahead, axis_name, forward)  7.66 us
  transfers between devices with their start and end apart: 19, of which 13 were waited for; matrix products, arithmetic and copies ran while one was open for 9% of the time, Pallas kernels for 0%

profile of v7, /device:TPU:1, one launch (start us, length us, event | category | flops | bytes accessed | tf_op | source)
XLA Modules:
  0.0 177.9 jit_solution(5571634910104750493)
XLA Ops:
  1.6 23.4 %all_to_all.10 = bf16[16,16,2048]{2,1,0:T(8,128)(2,1)S(1)} all-to-all(bf16[16,16,2048]{2,1,0:T(8,128)(2,1)S(1)} %broadcast_in_dim.8), channel_id=1, replica_groups=mesh['row'=8,'chip'=16,'core'=2] {'chip'}, dimensions={0} | all-to-all | bytes 2097152 | tf_op jit(solution)/shard_map/all_to_all | solution.py:151
  25.0 2.1 %collective-permute-start = (bf16[16,16,2048]{2,1,0:T(8,128)(2,1)S(1)}, bf16[16,16,2048]{2,1,0:T(8,128)(2,1)}, u32[]{:S(2)}, u32[]{:S(2)}) collective-permute-start(bf16[16,16,2048]{2,1,0:T(8,128)(2,1)S(1)} %all_to_all.10), channel_id=1, source_target_pairs={{0,1},{1,0},{2,3},{3,2},{4,5},{5,4},{6,7},{7,6},{8,9},{9,8},{10,11... | collective-permute-start | bytes 3145736 | tf_op jit(solution)/shard_map/ppermute | solution.py:152
  30.3 2.5 %copy.18 = bf16[1024,512]{0,1:T(8,128)(2,1)} copy(bf16[1024,512]{1,0:T(8,128)(2,1)} %param.10) | data formatting | bytes 2097152 | tf_op args[2]
  42.4 2.4 %copy.20 = f32[512,1536]{1,0:T(8,128)S(1)} copy(f32[512,1536]{0,1:T(8,128)} %pad_maximum_fusion.1) | data formatting | bytes 6291456 | tf_op jit(solution)/shard_map/concatenate | solution.py:184
  45.3 5.6 %collective-permute-start.5 = (f32[64,1536]{1,0:T(8,128)S(1)}, f32[64,1536]{1,0:T(8,128)S(1)}, u32[]{:S(2)}, u32[]{:S(2)}) collective-permute-start(f32[64,1536]{1,0:T(8,128)S(1)} %pad_maximum_fusion.5), channel_id=1, source_target_pairs={{0,224},{32,0},{64,32},{96,64},{128,96},{160,128},{192,160},{224,1... | collective-permute-start | bytes 1179656 | tf_op jit(solution)/shard_map/ppermute | solution.py:80
  51.1 8.3 %collective-permute-done.5 = f32[64,1536]{1,0:T(8,128)S(1)} collective-permute-done((f32[64,1536]{1,0:T(8,128)S(1)}, f32[64,1536]{1,0:T(8,128)S(1)}, u32[]{:S(2)}, u32[]{:S(2)}) %collective-permute-start.5) | collective-permute-done | bytes 393248 | tf_op jit(solution)/shard_map/ppermute | solution.py:80
  59.5 3.5 %collective-permute-start.6 = (f32[64,1536]{1,0:T(8,128)S(1)}, f32[64,1536]{1,0:T(8,128)S(1)}, u32[]{:S(2)}, u32[]{:S(2)}) collective-permute-start(f32[64,1536]{1,0:T(8,128)S(1)} %pad_maximum_fusion.6), channel_id=1, source_target_pairs={{0,224},{32,0},{64,32},{96,64},{128,96},{160,128},{192,160},{224,1... | collective-permute-start | bytes 1179656 | tf_op jit(solution)/shard_map/ppermute | solution.py:80
  63.1 7.4 %collective-permute-done.6 = f32[64,1536]{1,0:T(8,128)S(1)} collective-permute-done((f32[64,1536]{1,0:T(8,128)S(1)}, f32[64,1536]{1,0:T(8,128)S(1)}, u32[]{:S(2)}, u32[]{:S(2)}) %collective-permute-start.6) | collective-permute-done | bytes 393248 | tf_op jit(solution)/shard_map/ppermute | solution.py:80
  70.6 3.5 %collective-permute-start.7 = (f32[64,1536]{1,0:T(8,128)S(1)}, f32[64,1536]{1,0:T(8,128)S(1)}, u32[]{:S(2)}, u32[]{:S(2)}) collective-permute-start(f32[64,1536]{1,0:T(8,128)S(1)} %pad_maximum_fusion.7), channel_id=1, source_target_pairs={{0,224},{32,0},{64,32},{96,64},{128,96},{160,128},{192,160},{224,1... | collective-permute-start | bytes 1179656 | tf_op jit(solution)/shard_map/ppermute | solution.py:80
  74.3 6.6 %collective-permute-done.7 = f32[64,1536]{1,0:T(8,128)S(1)} collective-permute-done((f32[64,1536]{1,0:T(8,128)S(1)}, f32[64,1536]{1,0:T(8,128)S(1)}, u32[]{:S(2)}, u32[]{:S(2)}) %collective-permute-start.7) | collective-permute-done | bytes 393248 | tf_op jit(solution)/shard_map/ppermute | solution.py:80
  80.9 3.7 %collective-permute-start.8 = (f32[64,768]{1,0:T(8,128)S(1)}, f32[64,768]{1,0:T(8,128)S(1)}, u32[]{:S(2)}, u32[]{:S(2)}) collective-permute-start(f32[64,768]{1,0:T(8,128)S(1)} %slice_add_fusion), channel_id=1, source_target_pairs={{0,224},{32,0},{64,32},{96,64},{128,96},{160,128},{192,160},{224,1... | collective-permute-start | bytes 589832 | tf_op jit(solution)/shard_map/ppermute | solution.py:78
  84.7 2.5 %collective-permute-done.8 = f32[64,768]{1,0:T(8,128)S(1)} collective-permute-done((f32[64,768]{1,0:T(8,128)S(1)}, f32[64,768]{1,0:T(8,128)S(1)}, u32[]{:S(2)}, u32[]{:S(2)}) %collective-permute-start.8) | collective-permute-done | bytes 196640 | tf_op jit(solution)/shard_map/ppermute | solution.py:78
  87.2 3.2 %collective-permute-done.4 = f32[64,768]{1,0:T(8,128)S(1)} collective-permute-done((f32[64,768]{1,0:T(8,128)S(1)}, f32[64,768]{1,0:T(8,128)S(1)}, u32[]{:S(2)}, u32[]{:S(2)}) %collective-permute-start.4) | collective-permute-done | bytes 196640 | tf_op jit(solution)/shard_map/ppermute | solution.py:78
  92.2 3.0 %collective-permute-done.9 = bf16[64,1536]{1,0:T(8,128)(2,1)S(1)} collective-permute-done((bf16[64,1536]{1,0:T(8,128)(2,1)S(1)}, bf16[64,1536]{1,0:T(8,128)(2,1)S(1)}, u32[]{:S(2)}, u32[]{:S(2)}) %collective-permute-start.9) | collective-permute-done | bytes 196640 | tf_op jit(solution)/shard_map/ppermute | solution.py:127
  97.0 5.1 %collective-permute-done.10 = bf16[64,1536]{1,0:T(8,128)(2,1)S(1)} collective-permute-done((bf16[64,1536]{1,0:T(8,128)(2,1)S(1)}, bf16[64,1536]{1,0:T(8,128)(2,1)S(1)}, u32[]{:S(2)}, u32[]{:S(2)}) %collective-permute-start.10) | collective-permute-done | bytes 196640 | tf_op jit(solution)/shard_map/ppermute | solution.py:127
  103.8 7.2 %collective-permute-done.14 = bf16[64,1536]{1,0:T(8,128)(2,1)S(1)} collective-permute-done((bf16[64,1536]{1,0:T(8,128)(2,1)S(1)}, bf16[64,1536]{1,0:T(8,128)(2,1)S(1)}, u32[]{:S(2)}, u32[]{:S(2)}) %collective-permute-start.14) | collective-permute-done | bytes 196640 | tf_op jit(solution)/shard_map/ppermute | solution.py:126
  111.1 2.7 %collective-permute-start.16 = (bf16[64,768]{1,0:T(8,128)(2,1)S(1)}, bf16[64,768]{1,0:T(8,128)(2,1)S(1)}, u32[]{:S(2)}, u32[]{:S(2)}) collective-permute-start(bf16[64,768]{1,0:T(8,128)(2,1)S(1)} %slice.207), channel_id=1, source_target_pairs={{0,224},{32,0},{64,32},{96,64},{128,96},{160,128},{192,160},{224,1... | collective-permute-start | bytes 294920 | tf_op jit(solution)/shard_map/ppermute | solution.py:134
  113.8 2.5 %collective-permute-done.15 = bf16[64,768]{1,0:T(8,128)(2,1)S(1)} collective-permute-done((bf16[64,768]{1,0:T(8,128)(2,1)S(1)}, bf16[64,768]{1,0:T(8,128)(2,1)S(1)}, u32[]{:S(2)}, u32[]{:S(2)}) %collective-permute-start.15) | collective-permute-done | bytes 98336 | tf_op jit(solution)/shard_map/ppermute | solution.py:133
  125.1 8.1 %collective-permute-start.17 = (f32[16,16,2048]{2,1,0:T(8,128)}, f32[16,16,2048]{2,1,0:T(8,128)S(1)}, u32[]{:S(2)}, u32[]{:S(2)}) collective-permute-start(f32[16,16,2048]{2,1,0:T(8,128)} %dynamic-slice_bitcast_fusion), channel_id=1, source_target_pairs={{0,1},{1,0},{2,3},{3,2},{4,5},{5,4},{6,7},{7,6},{8,9},{9,8},{10,11... | collective-permute-start | bytes 6291464 | tf_op jit(solution)/shard_map/ppermute | solution.py:163
  133.3 4.0 %collective-permute-done.17 = f32[16,16,2048]{2,1,0:T(8,128)S(1)} collective-permute-done((f32[16,16,2048]{2,1,0:T(8,128)}, f32[16,16,2048]{2,1,0:T(8,128)S(1)}, u32[]{:S(2)}, u32[]{:S(2)}) %collective-permute-start.17) | collective-permute-done | bytes 2097184 | tf_op jit(solution)/shard_map/ppermute | solution.py:163
  137.3 3.2 %bitcast_add_fusion = f32[16,16,2048]{2,1,0:T(8,128)} fusion(f32[16,16,2048]{2,1,0:T(8,128)S(1)} %collective-permute-done.17, f32[16,2,16,2048]{3,2,1,0:T(8,128)} %bitcast.69, s32[]{:T(128)S(6)} %select_n.139), kind=kLoop, calls=%fused_computation.3 | loop fusion | flops 524288 | bytes 6291460 | tf_op jit(solution)/shard_map/add | solution.py:163
  140.5 3.9 %all-to-all-start.1 = ((f32[16,16,2048]{2,1,0:T(8,128)}), f32[16,16,2048]{2,1,0:T(8,128)S(1)}, u32[]{:S(2)}, u32[]{:S(2)}) async-start(f32[16,16,2048]{2,1,0:T(8,128)} %bitcast_add_fusion), calls=%async_computation.1 | async-start | bytes 4194304 | tf_op jit(solution)/shard_map/all_to_all | solution.py:164
  145.9 3.4 %convolution_select_fusion.1 = f32[1024,512]{1,0:T(8,128)} fusion(pred[1024,512]{1,0:T(32,128)(4,1)S(1)} %copy.22, bf16[512,2048]{1,0:T(8,128)(2,1)} %bitcast.84, bf16[512,1536]{1,0:T(8,128)(2,1)S(1)} %bitcast.78), kind=kOutput, calls=%fused_computation.6 | convolution fusion | flops 537395200 | bytes 4194304 | tf_op jit(solution)/shard_map/dot_general | solution.py:33
  153.4 23.8 %all-to-all-done.1 = f32[16,16,2048]{2,1,0:T(8,128)S(1)} async-done(((f32[16,16,2048]{2,1,0:T(8,128)}), f32[16,16,2048]{2,1,0:T(8,128)S(1)}, u32[]{:S(2)}, u32[]{:S(2)}) %all-to-all-start.1) | async-done | bytes 2097184 | tf_op jit(solution)/shard_map/all_to_all | solution.py:164
  (131 shorter events, 35.0 us)
Async XLA Ops:
  0.6 26.5 %slice-start = ((s32[2048]{0:T(1024)}), s32[1024]{0:T(1024)S(1)}, s32[]{:S(2)}) async-start(s32[2048]{0:T(1024)} %param.13), calls=%async_computation.2 | async-start | bytes 8192 | tf_op jit(solution)/shard_map/slice | solution.py:14
  0.6 26.5 %slice-start.1 = ((s32[2048]{0:T(1024)}), s32[1024]{0:T(1024)S(1)}, s32[]{:S(2)}) async-start(s32[2048]{0:T(1024)} %param.14), calls=%async_computation.3 | async-start | bytes 8192 | tf_op jit(solution)/shard_map/slice | solution.py:14
  25.0 9.5 %collective-permute-start = (bf16[16,16,2048]{2,1,0:T(8,128)(2,1)S(1)}, bf16[16,16,2048]{2,1,0:T(8,128)(2,1)}, u32[]{:S(2)}, u32[]{:S(2)}) collective-permute-start(bf16[16,16,2048]{2,1,0:T(8,128)(2,1)S(1)} %all_to_all.10), channel_id=1, source_target_pairs={{0,1},{1,0},{2,3},{3,2},{4,5},{5,4},{6,7},{7,6},{8,9},{9,8},{10,11... | collective-permute-start | bytes 3145736 | tf_op jit(solution)/shard_map/ppermute | solution.py:152
  28.0 8.4 %copy-start.1 = (pred[64,8,4,256]{3,1,2,0:T(8,128)(4,1)}, pred[64,8,4,256]{3,1,2,0:T(8,128)(4,1)S(1)}, u32[]{:S(2)}) copy-start(pred[64,8,4,256]{3,1,2,0:T(8,128)(4,1)S(1)} %copy.24) | copy-start | bytes 1572868
  29.7 6.7 %copy-start.3 = (bf16[1024,512]{0,1:T(8,128)(2,1)}, bf16[1024,512]{0,1:T(8,128)(2,1)S(1)}, u32[]{:S(2)}) copy-start(bf16[1024,512]{0,1:T(8,128)(2,1)S(1)} %copy.19) | copy-start | bytes 3145732
  30.3 6.8 %copy-start.9 = (pred[64,8,4,256]{3,1,2,0:T(8,128)(4,1)}, pred[64,8,4,256]{3,1,2,0:T(8,128)(4,1)S(1)}, u32[]{:S(2)}) copy-start(pred[64,8,4,256]{3,1,2,0:T(8,128)(4,1)S(1)} %copy.23) | copy-start | bytes 1572868
  45.3 14.1 %collective-permute-start.5 = (f32[64,1536]{1,0:T(8,128)S(1)}, f32[64,1536]{1,0:T(8,128)S(1)}, u32[]{:S(2)}, u32[]{:S(2)}) collective-permute-start(f32[64,1536]{1,0:T(8,128)S(1)} %pad_maximum_fusion.5), channel_id=1, source_target_pairs={{0,224},{32,0},{64,32},{96,64},{128,96},{160,128},{192,160},{224,1... | collective-permute-start | bytes 1179656 | tf_op jit(solution)/shard_map/ppermute | solution.py:80
  51.0 12.0 %collective-permute-start.1 = (f32[64,1536]{1,0:T(8,128)S(1)}, f32[64,1536]{1,0:T(8,128)S(1)}, u32[]{:S(2)}, u32[]{:S(2)}) collective-permute-start(f32[64,1536]{1,0:T(8,128)S(1)} %pad_maximum_fusion.2), channel_id=1, source_target_pairs={{0,32},{32,64},{64,96},{96,128},{128,160},{160,192},{192,224},{224... | collective-permute-start | bytes 1179656 | tf_op jit(solution)/shard_map/ppermute | solution.py:80
  59.5 11.1 %collective-permute-start.6 = (f32[64,1536]{1,0:T(8,128)S(1)}, f32[64,1536]{1,0:T(8,128)S(1)}, u32[]{:S(2)}, u32[]{:S(2)}) collective-permute-start(f32[64,1536]{1,0:T(8,128)S(1)} %pad_maximum_fusion.6), channel_id=1, source_target_pairs={{0,224},{32,0},{64,32},{96,64},{128,96},{160,128},{192,160},{224,1... | collective-permute-start | bytes 1179656 | tf_op jit(solution)/shard_map/ppermute | solution.py:80
  63.0 11.1 %collective-permute-start.2 = (f32[64,1536]{1,0:T(8,128)S(1)}, f32[64,1536]{1,0:T(8,128)S(1)}, u32[]{:S(2)}, u32[]{:S(2)}) collective-permute-start(f32[64,1536]{1,0:T(8,128)S(1)} %pad_maximum_fusion.3), channel_id=1, source_target_pairs={{0,32},{32,64},{64,96},{96,128},{128,160},{160,192},{192,224},{224... | collective-permute-start | bytes 1179656 | tf_op jit(solution)/shard_map/ppermute | solution.py:80
  70.6 10.2 %collective-permute-start.7 = (f32[64,1536]{1,0:T(8,128)S(1)}, f32[64,1536]{1,0:T(8,128)S(1)}, u32[]{:S(2)}, u32[]{:S(2)}) collective-permute-start(f32[64,1536]{1,0:T(8,128)S(1)} %pad_maximum_fusion.7), channel_id=1, source_target_pairs={{0,224},{32,0},{64,32},{96,64},{128,96},{160,128},{192,160},{224,1... | collective-permute-start | bytes 1179656 | tf_op jit(solution)/shard_map/ppermute | solution.py:80
  74.2 10.4 %collective-permute-start.3 = (f32[64,1536]{1,0:T(8,128)S(1)}, f32[64,1536]{1,0:T(8,128)S(1)}, u32[]{:S(2)}, u32[]{:S(2)}) collective-permute-start(f32[64,1536]{1,0:T(8,128)S(1)} %pad_maximum_fusion.4), channel_id=1, source_target_pairs={{0,32},{32,64},{64,96},{96,128},{128,160},{160,192},{192,224},{224... | collective-permute-start | bytes 1179656 | tf_op jit(solution)/shard_map/ppermute | solution.py:80
  80.9 6.3 %collective-permute-start.8 = (f32[64,768]{1,0:T(8,128)S(1)}, f32[64,768]{1,0:T(8,128)S(1)}, u32[]{:S(2)}, u32[]{:S(2)}) collective-permute-start(f32[64,768]{1,0:T(8,128)S(1)} %slice_add_fusion), channel_id=1, source_target_pairs={{0,224},{32,0},{64,32},{96,64},{128,96},{160,128},{192,160},{224,1... | collective-permute-start | bytes 589832 | tf_op jit(solution)/shard_map/ppermute | solution.py:78
  84.6 5.8 %collective-permute-start.4 = (f32[64,768]{1,0:T(8,128)S(1)}, f32[64,768]{1,0:T(8,128)S(1)}, u32[]{:S(2)}, u32[]{:S(2)}) collective-permute-start(f32[64,768]{1,0:T(8,128)S(1)} %slice_add_fusion.7), channel_id=1, source_target_pairs={{0,32},{32,64},{64,96},{96,128},{128,160},{160,192},{192,224},{224... | collective-permute-start | bytes 589832 | tf_op jit(solution)/shard_map/ppermute | solution.py:78
  90.6 4.6 %collective-permute-start.9 = (bf16[64,1536]{1,0:T(8,128)(2,1)S(1)}, bf16[64,1536]{1,0:T(8,128)(2,1)S(1)}, u32[]{:S(2)}, u32[]{:S(2)}) collective-permute-start(bf16[64,1536]{1,0:T(8,128)(2,1)S(1)} %pad_maximum_fusion.8), channel_id=1, source_target_pairs={{0,224},{32,0},{64,32},{96,64},{128,96},{160,128},{192,160},{224,1... | collective-permute-start | bytes 589832 | tf_op jit(solution)/shard_map/ppermute | solution.py:127
  90.7 5.8 %collective-permute-start.12 = (bf16[64,1536]{1,0:T(8,128)(2,1)S(1)}, bf16[64,1536]{1,0:T(8,128)(2,1)S(1)}, u32[]{:S(2)}, u32[]{:S(2)}) collective-permute-start(bf16[64,1536]{1,0:T(8,128)(2,1)S(1)} %pad_maximum_fusion.8), channel_id=1, source_target_pairs={{0,32},{32,64},{64,96},{96,128},{128,160},{160,192},{192,224},{224... | collective-permute-start | bytes 589832 | tf_op jit(solution)/shard_map/ppermute | solution.py:126
  95.2 6.9 %collective-permute-start.10 = (bf16[64,1536]{1,0:T(8,128)(2,1)S(1)}, bf16[64,1536]{1,0:T(8,128)(2,1)S(1)}, u32[]{:S(2)}, u32[]{:S(2)}) collective-permute-start(bf16[64,1536]{1,0:T(8,128)(2,1)S(1)} %collective-permute-done.9), channel_id=1, source_target_pairs={{0,224},{32,0},{64,32},{96,64},{128,96},{160,128},{192,160},{224,1... | collective-permute-start | bytes 589832 | tf_op jit(solution)/shard_map/ppermute | solution.py:127
  96.5 6.6 %collective-permute-start.13 = (bf16[64,1536]{1,0:T(8,128)(2,1)S(1)}, bf16[64,1536]{1,0:T(8,128)(2,1)S(1)}, u32[]{:S(2)}, u32[]{:S(2)}) collective-permute-start(bf16[64,1536]{1,0:T(8,128)(2,1)S(1)} %collective-permute-done.12), channel_id=1, source_target_pairs={{0,32},{32,64},{64,96},{96,128},{128,160},{160,192},{192,224},{224... | collective-permute-start | bytes 589832 | tf_op jit(solution)/shard_map/ppermute | solution.py:126
  102.1 9.0 %collective-permute-start.11 = (bf16[64,1536]{1,0:T(8,128)(2,1)S(1)}, bf16[64,1536]{1,0:T(8,128)(2,1)S(1)}, u32[]{:S(2)}, u32[]{:S(2)}) collective-permute-start(bf16[64,1536]{1,0:T(8,128)(2,1)S(1)} %collective-permute-done.10), channel_id=1, source_target_pairs={{0,224},{32,0},{64,32},{96,64},{128,96},{160,128},{192,160},{224,1... | collective-permute-start | bytes 589832 | tf_op jit(solution)/shard_map/ppermute | solution.py:127
  103.1 7.9 %collective-permute-start.14 = (bf16[64,1536]{1,0:T(8,128)(2,1)S(1)}, bf16[64,1536]{1,0:T(8,128)(2,1)S(1)}, u32[]{:S(2)}, u32[]{:S(2)}) collective-permute-start(bf16[64,1536]{1,0:T(8,128)(2,1)S(1)} %collective-permute-done.13), channel_id=1, source_target_pairs={{0,32},{32,64},{64,96},{96,128},{128,160},{160,192},{192,224},{224... | collective-permute-start | bytes 589832 | tf_op jit(solution)/shard_map/ppermute | solution.py:126
  111.0 5.3 %collective-permute-start.15 = (bf16[64,768]{1,0:T(8,128)(2,1)S(1)}, bf16[64,768]{1,0:T(8,128)(2,1)S(1)}, u32[]{:S(2)}, u32[]{:S(2)}) collective-permute-start(bf16[64,768]{1,0:T(8,128)(2,1)S(1)} %slice.206), channel_id=1, source_target_pairs={{0,32},{32,64},{64,96},{96,128},{128,160},{160,192},{192,224},{224... | collective-permute-start | bytes 294920 | tf_op jit(solution)/shard_map/ppermute | solution.py:133
  111.1 5.2 %collective-permute-start.16 = (bf16[64,768]{1,0:T(8,128)(2,1)S(1)}, bf16[64,768]{1,0:T(8,128)(2,1)S(1)}, u32[]{:S(2)}, u32[]{:S(2)}) collective-permute-start(bf16[64,768]{1,0:T(8,128)(2,1)S(1)} %slice.207), channel_id=1, source_target_pairs={{0,224},{32,0},{64,32},{96,64},{128,96},{160,128},{192,160},{224,1... | collective-permute-start | bytes 294920 | tf_op jit(solution)/shard_map/ppermute | solution.py:134
  125.1 12.1 %collective-permute-start.17 = (f32[16,16,2048]{2,1,0:T(8,128)}, f32[16,16,2048]{2,1,0:T(8,128)S(1)}, u32[]{:S(2)}, u32[]{:S(2)}) collective-permute-start(f32[16,16,2048]{2,1,0:T(8,128)} %dynamic-slice_bitcast_fusion), channel_id=1, source_target_pairs={{0,1},{1,0},{2,3},{3,2},{4,5},{5,4},{6,7},{7,6},{8,9},{9,8},{10,11... | collective-permute-start | bytes 6291464 | tf_op jit(solution)/shard_map/ppermute | solution.py:163
  140.5 36.7 %all-to-all-start.1 = ((f32[16,16,2048]{2,1,0:T(8,128)}), f32[16,16,2048]{2,1,0:T(8,128)S(1)}, u32[]{:S(2)}, u32[]{:S(2)}) async-start(f32[16,16,2048]{2,1,0:T(8,128)} %bitcast_add_fusion), calls=%async_computation.1 | async-start | bytes 4194304 | tf_op jit(solution)/shard_map/all_to_all | solution.py:164
  (16 other events, 31.6 us)

commit v8 on v7

--- a/solution.py
+++ b/solution.py
@@ -144,22 +144,22 @@
     return placed.reshape((count * block.shape[0],) + block.shape[1:])
 
 
-def col_gather(block):
+def col_gather(block, groups):
     chips = lax.axis_size("chip")
-    core = lax.axis_index("core")
     spread = jnp.broadcast_to(block[None], (chips,) + block.shape)
     mine = lax.all_to_all(spread, "chip", 0, 0, tiled=True)
     other = lax.ppermute(mine, "core", [(0, 1), (1, 0)])
-    paired = jnp.where(core == 0, jnp.stack([mine, other], 1), jnp.stack([other, mine], 1))
+    grouped = (groups, chips // groups) + block.shape
+    paired = jnp.stack([mine.reshape(grouped), other.reshape(grouped)], axis=1)
     return paired.reshape((chips * 2 * block.shape[0],) + block.shape[1:])
 
 
-def col_scatter_sum(parts):
+def col_scatter_sum(parts, groups):
     chips = lax.axis_size("chip")
-    core = lax.axis_index("core")
-    pieces = parts.reshape((chips, 2, parts.shape[0] // (2 * chips)) + parts.shape[1:])
-    mine = lax.dynamic_index_in_dim(pieces, core, 1, keepdims=False)
-    other = lax.dynamic_index_in_dim(pieces, 1 - core, 1, keepdims=False)
+    rows_each = parts.shape[0] // (2 * chips)
+    pieces = parts.reshape((groups, 2, chips // groups, rows_each) + parts.shape[1:])
+    mine = pieces[:, 0].reshape((chips, rows_each) + parts.shape[1:])
+    other = pieces[:, 1].reshape((chips, rows_each) + parts.shape[1:])
     pair_sum = mine + lax.ppermute(other, "core", [(0, 1), (1, 0)])
     return lax.all_to_all(pair_sum, "chip", 0, 0, tiled=True).sum(axis=0)
 
@@ -176,7 +176,8 @@
     keep_up = kept_table(order_up, row_start, col_start, rows_here, cols_here, hidden_blocks)
     keep_down = kept_table(order_down, col_start, row_start, cols_here, rows_here, width_blocks)
     width_here = tokens.shape[1]
-    inputs_all = col_gather(jnp.concatenate([tokens, cotangent], axis=1))
+    groups = lax.axis_size("row")
+    inputs_all = col_gather(jnp.concatenate([tokens, cotangent], axis=1), groups)
     tokens_all, cotangent_all = inputs_all[:, :width_here], inputs_all[:, width_here:]
     gate_term = apply_blocks(tokens_all, w_gate, keep_gate, "forward")
     up_term = apply_blocks(tokens_all, w_up, keep_up, "forward")
@@ -202,7 +203,7 @@
     up_weight_grad = apply_blocks(tokens_all, up_grad_all, keep_up, "weights")
     through_gate = apply_blocks(gate_grad_all, w_gate, keep_gate, "transposed")
     through_up = apply_blocks(up_grad_all, w_up, keep_up, "transposed")
-    outs = col_scatter_sum(jnp.concatenate([output_term, through_gate + through_up], axis=1))
+    outs = col_scatter_sum(jnp.concatenate([output_term, through_gate + through_up], axis=1), groups)
     output = outs[:, :width_here].astype(jnp.bfloat16)
     input_grad = outs[:, width_here:]
     return (

time: 179 us -> 172 us (0.961)
  local copies, waits for them, and re-layouts: 19.5 us -> 15.3 us
  other arithmetic: 9.61 us -> 7.62 us
    unnamed x52 -> x50, local copies, waits for them, and re-layouts: 11.8 us -> 9.09 us
    select_n x1 -> x0, other arithmetic: 1.84 us -> none  [col_gather(): jnp.where(core == 0, jnp.stack([mine, other], 1), jnp.stack([other, mine]...]
  transfers between devices with their start and end apart: 19 -> 19, of which waited for: 13 -> 13; matrix products, arithmetic and copies ran while one was open for 9% -> 10% of each run, Pallas kernels for 0% -> 0%
where the time goes in v8:
time: 172 us
  waiting for transfers between devices  74 us (43%)
  starting transfers between devices  38.2 us (22%)
  blocking collectives  23.4 us (14%)
  local copies, waits for them, and re-layouts  15.3 us (9%)
  matrix products  12 us (7%)
  other arithmetic  7.62 us (4%)
    all_to_all x1, waiting for transfers between devices, col_scatter_sum(): return lax.all_to_all(pair_sum, 'chip', 0, 0, tiled=True).sum(axis=0)  24 us
    all_to_all x1, blocking collectives, col_gather(): mine = lax.all_to_all(spread, 'chip', 0, 0, tiled=True)  23.4 us
    ppermute x6, waiting for transfers between devices, joint_permute(): moved = lax.ppermute(jnp.concatenate(values, axis=1), axis_name, pairs)  22.3 us
    ppermute x6, starting transfers between devices, joint_permute(): moved = lax.ppermute(jnp.concatenate(values, axis=1), axis_name, pairs)  12.9 us
    unnamed x50, local copies, waits for them, and re-layouts  9.09 us
    ppermute x1, starting transfers between devices, col_scatter_sum(): pair_sum = mine + lax.ppermute(other, 'core', [(0, 1), (1, 0)])  8.22 us
    ppermute x3, waiting for transfers between devices, relay_gather(): carry_behind = lax.ppermute(carry_behind, axis_name, backward)  8.13 us
    ppermute x3, waiting for transfers between devices, relay_gather(): carry_ahead = lax.ppermute(carry_ahead, axis_name, forward)  7.66 us
  transfers between devices with their start and end apart: 19, of which 13 were waited for; matrix products, arithmetic and copies ran while one was open for 10% of the time, Pallas kernels for 0%

profile of v8, /device:TPU:1, one launch (start us, length us, event | category | flops | bytes accessed | tf_op | source)
XLA Modules:
  0.0 171.8 jit_solution(17066892174489331237)
XLA Ops:
  1.6 23.4 %all_to_all.10 = bf16[16,16,2048]{2,1,0:T(8,128)(2,1)S(1)} all-to-all(bf16[16,16,2048]{2,1,0:T(8,128)(2,1)S(1)} %broadcast_in_dim.8), channel_id=1, replica_groups=mesh['row'=8,'chip'=16,'core'=2] {'chip'}, dimensions={0} | all-to-all | bytes 2097152 | tf_op jit(solution)/shard_map/all_to_all | solution.py:150
  25.0 2.1 %collective-permute-start = (bf16[16,16,2048]{2,1,0:T(8,128)(2,1)S(1)}, bf16[16,16,2048]{2,1,0:T(8,128)(2,1)}, u32[]{:S(2)}, u32[]{:S(2)}) collective-permute-start(bf16[16,16,2048]{2,1,0:T(8,128)(2,1)S(1)} %all_to_all.10), channel_id=1, source_target_pairs={{0,1},{1,0},{2,3},{3,2},{4,5},{5,4},{6,7},{7,6},{8,9},{9,8},{10,11... | collective-permute-start | bytes 3145736 | tf_op jit(solution)/shard_map/ppermute | solution.py:151
  30.3 2.5 %copy.18 = bf16[1024,512]{0,1:T(8,128)(2,1)} copy(bf16[1024,512]{1,0:T(8,128)(2,1)} %param.10) | data formatting | bytes 2097152 | tf_op args[2]
  41.4 2.4 %copy.20 = f32[512,1536]{1,0:T(8,128)S(1)} copy(f32[512,1536]{0,1:T(8,128)} %pad_maximum_fusion.1) | data formatting | bytes 6291456 | tf_op jit(solution)/shard_map/concatenate | solution.py:185
  44.2 5.7 %collective-permute-start.5 = (f32[64,1536]{1,0:T(8,128)S(1)}, f32[64,1536]{1,0:T(8,128)S(1)}, u32[]{:S(2)}, u32[]{:S(2)}) collective-permute-start(f32[64,1536]{1,0:T(8,128)S(1)} %pad_maximum_fusion.6), channel_id=1, source_target_pairs={{0,224},{32,0},{64,32},{96,64},{128,96},{160,128},{192,160},{224,1... | collective-permute-start | bytes 1179656 | tf_op jit(solution)/shard_map/ppermute | solution.py:80
  50.0 8.3 %collective-permute-done.5 = f32[64,1536]{1,0:T(8,128)S(1)} collective-permute-done((f32[64,1536]{1,0:T(8,128)S(1)}, f32[64,1536]{1,0:T(8,128)S(1)}, u32[]{:S(2)}, u32[]{:S(2)}) %collective-permute-start.5) | collective-permute-done | bytes 393248 | tf_op jit(solution)/shard_map/ppermute | solution.py:80
  58.4 3.5 %collective-permute-start.6 = (f32[64,1536]{1,0:T(8,128)S(1)}, f32[64,1536]{1,0:T(8,128)S(1)}, u32[]{:S(2)}, u32[]{:S(2)}) collective-permute-start(f32[64,1536]{1,0:T(8,128)S(1)} %pad_maximum_fusion.7), channel_id=1, source_target_pairs={{0,224},{32,0},{64,32},{96,64},{128,96},{160,128},{192,160},{224,1... | collective-permute-start | bytes 1179656 | tf_op jit(solution)/shard_map/ppermute | solution.py:80
  62.1 7.4 %collective-permute-done.6 = f32[64,1536]{1,0:T(8,128)S(1)} collective-permute-done((f32[64,1536]{1,0:T(8,128)S(1)}, f32[64,1536]{1,0:T(8,128)S(1)}, u32[]{:S(2)}, u32[]{:S(2)}) %collective-permute-start.6) | collective-permute-done | bytes 393248 | tf_op jit(solution)/shard_map/ppermute | solution.py:80
  69.6 3.5 %collective-permute-start.7 = (f32[64,1536]{1,0:T(8,128)S(1)}, f32[64,1536]{1,0:T(8,128)S(1)}, u32[]{:S(2)}, u32[]{:S(2)}) collective-permute-start(f32[64,1536]{1,0:T(8,128)S(1)} %pad_maximum_fusion.8), channel_id=1, source_target_pairs={{0,224},{32,0},{64,32},{96,64},{128,96},{160,128},{192,160},{224,1... | collective-permute-start | bytes 1179656 | tf_op jit(solution)/shard_map/ppermute | solution.py:80
  73.3 6.6 %collective-permute-done.7 = f32[64,1536]{1,0:T(8,128)S(1)} collective-permute-done((f32[64,1536]{1,0:T(8,128)S(1)}, f32[64,1536]{1,0:T(8,128)S(1)}, u32[]{:S(2)}, u32[]{:S(2)}) %collective-permute-start.7) | collective-permute-done | bytes 393248 | tf_op jit(solution)/shard_map/ppermute | solution.py:80
  79.9 3.7 %collective-permute-start.8 = (f32[64,768]{1,0:T(8,128)S(1)}, f32[64,768]{1,0:T(8,128)S(1)}, u32[]{:S(2)}, u32[]{:S(2)}) collective-permute-start(f32[64,768]{1,0:T(8,128)S(1)} %slice_add_fusion), channel_id=1, source_target_pairs={{0,224},{32,0},{64,32},{96,64},{128,96},{160,128},{192,160},{224,1... | collective-permute-start | bytes 589832 | tf_op jit(solution)/shard_map/ppermute | solution.py:78
  83.7 2.5 %collective-permute-done.8 = f32[64,768]{1,0:T(8,128)S(1)} collective-permute-done((f32[64,768]{1,0:T(8,128)S(1)}, f32[64,768]{1,0:T(8,128)S(1)}, u32[]{:S(2)}, u32[]{:S(2)}) %collective-permute-start.8) | collective-permute-done | bytes 196640 | tf_op jit(solution)/shard_map/ppermute | solution.py:78
  86.1 3.2 %collective-permute-done.4 = f32[64,768]{1,0:T(8,128)S(1)} collective-permute-done((f32[64,768]{1,0:T(8,128)S(1)}, f32[64,768]{1,0:T(8,128)S(1)}, u32[]{:S(2)}, u32[]{:S(2)}) %collective-permute-start.4) | collective-permute-done | bytes 196640 | tf_op jit(solution)/shard_map/ppermute | solution.py:78
  91.1 3.0 %collective-permute-done.9 = bf16[64,1536]{1,0:T(8,128)(2,1)S(1)} collective-permute-done((bf16[64,1536]{1,0:T(8,128)(2,1)S(1)}, bf16[64,1536]{1,0:T(8,128)(2,1)S(1)}, u32[]{:S(2)}, u32[]{:S(2)}) %collective-permute-start.9) | collective-permute-done | bytes 196640 | tf_op jit(solution)/shard_map/ppermute | solution.py:127
  95.9 5.1 %collective-permute-done.10 = bf16[64,1536]{1,0:T(8,128)(2,1)S(1)} collective-permute-done((bf16[64,1536]{1,0:T(8,128)(2,1)S(1)}, bf16[64,1536]{1,0:T(8,128)(2,1)S(1)}, u32[]{:S(2)}, u32[]{:S(2)}) %collective-permute-start.10) | collective-permute-done | bytes 196640 | tf_op jit(solution)/shard_map/ppermute | solution.py:127
  102.7 7.2 %collective-permute-done.14 = bf16[64,1536]{1,0:T(8,128)(2,1)S(1)} collective-permute-done((bf16[64,1536]{1,0:T(8,128)(2,1)S(1)}, bf16[64,1536]{1,0:T(8,128)(2,1)S(1)}, u32[]{:S(2)}, u32[]{:S(2)}) %collective-permute-start.14) | collective-permute-done | bytes 196640 | tf_op jit(solution)/shard_map/ppermute | solution.py:126
  110.0 2.7 %collective-permute-start.16 = (bf16[64,768]{1,0:T(8,128)(2,1)S(1)}, bf16[64,768]{1,0:T(8,128)(2,1)S(1)}, u32[]{:S(2)}, u32[]{:S(2)}) collective-permute-start(bf16[64,768]{1,0:T(8,128)(2,1)S(1)} %slice.215), channel_id=1, source_target_pairs={{0,224},{32,0},{64,32},{96,64},{128,96},{160,128},{192,160},{224,1... | collective-permute-start | bytes 294920 | tf_op jit(solution)/shard_map/ppermute | solution.py:134
  112.8 2.5 %collective-permute-done.15 = bf16[64,768]{1,0:T(8,128)(2,1)S(1)} collective-permute-done((bf16[64,768]{1,0:T(8,128)(2,1)S(1)}, bf16[64,768]{1,0:T(8,128)(2,1)S(1)}, u32[]{:S(2)}, u32[]{:S(2)}) %collective-permute-start.15) | collective-permute-done | bytes 98336 | tf_op jit(solution)/shard_map/ppermute | solution.py:133
  120.7 8.2 %collective-permute-start.17 = (f32[16,16,2048]{2,1,0:T(8,128)S(1)}, f32[16,16,2048]{2,1,0:T(8,128)S(1)}, u32[]{:S(2)}, u32[]{:S(2)}) collective-permute-start(f32[16,16,2048]{2,1,0:T(8,128)S(1)} %bitcast.91), channel_id=1, source_target_pairs={{0,1},{1,0},{2,3},{3,2},{4,5},{5,4},{6,7},{7,6},{8,9},{9,8},{10,11... | collective-permute-start | bytes 6291464 | tf_op jit(solution)/shard_map/ppermute | solution.py:163
  128.9 3.8 %collective-permute-done.17 = f32[16,16,2048]{2,1,0:T(8,128)S(1)} collective-permute-done((f32[16,16,2048]{2,1,0:T(8,128)S(1)}, f32[16,16,2048]{2,1,0:T(8,128)S(1)}, u32[]{:S(2)}, u32[]{:S(2)}) %collective-permute-start.17) | collective-permute-done | bytes 2097184 | tf_op jit(solution)/shard_map/ppermute | solution.py:163
  134.4 3.9 %all-to-all-start.1 = ((f32[16,16,2048]{2,1,0:T(8,128)}), f32[16,16,2048]{2,1,0:T(8,128)S(1)}, u32[]{:S(2)}, u32[]{:S(2)}) async-start(f32[16,16,2048]{2,1,0:T(8,128)} %bitcast_add_fusion), calls=%async_computation.1 | async-start | bytes 4194304 | tf_op jit(solution)/shard_map/all_to_all | solution.py:164
  139.6 3.4 %convolution_select_fusion.1 = f32[1024,512]{1,0:T(8,128)} fusion(pred[1024,512]{1,0:T(32,128)(4,1)S(1)} %copy.22, bf16[512,2048]{1,0:T(8,128)(2,1)} %bitcast.82, bf16[512,1536]{1,0:T(8,128)(2,1)} %bitcast.76), kind=kOutput, calls=%fused_computation.5 | convolution fusion | flops 537395200 | bytes 4194304 | tf_op jit(solution)/shard_map/dot_general | solution.py:33
  143.0 2.1 %convolution_select_fusion.2 = f32[1024,512]{1,0:T(8,128)} fusion(pred[1024,512]{1,0:T(32,128)(4,1)S(1)} %copy.21, bf16[512,2048]{1,0:T(8,128)(2,1)S(1)} %bitcast.83, bf16[512,1536]{1,0:T(8,128)(2,1)S(1)} %bitcast.77), kind=kOutput, calls=%fused_computation.6 | convolution fusion | flops 537395200 | bytes 4194304 | tf_op jit(solution)/shard_map/dot_general | solution.py:33
  147.2 24.0 %all-to-all-done.1 = f32[16,16,2048]{2,1,0:T(8,128)S(1)} async-done(((f32[16,16,2048]{2,1,0:T(8,128)}), f32[16,16,2048]{2,1,0:T(8,128)S(1)}, u32[]{:S(2)}, u32[]{:S(2)}) %all-to-all-start.1) | async-done | bytes 2097184 | tf_op jit(solution)/shard_map/all_to_all | solution.py:164
  (129 shorter events, 30.0 us)
Async XLA Ops:
  0.6 26.5 %slice-start = ((s32[2048]{0:T(1024)}), s32[1024]{0:T(1024)S(1)}, s32[]{:S(2)}) async-start(s32[2048]{0:T(1024)} %param.13), calls=%async_computation.2 | async-start | bytes 8192 | tf_op jit(solution)/shard_map/slice | solution.py:14
  0.6 26.5 %slice-start.1 = ((s32[2048]{0:T(1024)}), s32[1024]{0:T(1024)S(1)}, s32[]{:S(2)}) async-start(s32[2048]{0:T(1024)} %param.14), calls=%async_computation.3 | async-start | bytes 8192 | tf_op jit(solution)/shard_map/slice | solution.py:14
  25.0 9.5 %collective-permute-start = (bf16[16,16,2048]{2,1,0:T(8,128)(2,1)S(1)}, bf16[16,16,2048]{2,1,0:T(8,128)(2,1)}, u32[]{:S(2)}, u32[]{:S(2)}) collective-permute-start(bf16[16,16,2048]{2,1,0:T(8,128)(2,1)S(1)} %all_to_all.10), channel_id=1, source_target_pairs={{0,1},{1,0},{2,3},{3,2},{4,5},{5,4},{6,7},{7,6},{8,9},{9,8},{10,11... | collective-permute-start | bytes 3145736 | tf_op jit(solution)/shard_map/ppermute | solution.py:151
  28.0 8.0 %copy-start = (pred[64,8,4,256]{3,1,2,0:T(8,128)(4,1)}, pred[64,8,4,256]{3,1,2,0:T(8,128)(4,1)S(1)}, u32[]{:S(2)}) copy-start(pred[64,8,4,256]{3,1,2,0:T(8,128)(4,1)S(1)} %copy.24) | copy-start | bytes 1572868
  29.7 6.3 %copy-start.2 = (bf16[1024,512]{0,1:T(8,128)(2,1)}, bf16[1024,512]{0,1:T(8,128)(2,1)S(1)}, u32[]{:S(2)}) copy-start(bf16[1024,512]{0,1:T(8,128)(2,1)S(1)} %copy.19) | copy-start | bytes 3145732
  30.3 6.4 %copy-start.8 = (pred[64,8,4,256]{3,1,2,0:T(8,128)(4,1)}, pred[64,8,4,256]{3,1,2,0:T(8,128)(4,1)S(1)}, u32[]{:S(2)}) copy-start(pred[64,8,4,256]{3,1,2,0:T(8,128)(4,1)S(1)} %copy.23) | copy-start | bytes 1572868
  44.2 14.1 %collective-permute-start.5 = (f32[64,1536]{1,0:T(8,128)S(1)}, f32[64,1536]{1,0:T(8,128)S(1)}, u32[]{:S(2)}, u32[]{:S(2)}) collective-permute-start(f32[64,1536]{1,0:T(8,128)S(1)} %pad_maximum_fusion.6), channel_id=1, source_target_pairs={{0,224},{32,0},{64,32},{96,64},{128,96},{160,128},{192,160},{224,1... | collective-permute-start | bytes 1179656 | tf_op jit(solution)/shard_map/ppermute | solution.py:80
  49.9 12.0 %collective-permute-start.1 = (f32[64,1536]{1,0:T(8,128)S(1)}, f32[64,1536]{1,0:T(8,128)S(1)}, u32[]{:S(2)}, u32[]{:S(2)}) collective-permute-start(f32[64,1536]{1,0:T(8,128)S(1)} %pad_maximum_fusion.3), channel_id=1, source_target_pairs={{0,32},{32,64},{64,96},{96,128},{128,160},{160,192},{192,224},{224... | collective-permute-start | bytes 1179656 | tf_op jit(solution)/shard_map/ppermute | solution.py:80
  58.4 11.1 %collective-permute-start.6 = (f32[64,1536]{1,0:T(8,128)S(1)}, f32[64,1536]{1,0:T(8,128)S(1)}, u32[]{:S(2)}, u32[]{:S(2)}) collective-permute-start(f32[64,1536]{1,0:T(8,128)S(1)} %pad_maximum_fusion.7), channel_id=1, source_target_pairs={{0,224},{32,0},{64,32},{96,64},{128,96},{160,128},{192,160},{224,1... | collective-permute-start | bytes 1179656 | tf_op jit(solution)/shard_map/ppermute | solution.py:80
  62.0 11.1 %collective-permute-start.2 = (f32[64,1536]{1,0:T(8,128)S(1)}, f32[64,1536]{1,0:T(8,128)S(1)}, u32[]{:S(2)}, u32[]{:S(2)}) collective-permute-start(f32[64,1536]{1,0:T(8,128)S(1)} %pad_maximum_fusion.4), channel_id=1, source_target_pairs={{0,32},{32,64},{64,96},{96,128},{128,160},{160,192},{192,224},{224... | collective-permute-start | bytes 1179656 | tf_op jit(solution)/shard_map/ppermute | solution.py:80
  69.6 10.2 %collective-permute-start.7 = (f32[64,1536]{1,0:T(8,128)S(1)}, f32[64,1536]{1,0:T(8,128)S(1)}, u32[]{:S(2)}, u32[]{:S(2)}) collective-permute-start(f32[64,1536]{1,0:T(8,128)S(1)} %pad_maximum_fusion.8), channel_id=1, source_target_pairs={{0,224},{32,0},{64,32},{96,64},{128,96},{160,128},{192,160},{224,1... | collective-permute-start | bytes 1179656 | tf_op jit(solution)/shard_map/ppermute | solution.py:80
  73.2 10.4 %collective-permute-start.3 = (f32[64,1536]{1,0:T(8,128)S(1)}, f32[64,1536]{1,0:T(8,128)S(1)}, u32[]{:S(2)}, u32[]{:S(2)}) collective-permute-start(f32[64,1536]{1,0:T(8,128)S(1)} %pad_maximum_fusion.5), channel_id=1, source_target_pairs={{0,32},{32,64},{64,96},{96,128},{128,160},{160,192},{192,224},{224... | collective-permute-start | bytes 1179656 | tf_op jit(solution)/shard_map/ppermute | solution.py:80
  79.9 6.3 %collective-permute-start.8 = (f32[64,768]{1,0:T(8,128)S(1)}, f32[64,768]{1,0:T(8,128)S(1)}, u32[]{:S(2)}, u32[]{:S(2)}) collective-permute-start(f32[64,768]{1,0:T(8,128)S(1)} %slice_add_fusion), channel_id=1, source_target_pairs={{0,224},{32,0},{64,32},{96,64},{128,96},{160,128},{192,160},{224,1... | collective-permute-start | bytes 589832 | tf_op jit(solution)/shard_map/ppermute | solution.py:78
  83.6 5.8 %collective-permute-start.4 = (f32[64,768]{1,0:T(8,128)S(1)}, f32[64,768]{1,0:T(8,128)S(1)}, u32[]{:S(2)}, u32[]{:S(2)}) collective-permute-start(f32[64,768]{1,0:T(8,128)S(1)} %slice_add_fusion.7), channel_id=1, source_target_pairs={{0,32},{32,64},{64,96},{96,128},{128,160},{160,192},{192,224},{224... | collective-permute-start | bytes 589832 | tf_op jit(solution)/shard_map/ppermute | solution.py:78
  89.5 4.6 %collective-permute-start.9 = (bf16[64,1536]{1,0:T(8,128)(2,1)S(1)}, bf16[64,1536]{1,0:T(8,128)(2,1)S(1)}, u32[]{:S(2)}, u32[]{:S(2)}) collective-permute-start(bf16[64,1536]{1,0:T(8,128)(2,1)S(1)} %pad_maximum_fusion.9), channel_id=1, source_target_pairs={{0,224},{32,0},{64,32},{96,64},{128,96},{160,128},{192,160},{224,1... | collective-permute-start | bytes 589832 | tf_op jit(solution)/shard_map/ppermute | solution.py:127
  89.6 5.8 %collective-permute-start.12 = (bf16[64,1536]{1,0:T(8,128)(2,1)S(1)}, bf16[64,1536]{1,0:T(8,128)(2,1)S(1)}, u32[]{:S(2)}, u32[]{:S(2)}) collective-permute-start(bf16[64,1536]{1,0:T(8,128)(2,1)S(1)} %pad_maximum_fusion.9), channel_id=1, source_target_pairs={{0,32},{32,64},{64,96},{96,128},{128,160},{160,192},{192,224},{224... | collective-permute-start | bytes 589832 | tf_op jit(solution)/shard_map/ppermute | solution.py:126
  94.1 6.9 %collective-permute-start.10 = (bf16[64,1536]{1,0:T(8,128)(2,1)S(1)}, bf16[64,1536]{1,0:T(8,128)(2,1)S(1)}, u32[]{:S(2)}, u32[]{:S(2)}) collective-permute-start(bf16[64,1536]{1,0:T(8,128)(2,1)S(1)} %collective-permute-done.9), channel_id=1, source_target_pairs={{0,224},{32,0},{64,32},{96,64},{128,96},{160,128},{192,160},{224,1... | collective-permute-start | bytes 589832 | tf_op jit(solution)/shard_map/ppermute | solution.py:127
  95.5 6.6 %collective-permute-start.13 = (bf16[64,1536]{1,0:T(8,128)(2,1)S(1)}, bf16[64,1536]{1,0:T(8,128)(2,1)S(1)}, u32[]{:S(2)}, u32[]{:S(2)}) collective-permute-start(bf16[64,1536]{1,0:T(8,128)(2,1)S(1)} %collective-permute-done.12), channel_id=1, source_target_pairs={{0,32},{32,64},{64,96},{96,128},{128,160},{160,192},{192,224},{224... | collective-permute-start | bytes 589832 | tf_op jit(solution)/shard_map/ppermute | solution.py:126
  101.0 9.0 %collective-permute-start.11 = (bf16[64,1536]{1,0:T(8,128)(2,1)S(1)}, bf16[64,1536]{1,0:T(8,128)(2,1)S(1)}, u32[]{:S(2)}, u32[]{:S(2)}) collective-permute-start(bf16[64,1536]{1,0:T(8,128)(2,1)S(1)} %collective-permute-done.10), channel_id=1, source_target_pairs={{0,224},{32,0},{64,32},{96,64},{128,96},{160,128},{192,160},{224,1... | collective-permute-start | bytes 589832 | tf_op jit(solution)/shard_map/ppermute | solution.py:127
  102.0 7.9 %collective-permute-start.14 = (bf16[64,1536]{1,0:T(8,128)(2,1)S(1)}, bf16[64,1536]{1,0:T(8,128)(2,1)S(1)}, u32[]{:S(2)}, u32[]{:S(2)}) collective-permute-start(bf16[64,1536]{1,0:T(8,128)(2,1)S(1)} %collective-permute-done.13), channel_id=1, source_target_pairs={{0,32},{32,64},{64,96},{96,128},{128,160},{160,192},{192,224},{224... | collective-permute-start | bytes 589832 | tf_op jit(solution)/shard_map/ppermute | solution.py:126
  109.9 5.3 %collective-permute-start.15 = (bf16[64,768]{1,0:T(8,128)(2,1)S(1)}, bf16[64,768]{1,0:T(8,128)(2,1)S(1)}, u32[]{:S(2)}, u32[]{:S(2)}) collective-permute-start(bf16[64,768]{1,0:T(8,128)(2,1)S(1)} %slice.214), channel_id=1, source_target_pairs={{0,32},{32,64},{64,96},{96,128},{128,160},{160,192},{192,224},{224... | collective-permute-start | bytes 294920 | tf_op jit(solution)/shard_map/ppermute | solution.py:133
  110.0 5.2 %collective-permute-start.16 = (bf16[64,768]{1,0:T(8,128)(2,1)S(1)}, bf16[64,768]{1,0:T(8,128)(2,1)S(1)}, u32[]{:S(2)}, u32[]{:S(2)}) collective-permute-start(bf16[64,768]{1,0:T(8,128)(2,1)S(1)} %slice.215), channel_id=1, source_target_pairs={{0,224},{32,0},{64,32},{96,64},{128,96},{160,128},{192,160},{224,1... | collective-permute-start | bytes 294920 | tf_op jit(solution)/shard_map/ppermute | solution.py:134
  120.7 12.0 %collective-permute-start.17 = (f32[16,16,2048]{2,1,0:T(8,128)S(1)}, f32[16,16,2048]{2,1,0:T(8,128)S(1)}, u32[]{:S(2)}, u32[]{:S(2)}) collective-permute-start(f32[16,16,2048]{2,1,0:T(8,128)S(1)} %bitcast.91), channel_id=1, source_target_pairs={{0,1},{1,0},{2,3},{3,2},{4,5},{5,4},{6,7},{7,6},{8,9},{9,8},{10,11... | collective-permute-start | bytes 6291464 | tf_op jit(solution)/shard_map/ppermute | solution.py:163
  134.4 36.7 %all-to-all-start.1 = ((f32[16,16,2048]{2,1,0:T(8,128)}), f32[16,16,2048]{2,1,0:T(8,128)S(1)}, u32[]{:S(2)}, u32[]{:S(2)}) async-start(f32[16,16,2048]{2,1,0:T(8,128)} %bitcast_add_fusion), calls=%async_computation.1 | async-start | bytes 4194304 | tf_op jit(solution)/shard_map/all_to_all | solution.py:164
  (15 other events, 37.2 us)

commit v9 on v8

--- a/solution.py
+++ b/solution.py
@@ -1,6 +1,7 @@
 import jax
 import jax.numpy as jnp
 from jax import lax
+from jax.experimental.layout import Layout, with_layout_constraint
 from jax.sharding import Mesh, PartitionSpec as P
 
 BLOCK = 256
@@ -182,7 +183,9 @@
     gate_term = apply_blocks(tokens_all, w_gate, keep_gate, "forward")
     up_term = apply_blocks(tokens_all, w_up, keep_up, "forward")
     hidden_term = apply_blocks(cotangent_all, w_down, keep_down, "transposed")
-    sums = relay_scatter_sum(jnp.concatenate([gate_term, up_term, hidden_term], axis=1), "row")
+    row_major = Layout(major_to_minor=(0, 1))
+    partials = [with_layout_constraint(t, row_major) for t in (gate_term, up_term, hidden_term)]
+    sums = relay_scatter_sum(jnp.concatenate(partials, axis=1), "row")
     gate = sums[:, :hidden_here]
     up = sums[:, hidden_here : 2 * hidden_here]
     hidden_grad = sums[:, 2 * hidden_here :]

time: 172 us -> 171 us (level)
    concatenate x1 -> x0, local copies, waits for them, and re-layouts: 2.37 us -> none  [on_device(): jnp.concatenate([gate_term, up_term, hidden_term], axis=1)]
    concatenate x1, other arithmetic: 1.95 us -> 0.21 us  [on_device(): sums = relay_scatter_sum(jnp.concatenate(partials, axis=1), 'row')]
    unnamed x50 -> x42, local copies, waits for them, and re-layouts: 9.09 us -> 10.1 us
where the time goes in v9:
time: 171 us
  waiting for transfers between devices  74.1 us (43%)
  starting transfers between devices  37.8 us (22%)
  blocking collectives  23.4 us (14%)
  local copies, waits for them, and re-layouts  14 us (8%)
  matrix products  12 us (7%)
  other arithmetic  8.32 us (5%)
    all_to_all x1, waiting for transfers between devices, col_scatter_sum(): return lax.all_to_all(pair_sum, 'chip', 0, 0, tiled=True).sum(axis=0)  23.8 us
    all_to_all x1, blocking collectives, col_gather(): mine = lax.all_to_all(spread, 'chip', 0, 0, tiled=True)  23.4 us
    ppermute x6, waiting for transfers between devices, joint_permute(): moved = lax.ppermute(jnp.concatenate(values, axis=1), axis_name, pairs)  22.3 us
    ppermute x6, starting transfers between devices, joint_permute(): moved = lax.ppermute(jnp.concatenate(values, axis=1), axis_name, pairs)  12.9 us
    unnamed x42, local copies, waits for them, and re-layouts  10.1 us
    ppermute x1, starting transfers between devices, col_scatter_sum(): pair_sum = mine + lax.ppermute(other, 'core', [(0, 1), (1, 0)])  8.22 us
    ppermute x3, waiting for transfers between devices, relay_gather(): carry_behind = lax.ppermute(carry_behind, axis_name, backward)  8.12 us
    ppermute x3, waiting for transfers between devices, relay_gather(): carry_ahead = lax.ppermute(carry_ahead, axis_name, forward)  7.65 us
  transfers between devices with their start and end apart: 19, of which 13 were waited for; matrix products, arithmetic and copies ran while one was open for 10% of the time, Pallas kernels for 0%

profile of v9, /device:TPU:1, one launch (start us, length us, event | category | flops | bytes accessed | tf_op | source)
XLA Modules:
  0.0 170.8 jit_solution(5509723939663324421)
XLA Ops:
  1.6 23.4 %all_to_all.10 = bf16[16,16,2048]{2,1,0:T(8,128)(2,1)S(1)} all-to-all(bf16[16,16,2048]{2,1,0:T(8,128)(2,1)S(1)} %broadcast_in_dim.8), channel_id=1, replica_groups=mesh['row'=8,'chip'=16,'core'=2] {'chip'}, dimensions={0} | all-to-all | bytes 2097152 | tf_op jit(solution)/shard_map/all_to_all | solution.py:151
  25.0 2.1 %collective-permute-start = (bf16[16,16,2048]{2,1,0:T(8,128)(2,1)S(1)}, bf16[16,16,2048]{2,1,0:T(8,128)(2,1)}, u32[]{:S(2)}, u32[]{:S(2)}) collective-permute-start(bf16[16,16,2048]{2,1,0:T(8,128)(2,1)S(1)} %all_to_all.10), channel_id=1, source_target_pairs={{0,1},{1,0},{2,3},{3,2},{4,5},{5,4},{6,7},{7,6},{8,9},{9,8},{10,11... | collective-permute-start | bytes 3145736 | tf_op jit(solution)/shard_map/ppermute | solution.py:152
  30.1 2.3 %copy.17 = bf16[1024,512]{0,1:T(8,128)(2,1)} copy(bf16[1024,512]{1,0:T(8,128)(2,1)} %param.10) | data formatting | bytes 2097152 | tf_op args[2]
  40.3 5.7 %collective-permute-start.5 = (f32[64,1536]{1,0:T(8,128)S(1)}, f32[64,1536]{1,0:T(8,128)S(1)}, u32[]{:S(2)}, u32[]{:S(2)}) collective-permute-start(f32[64,1536]{1,0:T(8,128)S(1)} %pad_maximum_fusion.6), channel_id=1, source_target_pairs={{0,224},{32,0},{64,32},{96,64},{128,96},{160,128},{192,160},{224,1... | collective-permute-start | bytes 1179656 | tf_op jit(solution)/shard_map/ppermute | solution.py:81
  46.1 8.3 %collective-permute-done.5 = f32[64,1536]{1,0:T(8,128)S(1)} collective-permute-done((f32[64,1536]{1,0:T(8,128)S(1)}, f32[64,1536]{1,0:T(8,128)S(1)}, u32[]{:S(2)}, u32[]{:S(2)}) %collective-permute-start.5) | collective-permute-done | bytes 393248 | tf_op jit(solution)/shard_map/ppermute | solution.py:81
  54.5 3.5 %collective-permute-start.6 = (f32[64,1536]{1,0:T(8,128)S(1)}, f32[64,1536]{1,0:T(8,128)S(1)}, u32[]{:S(2)}, u32[]{:S(2)}) collective-permute-start(f32[64,1536]{1,0:T(8,128)S(1)} %pad_maximum_fusion.7), channel_id=1, source_target_pairs={{0,224},{32,0},{64,32},{96,64},{128,96},{160,128},{192,160},{224,1... | collective-permute-start | bytes 1179656 | tf_op jit(solution)/shard_map/ppermute | solution.py:81
  58.1 7.4 %collective-permute-done.6 = f32[64,1536]{1,0:T(8,128)S(1)} collective-permute-done((f32[64,1536]{1,0:T(8,128)S(1)}, f32[64,1536]{1,0:T(8,128)S(1)}, u32[]{:S(2)}, u32[]{:S(2)}) %collective-permute-start.6) | collective-permute-done | bytes 393248 | tf_op jit(solution)/shard_map/ppermute | solution.py:81
  65.7 3.5 %collective-permute-start.7 = (f32[64,1536]{1,0:T(8,128)S(1)}, f32[64,1536]{1,0:T(8,128)S(1)}, u32[]{:S(2)}, u32[]{:S(2)}) collective-permute-start(f32[64,1536]{1,0:T(8,128)S(1)} %pad_maximum_fusion.8), channel_id=1, source_target_pairs={{0,224},{32,0},{64,32},{96,64},{128,96},{160,128},{192,160},{224,1... | collective-permute-start | bytes 1179656 | tf_op jit(solution)/shard_map/ppermute | solution.py:81
  69.3 6.6 %collective-permute-done.7 = f32[64,1536]{1,0:T(8,128)S(1)} collective-permute-done((f32[64,1536]{1,0:T(8,128)S(1)}, f32[64,1536]{1,0:T(8,128)S(1)}, u32[]{:S(2)}, u32[]{:S(2)}) %collective-permute-start.7) | collective-permute-done | bytes 393248 | tf_op jit(solution)/shard_map/ppermute | solution.py:81
  76.6 3.4 %collective-permute-start.8 = (f32[64,768]{1,0:T(8,128)}, f32[64,768]{1,0:T(8,128)S(1)}, u32[]{:S(2)}, u32[]{:S(2)}) collective-permute-start(f32[64,768]{1,0:T(8,128)} %slice_add_fusion), channel_id=1, source_target_pairs={{0,224},{32,0},{64,32},{96,64},{128,96},{160,128},{192,160},{224,1... | collective-permute-start | bytes 589832 | tf_op jit(solution)/shard_map/ppermute | solution.py:79
  80.8 2.1 %collective-permute-done.8 = f32[64,768]{1,0:T(8,128)S(1)} collective-permute-done((f32[64,768]{1,0:T(8,128)}, f32[64,768]{1,0:T(8,128)S(1)}, u32[]{:S(2)}, u32[]{:S(2)}) %collective-permute-start.8) | collective-permute-done | bytes 196640 | tf_op jit(solution)/shard_map/ppermute | solution.py:79
  83.0 3.8 %collective-permute-done.4 = f32[64,768]{1,0:T(8,128)S(1)} collective-permute-done((f32[64,768]{1,0:T(8,128)}, f32[64,768]{1,0:T(8,128)S(1)}, u32[]{:S(2)}, u32[]{:S(2)}) %collective-permute-start.4) | collective-permute-done | bytes 196640 | tf_op jit(solution)/shard_map/ppermute | solution.py:79
  90.2 3.0 %collective-permute-done.9 = bf16[64,1536]{1,0:T(8,128)(2,1)S(1)} collective-permute-done((bf16[64,1536]{1,0:T(8,128)(2,1)S(1)}, bf16[64,1536]{1,0:T(8,128)(2,1)S(1)}, u32[]{:S(2)}, u32[]{:S(2)}) %collective-permute-start.9) | collective-permute-done | bytes 196640 | tf_op jit(solution)/shard_map/ppermute | solution.py:128
  95.0 5.1 %collective-permute-done.10 = bf16[64,1536]{1,0:T(8,128)(2,1)S(1)} collective-permute-done((bf16[64,1536]{1,0:T(8,128)(2,1)S(1)}, bf16[64,1536]{1,0:T(8,128)(2,1)S(1)}, u32[]{:S(2)}, u32[]{:S(2)}) %collective-permute-start.10) | collective-permute-done | bytes 196640 | tf_op jit(solution)/shard_map/ppermute | solution.py:128
  101.8 7.2 %collective-permute-done.14 = bf16[64,1536]{1,0:T(8,128)(2,1)S(1)} collective-permute-done((bf16[64,1536]{1,0:T(8,128)(2,1)S(1)}, bf16[64,1536]{1,0:T(8,128)(2,1)S(1)}, u32[]{:S(2)}, u32[]{:S(2)}) %collective-permute-start.14) | collective-permute-done | bytes 196640 | tf_op jit(solution)/shard_map/ppermute | solution.py:127
  109.1 2.7 %collective-permute-start.16 = (bf16[64,768]{1,0:T(8,128)(2,1)S(1)}, bf16[64,768]{1,0:T(8,128)(2,1)S(1)}, u32[]{:S(2)}, u32[]{:S(2)}) collective-permute-start(bf16[64,768]{1,0:T(8,128)(2,1)S(1)} %slice.215), channel_id=1, source_target_pairs={{0,224},{32,0},{64,32},{96,64},{128,96},{160,128},{192,160},{224,1... | collective-permute-start | bytes 294920 | tf_op jit(solution)/shard_map/ppermute | solution.py:135
  111.9 2.5 %collective-permute-done.15 = bf16[64,768]{1,0:T(8,128)(2,1)S(1)} collective-permute-done((bf16[64,768]{1,0:T(8,128)(2,1)S(1)}, bf16[64,768]{1,0:T(8,128)(2,1)S(1)}, u32[]{:S(2)}, u32[]{:S(2)}) %collective-permute-start.15) | collective-permute-done | bytes 98336 | tf_op jit(solution)/shard_map/ppermute | solution.py:134
  119.7 8.2 %collective-permute-start.17 = (f32[16,16,2048]{2,1,0:T(8,128)S(1)}, f32[16,16,2048]{2,1,0:T(8,128)S(1)}, u32[]{:S(2)}, u32[]{:S(2)}) collective-permute-start(f32[16,16,2048]{2,1,0:T(8,128)S(1)} %bitcast.91), channel_id=1, source_target_pairs={{0,1},{1,0},{2,3},{3,2},{4,5},{5,4},{6,7},{7,6},{8,9},{9,8},{10,11... | collective-permute-start | bytes 6291464 | tf_op jit(solution)/shard_map/ppermute | solution.py:164
  127.9 3.8 %collective-permute-done.17 = f32[16,16,2048]{2,1,0:T(8,128)S(1)} collective-permute-done((f32[16,16,2048]{2,1,0:T(8,128)S(1)}, f32[16,16,2048]{2,1,0:T(8,128)S(1)}, u32[]{:S(2)}, u32[]{:S(2)}) %collective-permute-start.17) | collective-permute-done | bytes 2097184 | tf_op jit(solution)/shard_map/ppermute | solution.py:164
  133.3 3.9 %all-to-all-start.1 = ((f32[16,16,2048]{2,1,0:T(8,128)}), f32[16,16,2048]{2,1,0:T(8,128)S(1)}, u32[]{:S(2)}, u32[]{:S(2)}) async-start(f32[16,16,2048]{2,1,0:T(8,128)} %bitcast_add_fusion), calls=%async_computation.1 | async-start | bytes 4194304 | tf_op jit(solution)/shard_map/all_to_all | solution.py:165
  138.7 3.4 %convolution_select_fusion.1 = f32[1024,512]{1,0:T(8,128)} fusion(pred[1024,512]{1,0:T(32,128)(4,1)S(1)} %copy.20, bf16[512,2048]{1,0:T(8,128)(2,1)} %bitcast.82, bf16[512,1536]{1,0:T(8,128)(2,1)S(1)} %bitcast.76), kind=kOutput, calls=%fused_computation.5 | convolution fusion | flops 537395200 | bytes 4194304 | tf_op jit(solution)/shard_map/dot_general | solution.py:34
  142.1 2.1 %convolution_select_fusion.2 = f32[1024,512]{1,0:T(8,128)} fusion(pred[1024,512]{1,0:T(32,128)(4,1)S(1)} %copy.19, bf16[512,2048]{1,0:T(8,128)(2,1)S(1)} %bitcast.83, bf16[512,1536]{1,0:T(8,128)(2,1)S(1)} %bitcast.77), kind=kOutput, calls=%fused_computation.6 | convolution fusion | flops 537395200 | bytes 4194304 | tf_op jit(solution)/shard_map/dot_general | solution.py:34
  144.2 2.0 %convolution_select_fusion = f32[512,1024]{1,0:T(8,128)} fusion(pred[512,1024]{1,0:T(8,128)(4,1)S(1)} %bitcast.94, bf16[512,2048]{1,0:T(8,128)(2,1)S(1)} %bitcast.84, bf16[512,1536]{1,0:T(8,128)(2,1)S(1)} %bitcast.78), kind=kOutput, calls=%fused_computation.4 | convolution fusion | flops 537395200 | bytes 4194304 | tf_op jit(solution)/shard_map/dot_general | solution.py:34
  146.3 23.8 %all-to-all-done.1 = f32[16,16,2048]{2,1,0:T(8,128)S(1)} async-done(((f32[16,16,2048]{2,1,0:T(8,128)}), f32[16,16,2048]{2,1,0:T(8,128)S(1)}, u32[]{:S(2)}, u32[]{:S(2)}) %all-to-all-start.1) | async-done | bytes 2097184 | tf_op jit(solution)/shard_map/all_to_all | solution.py:165
  (120 shorter events, 29.8 us)
Async XLA Ops:
  0.6 26.5 %slice-start = ((s32[2048]{0:T(1024)}), s32[1024]{0:T(1024)S(1)}, s32[]{:S(2)}) async-start(s32[2048]{0:T(1024)} %param.13), calls=%async_computation.2 | async-start | bytes 8192 | tf_op jit(solution)/shard_map/slice | solution.py:15
  0.6 26.5 %slice-start.1 = ((s32[2048]{0:T(1024)}), s32[1024]{0:T(1024)S(1)}, s32[]{:S(2)}) async-start(s32[2048]{0:T(1024)} %param.14), calls=%async_computation.3 | async-start | bytes 8192 | tf_op jit(solution)/shard_map/slice | solution.py:15
  25.0 9.1 %collective-permute-start = (bf16[16,16,2048]{2,1,0:T(8,128)(2,1)S(1)}, bf16[16,16,2048]{2,1,0:T(8,128)(2,1)}, u32[]{:S(2)}, u32[]{:S(2)}) collective-permute-start(bf16[16,16,2048]{2,1,0:T(8,128)(2,1)S(1)} %all_to_all.10), channel_id=1, source_target_pairs={{0,1},{1,0},{2,3},{3,2},{4,5},{5,4},{6,7},{7,6},{8,9},{9,8},{10,11... | collective-permute-start | bytes 3145736 | tf_op jit(solution)/shard_map/ppermute | solution.py:152
  29.5 3.0 %slice-start.2 = ((s32[2048]{0:T(1024)}), s32[1024]{0:T(1024)S(1)}, s32[]{:S(2)}) async-start(s32[2048]{0:T(1024)} %param.15), calls=%async_computation.4 | async-start | bytes 8192 | tf_op jit(solution)/shard_map/slice | solution.py:15
  40.3 14.1 %collective-permute-start.5 = (f32[64,1536]{1,0:T(8,128)S(1)}, f32[64,1536]{1,0:T(8,128)S(1)}, u32[]{:S(2)}, u32[]{:S(2)}) collective-permute-start(f32[64,1536]{1,0:T(8,128)S(1)} %pad_maximum_fusion.6), channel_id=1, source_target_pairs={{0,224},{32,0},{64,32},{96,64},{128,96},{160,128},{192,160},{224,1... | collective-permute-start | bytes 1179656 | tf_op jit(solution)/shard_map/ppermute | solution.py:81
  46.0 12.0 %collective-permute-start.1 = (f32[64,1536]{1,0:T(8,128)S(1)}, f32[64,1536]{1,0:T(8,128)S(1)}, u32[]{:S(2)}, u32[]{:S(2)}) collective-permute-start(f32[64,1536]{1,0:T(8,128)S(1)} %pad_maximum_fusion.3), channel_id=1, source_target_pairs={{0,32},{32,64},{64,96},{96,128},{128,160},{160,192},{192,224},{224... | collective-permute-start | bytes 1179656 | tf_op jit(solution)/shard_map/ppermute | solution.py:81
  54.5 11.1 %collective-permute-start.6 = (f32[64,1536]{1,0:T(8,128)S(1)}, f32[64,1536]{1,0:T(8,128)S(1)}, u32[]{:S(2)}, u32[]{:S(2)}) collective-permute-start(f32[64,1536]{1,0:T(8,128)S(1)} %pad_maximum_fusion.7), channel_id=1, source_target_pairs={{0,224},{32,0},{64,32},{96,64},{128,96},{160,128},{192,160},{224,1... | collective-permute-start | bytes 1179656 | tf_op jit(solution)/shard_map/ppermute | solution.py:81
  58.1 11.1 %collective-permute-start.2 = (f32[64,1536]{1,0:T(8,128)S(1)}, f32[64,1536]{1,0:T(8,128)S(1)}, u32[]{:S(2)}, u32[]{:S(2)}) collective-permute-start(f32[64,1536]{1,0:T(8,128)S(1)} %pad_maximum_fusion.4), channel_id=1, source_target_pairs={{0,32},{32,64},{64,96},{96,128},{128,160},{160,192},{192,224},{224... | collective-permute-start | bytes 1179656 | tf_op jit(solution)/shard_map/ppermute | solution.py:81
  65.7 10.2 %collective-permute-start.7 = (f32[64,1536]{1,0:T(8,128)S(1)}, f32[64,1536]{1,0:T(8,128)S(1)}, u32[]{:S(2)}, u32[]{:S(2)}) collective-permute-start(f32[64,1536]{1,0:T(8,128)S(1)} %pad_maximum_fusion.8), channel_id=1, source_target_pairs={{0,224},{32,0},{64,32},{96,64},{128,96},{160,128},{192,160},{224,1... | collective-permute-start | bytes 1179656 | tf_op jit(solution)/shard_map/ppermute | solution.py:81
  69.2 10.8 %collective-permute-start.3 = (f32[64,1536]{1,0:T(8,128)S(1)}, f32[64,1536]{1,0:T(8,128)S(1)}, u32[]{:S(2)}, u32[]{:S(2)}) collective-permute-start(f32[64,1536]{1,0:T(8,128)S(1)} %pad_maximum_fusion.5), channel_id=1, source_target_pairs={{0,32},{32,64},{64,96},{96,128},{128,160},{160,192},{192,224},{224... | collective-permute-start | bytes 1179656 | tf_op jit(solution)/shard_map/ppermute | solution.py:81
  76.6 6.3 %collective-permute-start.8 = (f32[64,768]{1,0:T(8,128)}, f32[64,768]{1,0:T(8,128)S(1)}, u32[]{:S(2)}, u32[]{:S(2)}) collective-permute-start(f32[64,768]{1,0:T(8,128)} %slice_add_fusion), channel_id=1, source_target_pairs={{0,224},{32,0},{64,32},{96,64},{128,96},{160,128},{192,160},{224,1... | collective-permute-start | bytes 589832 | tf_op jit(solution)/shard_map/ppermute | solution.py:79
  80.8 5.9 %collective-permute-start.4 = (f32[64,768]{1,0:T(8,128)}, f32[64,768]{1,0:T(8,128)S(1)}, u32[]{:S(2)}, u32[]{:S(2)}) collective-permute-start(f32[64,768]{1,0:T(8,128)} %slice_add_fusion.7), channel_id=1, source_target_pairs={{0,32},{32,64},{64,96},{96,128},{128,160},{160,192},{192,224},{224... | collective-permute-start | bytes 589832 | tf_op jit(solution)/shard_map/ppermute | solution.py:79
  88.7 4.6 %collective-permute-start.9 = (bf16[64,1536]{1,0:T(8,128)(2,1)S(1)}, bf16[64,1536]{1,0:T(8,128)(2,1)S(1)}, u32[]{:S(2)}, u32[]{:S(2)}) collective-permute-start(bf16[64,1536]{1,0:T(8,128)(2,1)S(1)} %pad_maximum_fusion.9), channel_id=1, source_target_pairs={{0,224},{32,0},{64,32},{96,64},{128,96},{160,128},{192,160},{224,1... | collective-permute-start | bytes 589832 | tf_op jit(solution)/shard_map/ppermute | solution.py:128
  88.7 5.8 %collective-permute-start.12 = (bf16[64,1536]{1,0:T(8,128)(2,1)S(1)}, bf16[64,1536]{1,0:T(8,128)(2,1)S(1)}, u32[]{:S(2)}, u32[]{:S(2)}) collective-permute-start(bf16[64,1536]{1,0:T(8,128)(2,1)S(1)} %pad_maximum_fusion.9), channel_id=1, source_target_pairs={{0,32},{32,64},{64,96},{96,128},{128,160},{160,192},{192,224},{224... | collective-permute-start | bytes 589832 | tf_op jit(solution)/shard_map/ppermute | solution.py:127
  93.3 6.9 %collective-permute-start.10 = (bf16[64,1536]{1,0:T(8,128)(2,1)S(1)}, bf16[64,1536]{1,0:T(8,128)(2,1)S(1)}, u32[]{:S(2)}, u32[]{:S(2)}) collective-permute-start(bf16[64,1536]{1,0:T(8,128)(2,1)S(1)} %collective-permute-done.9), channel_id=1, source_target_pairs={{0,224},{32,0},{64,32},{96,64},{128,96},{160,128},{192,160},{224,1... | collective-permute-start | bytes 589832 | tf_op jit(solution)/shard_map/ppermute | solution.py:128
  94.6 6.6 %collective-permute-start.13 = (bf16[64,1536]{1,0:T(8,128)(2,1)S(1)}, bf16[64,1536]{1,0:T(8,128)(2,1)S(1)}, u32[]{:S(2)}, u32[]{:S(2)}) collective-permute-start(bf16[64,1536]{1,0:T(8,128)(2,1)S(1)} %collective-permute-done.12), channel_id=1, source_target_pairs={{0,32},{32,64},{64,96},{96,128},{128,160},{160,192},{192,224},{224... | collective-permute-start | bytes 589832 | tf_op jit(solution)/shard_map/ppermute | solution.py:127
  100.1 9.0 %collective-permute-start.11 = (bf16[64,1536]{1,0:T(8,128)(2,1)S(1)}, bf16[64,1536]{1,0:T(8,128)(2,1)S(1)}, u32[]{:S(2)}, u32[]{:S(2)}) collective-permute-start(bf16[64,1536]{1,0:T(8,128)(2,1)S(1)} %collective-permute-done.10), channel_id=1, source_target_pairs={{0,224},{32,0},{64,32},{96,64},{128,96},{160,128},{192,160},{224,1... | collective-permute-start | bytes 589832 | tf_op jit(solution)/shard_map/ppermute | solution.py:128
  101.1 7.9 %collective-permute-start.14 = (bf16[64,1536]{1,0:T(8,128)(2,1)S(1)}, bf16[64,1536]{1,0:T(8,128)(2,1)S(1)}, u32[]{:S(2)}, u32[]{:S(2)}) collective-permute-start(bf16[64,1536]{1,0:T(8,128)(2,1)S(1)} %collective-permute-done.13), channel_id=1, source_target_pairs={{0,32},{32,64},{64,96},{96,128},{128,160},{160,192},{192,224},{224... | collective-permute-start | bytes 589832 | tf_op jit(solution)/shard_map/ppermute | solution.py:127
  109.0 5.3 %collective-permute-start.15 = (bf16[64,768]{1,0:T(8,128)(2,1)S(1)}, bf16[64,768]{1,0:T(8,128)(2,1)S(1)}, u32[]{:S(2)}, u32[]{:S(2)}) collective-permute-start(bf16[64,768]{1,0:T(8,128)(2,1)S(1)} %slice.214), channel_id=1, source_target_pairs={{0,32},{32,64},{64,96},{96,128},{128,160},{160,192},{192,224},{224... | collective-permute-start | bytes 294920 | tf_op jit(solution)/shard_map/ppermute | solution.py:134
  109.1 5.2 %collective-permute-start.16 = (bf16[64,768]{1,0:T(8,128)(2,1)S(1)}, bf16[64,768]{1,0:T(8,128)(2,1)S(1)}, u32[]{:S(2)}, u32[]{:S(2)}) collective-permute-start(bf16[64,768]{1,0:T(8,128)(2,1)S(1)} %slice.215), channel_id=1, source_target_pairs={{0,224},{32,0},{64,32},{96,64},{128,96},{160,128},{192,160},{224,1... | collective-permute-start | bytes 294920 | tf_op jit(solution)/shard_map/ppermute | solution.py:135
  114.8 3.4 %copy-start = (bf16[8,64,1536]{2,1,0:T(8,128)(2,1)}, bf16[8,64,1536]{2,1,0:T(8,128)(2,1)S(1)}, u32[]{:S(2)}) copy-start(bf16[8,64,1536]{2,1,0:T(8,128)(2,1)S(1)} %constant_dynamic-slice_fusion) | copy-start | bytes 4718596
  119.7 12.0 %collective-permute-start.17 = (f32[16,16,2048]{2,1,0:T(8,128)S(1)}, f32[16,16,2048]{2,1,0:T(8,128)S(1)}, u32[]{:S(2)}, u32[]{:S(2)}) collective-permute-start(f32[16,16,2048]{2,1,0:T(8,128)S(1)} %bitcast.91), channel_id=1, source_target_pairs={{0,1},{1,0},{2,3},{3,2},{4,5},{5,4},{6,7},{7,6},{8,9},{9,8},{10,11... | collective-permute-start | bytes 6291464 | tf_op jit(solution)/shard_map/ppermute | solution.py:164
  133.3 36.7 %all-to-all-start.1 = ((f32[16,16,2048]{2,1,0:T(8,128)}), f32[16,16,2048]{2,1,0:T(8,128)S(1)}, u32[]{:S(2)}, u32[]{:S(2)}) async-start(f32[16,16,2048]{2,1,0:T(8,128)} %bitcast_add_fusion), calls=%async_computation.1 | async-start | bytes 4194304 | tf_op jit(solution)/shard_map/all_to_all | solution.py:165
  138.7 3.4 %copy-start.3 = (bf16[8,2,2,16,2048]{4,3,2,1,0:T(8,128)(2,1)S(1)}, bf16[8,2,2,16,2048]{4,3,2,1,0:T(8,128)(2,1)}, u32[]{:S(2)}) copy-start(bf16[8,2,2,16,2048]{4,3,2,1,0:T(8,128)(2,1)} %copy-done.2) | copy-start | bytes 6291460
  (11 other events, 16.0 us)

commit v10 on v9

--- a/solution.py
+++ b/solution.py
@@ -83,35 +83,32 @@
     return [moved[:, edges[k] : edges[k + 1]] for k in range(len(values))]
 
 
-def relay_scatter_sum(parts, axis_name):
+def relay_scatter_sum(chains, axis_name):
     count = lax.axis_size(axis_name)
     here = lax.axis_index(axis_name)
-    pieces = parts.reshape((count, parts.shape[0] // count) + parts.shape[1:])
-    half = parts.shape[1] // 2
-    spans = (slice(0, half), slice(half, parts.shape[1]))
-
-    def piece_for(offset, span):
-        return lax.dynamic_index_in_dim(pieces, (here + offset) % count, 0, keepdims=False)[:, span]
+    split = [
+        (part.reshape((count, part.shape[0] // count) + part.shape[1:]), reach)
+        for part, reach in chains
+    ]
+
+    def piece_for(c, offset):
+        return lax.dynamic_index_in_dim(split[c][0], (here + offset) % count, 0, keepdims=False)
 
     forward = [(i, (i + 1) % count) for i in range(count)]
     backward = [(i, (i - 1) % count) for i in range(count)]
-    longer = count // 2
-    shorter = count - 1 - longer
-    reach = ((longer, shorter), (shorter, longer))
-    ahead = [piece_for(r[0], span) for r, span in zip(reach, spans)]
-    behind = [piece_for(-r[1], span) for r, span in zip(reach, spans)]
-    for step in range(1, longer + 1):
+    reach = [r for _, r in split]
+    ahead = [piece_for(c, r[0]) for c, r in enumerate(reach)]
+    behind = [piece_for(c, -r[1]) for c, r in enumerate(reach)]
+    for step in range(1, max(max(r) for r in reach) + 1):
         going = [c for c, r in enumerate(reach) if step <= r[0]]
         coming = [c for c, r in enumerate(reach) if step <= r[1]]
         sent_ahead = joint_permute([ahead[c] for c in going], axis_name, forward)
         sent_behind = joint_permute([behind[c] for c in coming], axis_name, backward)
         for c, value in zip(going, sent_ahead):
-            ahead[c] = value + piece_for(reach[c][0] - step, spans[c]) if step < reach[c][0] else value
+            ahead[c] = value + piece_for(c, reach[c][0] - step) if step < reach[c][0] else value
         for c, value in zip(coming, sent_behind):
-            behind[c] = value + piece_for(step - reach[c][1], spans[c]) if step < reach[c][1] else value
-    return jnp.concatenate(
-        [piece_for(0, span) + ahead[c] + behind[c] for c, span in enumerate(spans)], axis=1
-    )
+            behind[c] = value + piece_for(c, step - reach[c][1]) if step < reach[c][1] else value
+    return [piece_for(c, 0) + ahead[c] + behind[c] for c in range(len(split))]
 
 
 def relay_gather(block, axis_name):
@@ -184,11 +181,23 @@
     up_term = apply_blocks(tokens_all, w_up, keep_up, "forward")
     hidden_term = apply_blocks(cotangent_all, w_down, keep_down, "transposed")
     row_major = Layout(major_to_minor=(0, 1))
-    partials = [with_layout_constraint(t, row_major) for t in (gate_term, up_term, hidden_term)]
-    sums = relay_scatter_sum(jnp.concatenate(partials, axis=1), "row")
-    gate = sums[:, :hidden_here]
-    up = sums[:, hidden_here : 2 * hidden_here]
-    hidden_grad = sums[:, 2 * hidden_here :]
+    gate_term, up_term, hidden_term = (
+        with_layout_constraint(t, row_major) for t in (gate_term, up_term, hidden_term)
+    )
+    groups_row = lax.axis_size("row")
+    longer = groups_row // 2
+    shorter = groups_row - 1 - longer
+    half_up = hidden_here // 2
+    gate, up_first, up_second, hidden_grad = relay_scatter_sum(
+        [
+            (gate_term, (longer, shorter)),
+            (up_term[:, :half_up], (longer, shorter)),
+            (up_term[:, half_up:], (shorter, longer)),
+            (hidden_term, (shorter, longer)),
+        ],
+        "row",
+    )
+    up = jnp.concatenate([up_first, up_second], axis=1)
     sigmoid_gate = jax.nn.sigmoid(gate)
     activation = gate * sigmoid_gate
     hidden = (activation * up).astype(jnp.bfloat16)

time: 171 us -> 209 us (1.22)
  waiting for transfers between devices: 74.1 us -> 93 us
  other arithmetic: 8.32 us -> 26.6 us
    ppermute x6 -> x8, waiting for transfers between devices: 22.3 us -> 48.8 us  [joint_permute(): moved = lax.ppermute(jnp.concatenate(values, axis=1), axis_name, pairs)]
    add x7 -> x11, other arithmetic: 2.74 us -> 12.9 us  [the longest x8 10.1 us: relay_scatter_sum(): value + piece_for(c, reach[c][0] - step)]
    ppermute x3, starting transfers between devices: 1.94 us -> 9.72 us  [relay_gather(): carry_behind = lax.ppermute(carry_behind, axis_name, backward)]
    concatenate x6 -> x8, other arithmetic: 0.17 us -> 6.47 us  [joint_permute(): moved = lax.ppermute(jnp.concatenate(values, axis=1), axis_name, pairs)]
    ppermute x2 -> x0, waiting for transfers between devices: 5.94 us -> none  [joint_permute(): return [lax.ppermute(values[0], axis_name, pairs)]]
    ppermute x2 -> x0, starting transfers between devices: 3.41 us -> none  [joint_permute(): return [lax.ppermute(values[0], axis_name, pairs)]]
    ppermute x6 -> x8, starting transfers between devices: 12.9 us -> 9.51 us  [joint_permute(): moved = lax.ppermute(jnp.concatenate(values, axis=1), axis_name, pairs)]
    ppermute x3, starting transfers between devices: 2.57 us -> 0.01 us  [relay_gather(): carry_ahead = lax.ppermute(carry_ahead, axis_name, forward)]
  transfers between devices with their start and end apart: 19 -> 19, of which waited for: 13 -> 14; matrix products, arithmetic and copies ran while one was open for 10% -> 9% of each run, Pallas kernels for 0% -> 0%
where the time goes in v10:
time: 209 us; the launch traced here: 207 us
  waiting for transfers between devices  93 us (44%)
  starting transfers between devices  37.4 us (18%)
  other arithmetic  26.6 us (13%)
  blocking collectives  23.4 us (11%)
  local copies, waits for them, and re-layouts  13.8 us (7%)
  matrix products  12 us (6%)
    ppermute x8, waiting for transfers between devices, joint_permute(): moved = lax.ppermute(jnp.concatenate(values, axis=1), axis_name, pairs)  48.8 us
    all_to_all x1, waiting for transfers between devices, col_scatter_sum(): return lax.all_to_all(pair_sum, 'chip', 0, 0, tiled=True).sum(axis=0)  23.8 us
    all_to_all x1, blocking collectives, col_gather(): mine = lax.all_to_all(spread, 'chip', 0, 0, tiled=True)  23.4 us
    unnamed x44, local copies, waits for them, and re-layouts  10.2 us
    add x8, other arithmetic, relay_scatter_sum(): value + piece_for(c, reach[c][0] - step)  10.1 us
    ppermute x3, starting transfers between devices, relay_gather(): carry_behind = lax.ppermute(carry_behind, axis_name, backward)  9.72 us
    ppermute x8, starting transfers between devices, joint_permute(): moved = lax.ppermute(jnp.concatenate(values, axis=1), axis_name, pairs)  9.51 us
    ppermute x1, starting transfers between devices, col_scatter_sum(): pair_sum = mine + lax.ppermute(other, 'core', [(0, 1), (1, 0)])  9.39 us
  transfers between devices with their start and end apart: 19, of which 14 were waited for; matrix products, arithmetic and copies ran while one was open for 9% of the time, Pallas kernels for 0%

profile of v10, /device:TPU:1, one launch (start us, length us, event | category | flops | bytes accessed | tf_op | source)
XLA Modules:
  0.0 207.4 jit_solution(4850771595952502698)
XLA Ops:
  1.6 23.4 %all_to_all.10 = bf16[16,16,2048]{2,1,0:T(8,128)(2,1)S(1)} all-to-all(bf16[16,16,2048]{2,1,0:T(8,128)(2,1)S(1)} %broadcast_in_dim.8), channel_id=1, replica_groups=mesh['row'=8,'chip'=16,'core'=2] {'chip'}, dimensions={0} | all-to-all | bytes 2097152 | tf_op jit(solution)/shard_map/all_to_all | solution.py:148
  25.0 2.1 collective-permute-start
  30.1 2.3 %copy.17 = bf16[1024,512]{0,1:T(8,128)(2,1)} copy(bf16[1024,512]{1,0:T(8,128)(2,1)} %param.10) | data formatting | bytes 2097152 | tf_op args[2]
  40.7 5.7 %collective-permute-start.5 = (f32[64,1536]{1,0:T(8,128)S(1)}, f32[64,1536]{1,0:T(8,128)}, u32[]{:S(2)}, u32[]{:S(2)}) collective-permute-start(f32[64,1536]{1,0:T(8,128)S(1)} %pad_maximum_fusion.5), channel_id=1, source_target_pairs={{0,224},{32,0},{64,32},{96,64},{128,96},{160,128},{192,160},{224,1... | collective-permute-start | bytes 1179656 | tf_op jit(solution)/shard_map/ppermute | solution.py:81
  47.1 7.7 %collective-permute-done.5 = f32[64,1536]{1,0:T(8,128)} collective-permute-done((f32[64,1536]{1,0:T(8,128)S(1)}, f32[64,1536]{1,0:T(8,128)}, u32[]{:S(2)}, u32[]{:S(2)}) %collective-permute-start.5) | collective-permute-done | bytes 393248 | tf_op jit(solution)/shard_map/ppermute | solution.py:81
  54.8 4.2 %collective-permute-done.1 = f32[64,1536]{1,0:T(8,128)} collective-permute-done((f32[64,1536]{1,0:T(8,128)}, f32[64,1536]{1,0:T(8,128)}, u32[]{:S(2)}, u32[]{:S(2)}) %collective-permute-start.1) | collective-permute-done | bytes 393248 | tf_op jit(solution)/shard_map/ppermute | solution.py:81
  62.1 11.1 %collective-permute-done.2 = f32[64,1536]{1,0:T(8,128)} collective-permute-done((f32[64,1536]{1,0:T(8,128)}, f32[64,1536]{1,0:T(8,128)}, u32[]{:S(2)}, u32[]{:S(2)}) %collective-permute-start.2) | collective-permute-done | bytes 393248 | tf_op jit(solution)/shard_map/ppermute | solution.py:81
  76.5 9.0 %collective-permute-done.6 = f32[64,1536]{1,0:T(8,128)} collective-permute-done((f32[64,1536]{1,0:T(8,128)}, f32[64,1536]{1,0:T(8,128)}, u32[]{:S(2)}, u32[]{:S(2)}) %collective-permute-start.6) | collective-permute-done | bytes 393248 | tf_op jit(solution)/shard_map/ppermute | solution.py:81
  89.8 9.4 %collective-permute-done.3 = f32[64,1536]{1,0:T(8,128)} collective-permute-done((f32[64,1536]{1,0:T(8,128)}, f32[64,1536]{1,0:T(8,128)}, u32[]{:S(2)}, u32[]{:S(2)}) %collective-permute-start.3) | collective-permute-done | bytes 393248 | tf_op jit(solution)/shard_map/ppermute | solution.py:81
  105.8 4.9 %collective-permute-done.7 = f32[64,1536]{1,0:T(8,128)} collective-permute-done((f32[64,1536]{1,0:T(8,128)}, f32[64,1536]{1,0:T(8,128)}, u32[]{:S(2)}, u32[]{:S(2)}) %collective-permute-start.7) | collective-permute-done | bytes 393248 | tf_op jit(solution)/shard_map/ppermute | solution.py:81
  112.6 2.3 %collective-permute-start.8 = (f32[64,768]{1,0:T(8,128)S(1)}, f32[64,768]{1,0:T(8,128)S(1)}, u32[]{:S(2)}, u32[]{:S(2)}) collective-permute-start(f32[64,768]{1,0:T(8,128)S(1)} %pad_maximum_fusion.9), channel_id=1, source_target_pairs={{0,224},{32,0},{64,32},{96,64},{128,96},{160,128},{192,160},{224,1... | collective-permute-start | bytes 589832 | tf_op jit(solution)/shard_map/ppermute | solution.py:81
  114.9 2.6 %collective-permute-done.8 = f32[64,768]{1,0:T(8,128)S(1)} collective-permute-done((f32[64,768]{1,0:T(8,128)S(1)}, f32[64,768]{1,0:T(8,128)S(1)}, u32[]{:S(2)}, u32[]{:S(2)}) %collective-permute-start.8) | collective-permute-done | bytes 196640 | tf_op jit(solution)/shard_map/ppermute | solution.py:81
  120.7 3.2 %collective-permute-start.9 = (bf16[64,1536]{1,0:T(8,128)(2,1)S(1)}, bf16[64,1536]{1,0:T(8,128)(2,1)S(1)}, u32[]{:S(2)}, u32[]{:S(2)}) collective-permute-start(bf16[64,1536]{1,0:T(8,128)(2,1)S(1)} %pad_maximum_fusion.10), channel_id=1, source_target_pairs={{0,224},{32,0},{64,32},{96,64},{128,96},{160,128},{192,160},{224,1... | collective-permute-start | bytes 589832 | tf_op jit(solution)/shard_map/ppermute | solution.py:125
  123.9 2.6 %collective-permute-done.9 = bf16[64,1536]{1,0:T(8,128)(2,1)S(1)} collective-permute-done((bf16[64,1536]{1,0:T(8,128)(2,1)S(1)}, bf16[64,1536]{1,0:T(8,128)(2,1)S(1)}, u32[]{:S(2)}, u32[]{:S(2)}) %collective-permute-start.9) | collective-permute-done | bytes 196640 | tf_op jit(solution)/shard_map/ppermute | solution.py:125
  126.5 3.1 %collective-permute-start.10 = (bf16[64,1536]{1,0:T(8,128)(2,1)S(1)}, bf16[64,1536]{1,0:T(8,128)(2,1)S(1)}, u32[]{:S(2)}, u32[]{:S(2)}) collective-permute-start(bf16[64,1536]{1,0:T(8,128)(2,1)S(1)} %collective-permute-done.9), channel_id=1, source_target_pairs={{0,224},{32,0},{64,32},{96,64},{128,96},{160,128},{192,160},{224,1... | collective-permute-start | bytes 589832 | tf_op jit(solution)/shard_map/ppermute | solution.py:125
  129.6 4.5 %collective-permute-done.10 = bf16[64,1536]{1,0:T(8,128)(2,1)S(1)} collective-permute-done((bf16[64,1536]{1,0:T(8,128)(2,1)S(1)}, bf16[64,1536]{1,0:T(8,128)(2,1)S(1)}, u32[]{:S(2)}, u32[]{:S(2)}) %collective-permute-start.10) | collective-permute-done | bytes 196640 | tf_op jit(solution)/shard_map/ppermute | solution.py:125
  134.2 3.4 %collective-permute-start.11 = (bf16[64,1536]{1,0:T(8,128)(2,1)S(1)}, bf16[64,1536]{1,0:T(8,128)(2,1)S(1)}, u32[]{:S(2)}, u32[]{:S(2)}) collective-permute-start(bf16[64,1536]{1,0:T(8,128)(2,1)S(1)} %collective-permute-done.10), channel_id=1, source_target_pairs={{0,224},{32,0},{64,32},{96,64},{128,96},{160,128},{192,160},{224,1... | collective-permute-start | bytes 589832 | tf_op jit(solution)/shard_map/ppermute | solution.py:125
  137.6 6.8 %collective-permute-done.14 = bf16[64,1536]{1,0:T(8,128)(2,1)S(1)} collective-permute-done((bf16[64,1536]{1,0:T(8,128)(2,1)S(1)}, bf16[64,1536]{1,0:T(8,128)(2,1)S(1)}, u32[]{:S(2)}, u32[]{:S(2)}) %collective-permute-start.14) | collective-permute-done | bytes 196640 | tf_op jit(solution)/shard_map/ppermute | solution.py:124
  144.5 2.7 %collective-permute-start.16 = (bf16[64,768]{1,0:T(8,128)(2,1)S(1)}, bf16[64,768]{1,0:T(8,128)(2,1)S(1)}, u32[]{:S(2)}, u32[]{:S(2)}) collective-permute-start(bf16[64,768]{1,0:T(8,128)(2,1)S(1)} %slice.211), channel_id=1, source_target_pairs={{0,224},{32,0},{64,32},{96,64},{128,96},{160,128},{192,160},{224,1... | collective-permute-start | bytes 294920 | tf_op jit(solution)/shard_map/ppermute | solution.py:132
  155.2 9.4 %collective-permute-start.17 = (f32[16,16,2048]{2,1,0:T(8,128)S(1)}, f32[16,16,2048]{2,1,0:T(8,128)S(1)}, u32[]{:S(2)}, u32[]{:S(2)}) collective-permute-start(f32[16,16,2048]{2,1,0:T(8,128)S(1)} %bitcast.151), channel_id=1, source_target_pairs={{0,1},{1,0},{2,3},{3,2},{4,5},{5,4},{6,7},{7,6},{8,9},{9,8},{10,11... | collective-permute-start | bytes 6291464 | tf_op jit(solution)/shard_map/ppermute | solution.py:161
  164.6 3.8 %collective-permute-done.17 = f32[16,16,2048]{2,1,0:T(8,128)S(1)} collective-permute-done((f32[16,16,2048]{2,1,0:T(8,128)S(1)}, f32[16,16,2048]{2,1,0:T(8,128)S(1)}, u32[]{:S(2)}, u32[]{:S(2)}) %collective-permute-start.17) | collective-permute-done | bytes 2097184 | tf_op jit(solution)/shard_map/ppermute | solution.py:161
  170.0 3.9 %all-to-all-start.1 = ((f32[16,16,2048]{2,1,0:T(8,128)}), f32[16,16,2048]{2,1,0:T(8,128)S(1)}, u32[]{:S(2)}, u32[]{:S(2)}) async-start(f32[16,16,2048]{2,1,0:T(8,128)} %bitcast_add_fusion), calls=%async_computation.1 | async-start | bytes 4194304 | tf_op jit(solution)/shard_map/all_to_all | solution.py:162
  175.3 3.4 %convolution_select_fusion.1 = f32[1024,512]{1,0:T(8,128)} fusion(pred[1024,512]{1,0:T(32,128)(4,1)S(1)} %copy.20, bf16[512,2048]{1,0:T(8,128)(2,1)} %bitcast.132, bf16[512,1536]{1,0:T(8,128)(2,1)S(1)} %bitcast.126), kind=kOutput, calls=%fused_computation.4 | convolution fusion | flops 537395200 | bytes 4194304 | tf_op jit(solution)/shard_map/dot_general | solution.py:34
  182.9 23.8 %all-to-all-done.1 = f32[16,16,2048]{2,1,0:T(8,128)S(1)} async-done(((f32[16,16,2048]{2,1,0:T(8,128)}), f32[16,16,2048]{2,1,0:T(8,128)S(1)}, u32[]{:S(2)}, u32[]{:S(2)}) %all-to-all-start.1) | async-done | bytes 2097184 | tf_op jit(solution)/shard_map/all_to_all | solution.py:162
  (129 shorter events, 51.0 us)
Async XLA Ops:
  0.6 26.5 %slice-start = ((s32[2048]{0:T(1024)}), s32[1024]{0:T(1024)S(1)}, s32[]{:S(2)}) async-start(s32[2048]{0:T(1024)} %param.13), calls=%async_computation.2 | async-start | bytes 8192 | tf_op jit(solution)/shard_map/slice | solution.py:15
  0.6 26.5 %slice-start.1 = ((s32[2048]{0:T(1024)}), s32[1024]{0:T(1024)S(1)}, s32[]{:S(2)}) async-start(s32[2048]{0:T(1024)} %param.14), calls=%async_computation.3 | async-start | bytes 8192 | tf_op jit(solution)/shard_map/slice | solution.py:15
  25.0 9.1 %collective-permute-start = (bf16[16,16,2048]{2,1,0:T(8,128)(2,1)S(1)}, bf16[16,16,2048]{2,1,0:T(8,128)(2,1)}, u32[]{:S(2)}, u32[]{:S(2)}) collective-permute-start(bf16[16,16,2048]{2,1,0:T(8,128)(2,1)S(1)} %all_to_all.10), channel_id=1, source_target_pairs={{0,1},{1,0},{2,3},{3,2},{4,5},{5,4},{6,7},{7,6},{8,9},{9,8},{10,11... | collective-permute-start | bytes 3145736 | tf_op jit(solution)/shard_map/ppermute | solution.py:149
  29.5 3.0 %slice-start.2 = ((s32[2048]{0:T(1024)}), s32[1024]{0:T(1024)S(1)}, s32[]{:S(2)}) async-start(s32[2048]{0:T(1024)} %param.15), calls=%async_computation.4 | async-start | bytes 8192 | tf_op jit(solution)/shard_map/slice | solution.py:15
  40.7 14.1 %collective-permute-start.5 = (f32[64,1536]{1,0:T(8,128)S(1)}, f32[64,1536]{1,0:T(8,128)}, u32[]{:S(2)}, u32[]{:S(2)}) collective-permute-start(f32[64,1536]{1,0:T(8,128)S(1)} %pad_maximum_fusion.5), channel_id=1, source_target_pairs={{0,224},{32,0},{64,32},{96,64},{128,96},{160,128},{192,160},{224,1... | collective-permute-start | bytes 1179656 | tf_op jit(solution)/shard_map/ppermute | solution.py:81
  47.1 11.9 %collective-permute-start.1 = (f32[64,1536]{1,0:T(8,128)}, f32[64,1536]{1,0:T(8,128)}, u32[]{:S(2)}, u32[]{:S(2)}) collective-permute-start(f32[64,1536]{1,0:T(8,128)} %pad_maximum_fusion.2), channel_id=1, source_target_pairs={{0,32},{32,64},{64,96},{96,128},{128,160},{160,192},{192,224},{224... | collective-permute-start | bytes 1179656 | tf_op jit(solution)/shard_map/ppermute | solution.py:81
  62.0 11.1 %collective-permute-start.2 = (f32[64,1536]{1,0:T(8,128)}, f32[64,1536]{1,0:T(8,128)}, u32[]{:S(2)}, u32[]{:S(2)}) collective-permute-start(f32[64,1536]{1,0:T(8,128)} %pad_maximum_fusion.3), channel_id=1, source_target_pairs={{0,32},{32,64},{64,96},{96,128},{128,160},{160,192},{192,224},{224... | collective-permute-start | bytes 1179656 | tf_op jit(solution)/shard_map/ppermute | solution.py:81
  76.5 9.0 %collective-permute-start.6 = (f32[64,1536]{1,0:T(8,128)}, f32[64,1536]{1,0:T(8,128)}, u32[]{:S(2)}, u32[]{:S(2)}) collective-permute-start(f32[64,1536]{1,0:T(8,128)} %pad_maximum_fusion.6), channel_id=1, source_target_pairs={{0,224},{32,0},{64,32},{96,64},{128,96},{160,128},{192,160},{224,1... | collective-permute-start | bytes 1179656 | tf_op jit(solution)/shard_map/ppermute | solution.py:81
  89.8 9.4 %collective-permute-start.3 = (f32[64,1536]{1,0:T(8,128)}, f32[64,1536]{1,0:T(8,128)}, u32[]{:S(2)}, u32[]{:S(2)}) collective-permute-start(f32[64,1536]{1,0:T(8,128)} %pad_maximum_fusion.4), channel_id=1, source_target_pairs={{0,32},{32,64},{64,96},{96,128},{128,160},{160,192},{192,224},{224... | collective-permute-start | bytes 1179656 | tf_op jit(solution)/shard_map/ppermute | solution.py:81
  103.4 7.3 %collective-permute-start.7 = (f32[64,1536]{1,0:T(8,128)}, f32[64,1536]{1,0:T(8,128)}, u32[]{:S(2)}, u32[]{:S(2)}) collective-permute-start(f32[64,1536]{1,0:T(8,128)} %pad_maximum_fusion.7), channel_id=1, source_target_pairs={{0,224},{32,0},{64,32},{96,64},{128,96},{160,128},{192,160},{224,1... | collective-permute-start | bytes 1179656 | tf_op jit(solution)/shard_map/ppermute | solution.py:81
  104.8 6.9 %collective-permute-start.4 = (f32[64,768]{1,0:T(8,128)S(1)}, f32[64,768]{1,0:T(8,128)S(1)}, u32[]{:S(2)}, u32[]{:S(2)}) collective-permute-start(f32[64,768]{1,0:T(8,128)S(1)} %pad_maximum_fusion.8), channel_id=1, source_target_pairs={{0,32},{32,64},{64,96},{96,128},{128,160},{160,192},{192,224},{224... | collective-permute-start | bytes 589832 | tf_op jit(solution)/shard_map/ppermute | solution.py:81
  112.6 4.9 %collective-permute-start.8 = (f32[64,768]{1,0:T(8,128)S(1)}, f32[64,768]{1,0:T(8,128)S(1)}, u32[]{:S(2)}, u32[]{:S(2)}) collective-permute-start(f32[64,768]{1,0:T(8,128)S(1)} %pad_maximum_fusion.9), channel_id=1, source_target_pairs={{0,224},{32,0},{64,32},{96,64},{128,96},{160,128},{192,160},{224,1... | collective-permute-start | bytes 589832 | tf_op jit(solution)/shard_map/ppermute | solution.py:81
  120.7 5.8 %collective-permute-start.9 = (bf16[64,1536]{1,0:T(8,128)(2,1)S(1)}, bf16[64,1536]{1,0:T(8,128)(2,1)S(1)}, u32[]{:S(2)}, u32[]{:S(2)}) collective-permute-start(bf16[64,1536]{1,0:T(8,128)(2,1)S(1)} %pad_maximum_fusion.10), channel_id=1, source_target_pairs={{0,224},{32,0},{64,32},{96,64},{128,96},{160,128},{192,160},{224,1... | collective-permute-start | bytes 589832 | tf_op jit(solution)/shard_map/ppermute | solution.py:125
  123.9 5.7 %collective-permute-start.12 = (bf16[64,1536]{1,0:T(8,128)(2,1)S(1)}, bf16[64,1536]{1,0:T(8,128)(2,1)S(1)}, u32[]{:S(2)}, u32[]{:S(2)}) collective-permute-start(bf16[64,1536]{1,0:T(8,128)(2,1)S(1)} %pad_maximum_fusion.10), channel_id=1, source_target_pairs={{0,32},{32,64},{64,96},{96,128},{128,160},{160,192},{192,224},{224... | collective-permute-start | bytes 589832 | tf_op jit(solution)/shard_map/ppermute | solution.py:124
  126.5 7.7 %collective-permute-start.10 = (bf16[64,1536]{1,0:T(8,128)(2,1)S(1)}, bf16[64,1536]{1,0:T(8,128)(2,1)S(1)}, u32[]{:S(2)}, u32[]{:S(2)}) collective-permute-start(bf16[64,1536]{1,0:T(8,128)(2,1)S(1)} %collective-permute-done.9), channel_id=1, source_target_pairs={{0,224},{32,0},{64,32},{96,64},{128,96},{160,128},{192,160},{224,1... | collective-permute-start | bytes 589832 | tf_op jit(solution)/shard_map/ppermute | solution.py:125
  129.6 8.0 %collective-permute-start.13 = (bf16[64,1536]{1,0:T(8,128)(2,1)S(1)}, bf16[64,1536]{1,0:T(8,128)(2,1)S(1)}, u32[]{:S(2)}, u32[]{:S(2)}) collective-permute-start(bf16[64,1536]{1,0:T(8,128)(2,1)S(1)} %collective-permute-done.12), channel_id=1, source_target_pairs={{0,32},{32,64},{64,96},{96,128},{128,160},{160,192},{192,224},{224... | collective-permute-start | bytes 589832 | tf_op jit(solution)/shard_map/ppermute | solution.py:124
  134.2 10.4 %collective-permute-start.11 = (bf16[64,1536]{1,0:T(8,128)(2,1)S(1)}, bf16[64,1536]{1,0:T(8,128)(2,1)S(1)}, u32[]{:S(2)}, u32[]{:S(2)}) collective-permute-start(bf16[64,1536]{1,0:T(8,128)(2,1)S(1)} %collective-permute-done.10), channel_id=1, source_target_pairs={{0,224},{32,0},{64,32},{96,64},{128,96},{160,128},{192,160},{224,1... | collective-permute-start | bytes 589832 | tf_op jit(solution)/shard_map/ppermute | solution.py:125
  137.6 6.8 %collective-permute-start.14 = (bf16[64,1536]{1,0:T(8,128)(2,1)S(1)}, bf16[64,1536]{1,0:T(8,128)(2,1)S(1)}, u32[]{:S(2)}, u32[]{:S(2)}) collective-permute-start(bf16[64,1536]{1,0:T(8,128)(2,1)S(1)} %collective-permute-done.13), channel_id=1, source_target_pairs={{0,32},{32,64},{64,96},{96,128},{128,160},{160,192},{192,224},{224... | collective-permute-start | bytes 589832 | tf_op jit(solution)/shard_map/ppermute | solution.py:124
  144.4 4.8 %collective-permute-start.15 = (bf16[64,768]{1,0:T(8,128)(2,1)S(1)}, bf16[64,768]{1,0:T(8,128)(2,1)S(1)}, u32[]{:S(2)}, u32[]{:S(2)}) collective-permute-start(bf16[64,768]{1,0:T(8,128)(2,1)S(1)} %slice.210), channel_id=1, source_target_pairs={{0,32},{32,64},{64,96},{96,128},{128,160},{160,192},{192,224},{224... | collective-permute-start | bytes 294920 | tf_op jit(solution)/shard_map/ppermute | solution.py:131
  144.5 5.3 %collective-permute-start.16 = (bf16[64,768]{1,0:T(8,128)(2,1)S(1)}, bf16[64,768]{1,0:T(8,128)(2,1)S(1)}, u32[]{:S(2)}, u32[]{:S(2)}) collective-permute-start(bf16[64,768]{1,0:T(8,128)(2,1)S(1)} %slice.211), channel_id=1, source_target_pairs={{0,224},{32,0},{64,32},{96,64},{128,96},{160,128},{192,160},{224,1... | collective-permute-start | bytes 294920 | tf_op jit(solution)/shard_map/ppermute | solution.py:132
  150.3 3.4 %copy-start = (bf16[8,64,1536]{2,1,0:T(8,128)(2,1)}, bf16[8,64,1536]{2,1,0:T(8,128)(2,1)S(1)}, u32[]{:S(2)}) copy-start(bf16[8,64,1536]{2,1,0:T(8,128)(2,1)S(1)} %constant_dynamic-slice_fusion) | copy-start | bytes 4718596
  155.2 13.2 %collective-permute-start.17 = (f32[16,16,2048]{2,1,0:T(8,128)S(1)}, f32[16,16,2048]{2,1,0:T(8,128)S(1)}, u32[]{:S(2)}, u32[]{:S(2)}) collective-permute-start(f32[16,16,2048]{2,1,0:T(8,128)S(1)} %bitcast.151), channel_id=1, source_target_pairs={{0,1},{1,0},{2,3},{3,2},{4,5},{5,4},{6,7},{7,6},{8,9},{9,8},{10,11... | collective-permute-start | bytes 6291464 | tf_op jit(solution)/shard_map/ppermute | solution.py:161
  170.0 36.7 %all-to-all-start.1 = ((f32[16,16,2048]{2,1,0:T(8,128)}), f32[16,16,2048]{2,1,0:T(8,128)S(1)}, u32[]{:S(2)}, u32[]{:S(2)}) async-start(f32[16,16,2048]{2,1,0:T(8,128)} %bitcast_add_fusion), calls=%async_computation.1 | async-start | bytes 4194304 | tf_op jit(solution)/shard_map/all_to_all | solution.py:162
  175.3 3.4 %copy-start.3 = (bf16[8,2,2,16,2048]{4,3,2,1,0:T(8,128)(2,1)S(1)}, bf16[8,2,2,16,2048]{4,3,2,1,0:T(8,128)(2,1)}, u32[]{:S(2)}) copy-start(bf16[8,2,2,16,2048]{4,3,2,1,0:T(8,128)(2,1)} %copy-done.2) | copy-start | bytes 6291460
  (12 other events, 18.2 us)

commit v11 on v9

--- a/solution.py
+++ b/solution.py
@@ -155,13 +155,11 @@
     return paired.reshape((chips * 2 * block.shape[0],) + block.shape[1:])
 
 
-def col_scatter_sum(parts, groups):
+def col_scatter_sum(mine_part, other_part):
     chips = lax.axis_size("chip")
-    rows_each = parts.shape[0] // (2 * chips)
-    pieces = parts.reshape((groups, 2, chips // groups, rows_each) + parts.shape[1:])
-    mine = pieces[:, 0].reshape((chips, rows_each) + parts.shape[1:])
-    other = pieces[:, 1].reshape((chips, rows_each) + parts.shape[1:])
-    pair_sum = mine + lax.ppermute(other, "core", [(0, 1), (1, 0)])
+    shape = (chips, mine_part.shape[0] // chips) + mine_part.shape[1:]
+    swapped = lax.ppermute(other_part.reshape(shape), "core", [(0, 1), (1, 0)])
+    pair_sum = mine_part.reshape(shape) + swapped
     return lax.all_to_all(pair_sum, "chip", 0, 0, tiled=True).sum(axis=0)
 
 
@@ -200,13 +198,19 @@
     hidden_all = acts_all[:, :hidden_here]
     gate_grad_all = acts_all[:, hidden_here : 2 * hidden_here]
     up_grad_all = acts_all[:, 2 * hidden_here :]
-    output_term = apply_blocks(hidden_all, w_down, keep_down, "forward")
     down_weight_grad = apply_blocks(hidden_all, cotangent_all, keep_down, "weights")
     gate_weight_grad = apply_blocks(tokens_all, gate_grad_all, keep_gate, "weights")
     up_weight_grad = apply_blocks(tokens_all, up_grad_all, keep_up, "weights")
-    through_gate = apply_blocks(gate_grad_all, w_gate, keep_gate, "transposed")
-    through_up = apply_blocks(up_grad_all, w_up, keep_up, "transposed")
-    outs = col_scatter_sum(jnp.concatenate([output_term, through_gate + through_up], axis=1), groups)
+    by_core = acts_all.reshape((groups, 2, -1) + acts_all.shape[1:])
+
+    def sum_terms(rows):
+        rows = rows.reshape((-1,) + acts_all.shape[1:])
+        output_term = apply_blocks(rows[:, :hidden_here], w_down, keep_down, "forward")
+        through_gate = apply_blocks(rows[:, hidden_here : 2 * hidden_here], w_gate, keep_gate, "transposed")
+        through_up = apply_blocks(rows[:, 2 * hidden_here :], w_up, keep_up, "transposed")
+        return jnp.concatenate([output_term, through_gate + through_up], axis=1)
+
+    outs = col_scatter_sum(sum_terms(by_core[:, 0]), sum_terms(by_core[:, 1]))
     output = outs[:, :width_here].astype(jnp.bfloat16)
     input_grad = outs[:, width_here:]
     return (

time: 171 us -> 168 us (0.982)
  local copies, waits for them, and re-layouts: 14 us -> 11.7 us
    unnamed x42 -> x40, local copies, waits for them, and re-layouts: 10.1 us -> 8.02 us
  transfers between devices with their start and end apart: 19 -> 19, of which waited for: 13 -> 13; matrix products, arithmetic and copies ran while one was open for 10% -> 11% of each run, Pallas kernels for 0% -> 0%
where the time goes in v11:
time: 168 us
  waiting for transfers between devices  72.6 us (43%)
  starting transfers between devices  39 us (23%)
  blocking collectives  23.4 us (14%)
  matrix products  12.4 us (7%)
  local copies, waits for them, and re-layouts  11.7 us (7%)
  other arithmetic  7.23 us (4%)
    all_to_all x1, waiting for transfers between devices, col_scatter_sum(): return lax.all_to_all(pair_sum, 'chip', 0, 0, tiled=True).sum(axis=0)  24.1 us
    all_to_all x1, blocking collectives, col_gather(): mine = lax.all_to_all(spread, 'chip', 0, 0, tiled=True)  23.4 us
    ppermute x6, waiting for transfers between devices, joint_permute(): moved = lax.ppermute(jnp.concatenate(values, axis=1), axis_name, pairs)  22.3 us
    ppermute x6, starting transfers between devices, joint_permute(): moved = lax.ppermute(jnp.concatenate(values, axis=1), axis_name, pairs)  12.9 us
    ppermute x1, starting transfers between devices, col_scatter_sum(): swapped = lax.ppermute(other_part.reshape(shape), 'core', [(0, 1), (1, 0)])  8.22 us
    ppermute x3, waiting for transfers between devices, relay_gather(): carry_behind = lax.ppermute(carry_behind, axis_name, backward)  8.12 us
    unnamed x40, local copies, waits for them, and re-layouts  8.02 us
    ppermute x3, waiting for transfers between devices, relay_gather(): carry_ahead = lax.ppermute(carry_ahead, axis_name, forward)  7.65 us
  transfers between devices with their start and end apart: 19, of which 13 were waited for; matrix products, arithmetic and copies ran while one was open for 11% of the time, Pallas kernels for 0%

profile of v11, /device:TPU:1, one launch (start us, length us, event | category | flops | bytes accessed | tf_op | source)
XLA Modules:
  0.0 167.7 jit_solution(956457229173440027)
XLA Ops:
  1.6 23.4 %all_to_all.10 = bf16[16,16,2048]{2,1,0:T(8,128)(2,1)S(1)} all-to-all(bf16[16,16,2048]{2,1,0:T(8,128)(2,1)S(1)} %broadcast_in_dim.8), channel_id=1, replica_groups=mesh['row'=8,'chip'=16,'core'=2] {'chip'}, dimensions={0} | all-to-all | bytes 2097152 | tf_op jit(solution)/shard_map/all_to_all | solution.py:151
  25.0 2.1 %collective-permute-start = (bf16[16,16,2048]{2,1,0:T(8,128)(2,1)S(1)}, bf16[16,16,2048]{2,1,0:T(8,128)(2,1)}, u32[]{:S(2)}, u32[]{:S(2)}) collective-permute-start(bf16[16,16,2048]{2,1,0:T(8,128)(2,1)S(1)} %all_to_all.10), channel_id=1, source_target_pairs={{0,1},{1,0},{2,3},{3,2},{4,5},{5,4},{6,7},{7,6},{8,9},{9,8},{10,11... | collective-permute-start | bytes 3145736 | tf_op jit(solution)/shard_map/ppermute | solution.py:152
  30.1 2.5 %copy.17 = bf16[1024,512]{0,1:T(8,128)(2,1)} copy(bf16[1024,512]{1,0:T(8,128)(2,1)} %param.10) | data formatting | bytes 2097152 | tf_op args[2]
  39.8 5.7 %collective-permute-start.5 = (f32[64,1536]{1,0:T(8,128)S(1)}, f32[64,1536]{1,0:T(8,128)S(1)}, u32[]{:S(2)}, u32[]{:S(2)}) collective-permute-start(f32[64,1536]{1,0:T(8,128)S(1)} %pad_maximum_fusion.7), channel_id=1, source_target_pairs={{0,224},{32,0},{64,32},{96,64},{128,96},{160,128},{192,160},{224,1... | collective-permute-start | bytes 1179656 | tf_op jit(solution)/shard_map/ppermute | solution.py:81
  45.6 8.3 %collective-permute-done.5 = f32[64,1536]{1,0:T(8,128)S(1)} collective-permute-done((f32[64,1536]{1,0:T(8,128)S(1)}, f32[64,1536]{1,0:T(8,128)S(1)}, u32[]{:S(2)}, u32[]{:S(2)}) %collective-permute-start.5) | collective-permute-done | bytes 393248 | tf_op jit(solution)/shard_map/ppermute | solution.py:81
  54.0 3.5 %collective-permute-start.6 = (f32[64,1536]{1,0:T(8,128)S(1)}, f32[64,1536]{1,0:T(8,128)S(1)}, u32[]{:S(2)}, u32[]{:S(2)}) collective-permute-start(f32[64,1536]{1,0:T(8,128)S(1)} %pad_maximum_fusion.8), channel_id=1, source_target_pairs={{0,224},{32,0},{64,32},{96,64},{128,96},{160,128},{192,160},{224,1... | collective-permute-start | bytes 1179656 | tf_op jit(solution)/shard_map/ppermute | solution.py:81
  57.7 7.4 %collective-permute-done.6 = f32[64,1536]{1,0:T(8,128)S(1)} collective-permute-done((f32[64,1536]{1,0:T(8,128)S(1)}, f32[64,1536]{1,0:T(8,128)S(1)}, u32[]{:S(2)}, u32[]{:S(2)}) %collective-permute-start.6) | collective-permute-done | bytes 393248 | tf_op jit(solution)/shard_map/ppermute | solution.py:81
  65.2 3.5 %collective-permute-start.7 = (f32[64,1536]{1,0:T(8,128)S(1)}, f32[64,1536]{1,0:T(8,128)S(1)}, u32[]{:S(2)}, u32[]{:S(2)}) collective-permute-start(f32[64,1536]{1,0:T(8,128)S(1)} %pad_maximum_fusion.9), channel_id=1, source_target_pairs={{0,224},{32,0},{64,32},{96,64},{128,96},{160,128},{192,160},{224,1... | collective-permute-start | bytes 1179656 | tf_op jit(solution)/shard_map/ppermute | solution.py:81
  68.9 6.6 %collective-permute-done.7 = f32[64,1536]{1,0:T(8,128)S(1)} collective-permute-done((f32[64,1536]{1,0:T(8,128)S(1)}, f32[64,1536]{1,0:T(8,128)S(1)}, u32[]{:S(2)}, u32[]{:S(2)}) %collective-permute-start.7) | collective-permute-done | bytes 393248 | tf_op jit(solution)/shard_map/ppermute | solution.py:81
  75.5 3.7 %collective-permute-start.8 = (f32[64,768]{1,0:T(8,128)S(1)}, f32[64,768]{1,0:T(8,128)S(1)}, u32[]{:S(2)}, u32[]{:S(2)}) collective-permute-start(f32[64,768]{1,0:T(8,128)S(1)} %slice_add_fusion), channel_id=1, source_target_pairs={{0,224},{32,0},{64,32},{96,64},{128,96},{160,128},{192,160},{224,1... | collective-permute-start | bytes 589832 | tf_op jit(solution)/shard_map/ppermute | solution.py:79
  79.3 2.5 %collective-permute-done.8 = f32[64,768]{1,0:T(8,128)S(1)} collective-permute-done((f32[64,768]{1,0:T(8,128)S(1)}, f32[64,768]{1,0:T(8,128)S(1)}, u32[]{:S(2)}, u32[]{:S(2)}) %collective-permute-start.8) | collective-permute-done | bytes 196640 | tf_op jit(solution)/shard_map/ppermute | solution.py:79
  81.8 3.2 %collective-permute-done.4 = f32[64,768]{1,0:T(8,128)S(1)} collective-permute-done((f32[64,768]{1,0:T(8,128)S(1)}, f32[64,768]{1,0:T(8,128)S(1)}, u32[]{:S(2)}, u32[]{:S(2)}) %collective-permute-start.4) | collective-permute-done | bytes 196640 | tf_op jit(solution)/shard_map/ppermute | solution.py:79
  86.7 3.0 %collective-permute-done.9 = bf16[64,1536]{1,0:T(8,128)(2,1)S(1)} collective-permute-done((bf16[64,1536]{1,0:T(8,128)(2,1)S(1)}, bf16[64,1536]{1,0:T(8,128)(2,1)S(1)}, u32[]{:S(2)}, u32[]{:S(2)}) %collective-permute-start.9) | collective-permute-done | bytes 196640 | tf_op jit(solution)/shard_map/ppermute | solution.py:128
  91.5 5.1 %collective-permute-done.10 = bf16[64,1536]{1,0:T(8,128)(2,1)S(1)} collective-permute-done((bf16[64,1536]{1,0:T(8,128)(2,1)S(1)}, bf16[64,1536]{1,0:T(8,128)(2,1)S(1)}, u32[]{:S(2)}, u32[]{:S(2)}) %collective-permute-start.10) | collective-permute-done | bytes 196640 | tf_op jit(solution)/shard_map/ppermute | solution.py:128
  98.3 7.2 %collective-permute-done.14 = bf16[64,1536]{1,0:T(8,128)(2,1)S(1)} collective-permute-done((bf16[64,1536]{1,0:T(8,128)(2,1)S(1)}, bf16[64,1536]{1,0:T(8,128)(2,1)S(1)}, u32[]{:S(2)}, u32[]{:S(2)}) %collective-permute-start.14) | collective-permute-done | bytes 196640 | tf_op jit(solution)/shard_map/ppermute | solution.py:127
  105.6 2.7 %collective-permute-start.16 = (bf16[64,768]{1,0:T(8,128)(2,1)S(1)}, bf16[64,768]{1,0:T(8,128)(2,1)S(1)}, u32[]{:S(2)}, u32[]{:S(2)}) collective-permute-start(bf16[64,768]{1,0:T(8,128)(2,1)S(1)} %slice.239), channel_id=1, source_target_pairs={{0,224},{32,0},{64,32},{96,64},{128,96},{160,128},{192,160},{224,1... | collective-permute-start | bytes 294920 | tf_op jit(solution)/shard_map/ppermute | solution.py:135
  108.4 2.5 %collective-permute-done.15 = bf16[64,768]{1,0:T(8,128)(2,1)S(1)} collective-permute-done((bf16[64,768]{1,0:T(8,128)(2,1)S(1)}, bf16[64,768]{1,0:T(8,128)(2,1)S(1)}, u32[]{:S(2)}, u32[]{:S(2)}) %collective-permute-start.15) | collective-permute-done | bytes 98336 | tf_op jit(solution)/shard_map/ppermute | solution.py:134
  114.1 8.2 %collective-permute-start.17 = (f32[16,16,2048]{2,1,0:T(8,128)S(1)}, f32[16,16,2048]{2,1,0:T(8,128)S(1)}, u32[]{:S(2)}, u32[]{:S(2)}) collective-permute-start(f32[16,16,2048]{2,1,0:T(8,128)S(1)} %bitcast.85), channel_id=1, source_target_pairs={{0,1},{1,0},{2,3},{3,2},{4,5},{5,4},{6,7},{7,6},{8,9},{9,8},{10,11... | collective-permute-start | bytes 6291464 | tf_op jit(solution)/shard_map/ppermute | solution.py:161
  123.9 2.2 %collective-permute-done.17 = f32[16,16,2048]{2,1,0:T(8,128)S(1)} collective-permute-done((f32[16,16,2048]{2,1,0:T(8,128)S(1)}, f32[16,16,2048]{2,1,0:T(8,128)S(1)}, u32[]{:S(2)}, u32[]{:S(2)}) %collective-permute-start.17) | collective-permute-done | bytes 2097184 | tf_op jit(solution)/shard_map/ppermute | solution.py:161
  127.7 4.8 %all-to-all-start.1 = ((f32[16,16,2048]{2,1,0:T(8,128)}), f32[16,16,2048]{2,1,0:T(8,128)}, u32[]{:S(2)}, u32[]{:S(2)}) async-start(f32[16,16,2048]{2,1,0:T(8,128)} %add.301), calls=%async_computation.1 | async-start | bytes 4194304 | tf_op jit(solution)/shard_map/all_to_all | solution.py:163
  133.8 3.3 %convolution_select_fusion.1 = f32[1024,512]{1,0:T(8,128)} fusion(pred[1024,512]{1,0:T(32,128)(4,1)S(1)} %copy.20, bf16[512,2048]{1,0:T(8,128)(2,1)} %bitcast.82, bf16[512,1536]{1,0:T(8,128)(2,1)S(1)} %bitcast.75), kind=kOutput, calls=%fused_computation.5 | convolution fusion | flops 537395200 | bytes 4194304 | tf_op jit(solution)/shard_map/dot_general | solution.py:34
  137.1 2.1 %convolution_select_fusion.2 = f32[1024,512]{1,0:T(8,128)} fusion(pred[1024,512]{1,0:T(32,128)(4,1)S(1)} %copy.19, bf16[512,2048]{1,0:T(8,128)(2,1)S(1)} %bitcast.83, bf16[512,1536]{1,0:T(8,128)(2,1)S(1)} %bitcast.76), kind=kOutput, calls=%fused_computation.6 | convolution fusion | flops 537395200 | bytes 4194304 | tf_op jit(solution)/shard_map/dot_general | solution.py:34
  139.2 2.0 %convolution_select_fusion = f32[512,1024]{1,0:T(8,128)} fusion(pred[512,1024]{1,0:T(8,128)(4,1)S(1)} %bitcast.102, bf16[512,2048]{1,0:T(8,128)(2,1)S(1)} %bitcast.84, bf16[512,1536]{1,0:T(8,128)(2,1)S(1)} %bitcast.77), kind=kOutput, calls=%fused_computation.4 | convolution fusion | flops 537395200 | bytes 4194304 | tf_op jit(solution)/shard_map/dot_general | solution.py:34
  141.2 24.1 %all-to-all-done.1 = f32[16,16,2048]{2,1,0:T(8,128)} async-done(((f32[16,16,2048]{2,1,0:T(8,128)}), f32[16,16,2048]{2,1,0:T(8,128)}, u32[]{:S(2)}, u32[]{:S(2)}) %all-to-all-start.1) | async-done | bytes 2097184 | tf_op jit(solution)/shard_map/all_to_all | solution.py:163
  (122 shorter events, 26.8 us)
Async XLA Ops:
  0.6 26.5 %slice-start = ((s32[2048]{0:T(1024)}), s32[1024]{0:T(1024)S(1)}, s32[]{:S(2)}) async-start(s32[2048]{0:T(1024)} %param.13), calls=%async_computation.2 | async-start | bytes 8192 | tf_op jit(solution)/shard_map/slice | solution.py:15
  0.6 26.5 %slice-start.1 = ((s32[2048]{0:T(1024)}), s32[1024]{0:T(1024)S(1)}, s32[]{:S(2)}) async-start(s32[2048]{0:T(1024)} %param.14), calls=%async_computation.3 | async-start | bytes 8192 | tf_op jit(solution)/shard_map/slice | solution.py:15
  25.0 9.3 %collective-permute-start = (bf16[16,16,2048]{2,1,0:T(8,128)(2,1)S(1)}, bf16[16,16,2048]{2,1,0:T(8,128)(2,1)}, u32[]{:S(2)}, u32[]{:S(2)}) collective-permute-start(bf16[16,16,2048]{2,1,0:T(8,128)(2,1)S(1)} %all_to_all.10), channel_id=1, source_target_pairs={{0,1},{1,0},{2,3},{3,2},{4,5},{5,4},{6,7},{7,6},{8,9},{9,8},{10,11... | collective-permute-start | bytes 3145736 | tf_op jit(solution)/shard_map/ppermute | solution.py:152
  28.0 4.7 %slice-start.2 = ((s32[2048]{0:T(1024)}), s32[1024]{0:T(1024)S(1)}, s32[]{:S(2)}) async-start(s32[2048]{0:T(1024)} %param.15), calls=%async_computation.4 | async-start | bytes 8192 | tf_op jit(solution)/shard_map/slice | solution.py:15
  30.1 6.4 %copy-start.2 = (pred[64,8,4,256]{3,1,2,0:T(8,128)(4,1)}, pred[64,8,4,256]{3,1,2,0:T(8,128)(4,1)S(1)}, u32[]{:S(2)}) copy-start(pred[64,8,4,256]{3,1,2,0:T(8,128)(4,1)S(1)} %copy.21) | copy-start | bytes 1572868
  39.8 14.1 %collective-permute-start.5 = (f32[64,1536]{1,0:T(8,128)S(1)}, f32[64,1536]{1,0:T(8,128)S(1)}, u32[]{:S(2)}, u32[]{:S(2)}) collective-permute-start(f32[64,1536]{1,0:T(8,128)S(1)} %pad_maximum_fusion.7), channel_id=1, source_target_pairs={{0,224},{32,0},{64,32},{96,64},{128,96},{160,128},{192,160},{224,1... | collective-permute-start | bytes 1179656 | tf_op jit(solution)/shard_map/ppermute | solution.py:81
  45.5 12.0 %collective-permute-start.1 = (f32[64,1536]{1,0:T(8,128)S(1)}, f32[64,1536]{1,0:T(8,128)S(1)}, u32[]{:S(2)}, u32[]{:S(2)}) collective-permute-start(f32[64,1536]{1,0:T(8,128)S(1)} %pad_maximum_fusion.4), channel_id=1, source_target_pairs={{0,32},{32,64},{64,96},{96,128},{128,160},{160,192},{192,224},{224... | collective-permute-start | bytes 1179656 | tf_op jit(solution)/shard_map/ppermute | solution.py:81
  54.0 11.1 %collective-permute-start.6 = (f32[64,1536]{1,0:T(8,128)S(1)}, f32[64,1536]{1,0:T(8,128)S(1)}, u32[]{:S(2)}, u32[]{:S(2)}) collective-permute-start(f32[64,1536]{1,0:T(8,128)S(1)} %pad_maximum_fusion.8), channel_id=1, source_target_pairs={{0,224},{32,0},{64,32},{96,64},{128,96},{160,128},{192,160},{224,1... | collective-permute-start | bytes 1179656 | tf_op jit(solution)/shard_map/ppermute | solution.py:81
  57.6 11.1 %collective-permute-start.2 = (f32[64,1536]{1,0:T(8,128)S(1)}, f32[64,1536]{1,0:T(8,128)S(1)}, u32[]{:S(2)}, u32[]{:S(2)}) collective-permute-start(f32[64,1536]{1,0:T(8,128)S(1)} %pad_maximum_fusion.5), channel_id=1, source_target_pairs={{0,32},{32,64},{64,96},{96,128},{128,160},{160,192},{192,224},{224... | collective-permute-start | bytes 1179656 | tf_op jit(solution)/shard_map/ppermute | solution.py:81
  65.2 10.2 %collective-permute-start.7 = (f32[64,1536]{1,0:T(8,128)S(1)}, f32[64,1536]{1,0:T(8,128)S(1)}, u32[]{:S(2)}, u32[]{:S(2)}) collective-permute-start(f32[64,1536]{1,0:T(8,128)S(1)} %pad_maximum_fusion.9), channel_id=1, source_target_pairs={{0,224},{32,0},{64,32},{96,64},{128,96},{160,128},{192,160},{224,1... | collective-permute-start | bytes 1179656 | tf_op jit(solution)/shard_map/ppermute | solution.py:81
  68.8 10.4 %collective-permute-start.3 = (f32[64,1536]{1,0:T(8,128)S(1)}, f32[64,1536]{1,0:T(8,128)S(1)}, u32[]{:S(2)}, u32[]{:S(2)}) collective-permute-start(f32[64,1536]{1,0:T(8,128)S(1)} %pad_maximum_fusion.6), channel_id=1, source_target_pairs={{0,32},{32,64},{64,96},{96,128},{128,160},{160,192},{192,224},{224... | collective-permute-start | bytes 1179656 | tf_op jit(solution)/shard_map/ppermute | solution.py:81
  75.5 6.3 %collective-permute-start.8 = (f32[64,768]{1,0:T(8,128)S(1)}, f32[64,768]{1,0:T(8,128)S(1)}, u32[]{:S(2)}, u32[]{:S(2)}) collective-permute-start(f32[64,768]{1,0:T(8,128)S(1)} %slice_add_fusion), channel_id=1, source_target_pairs={{0,224},{32,0},{64,32},{96,64},{128,96},{160,128},{192,160},{224,1... | collective-permute-start | bytes 589832 | tf_op jit(solution)/shard_map/ppermute | solution.py:79
  79.2 5.8 %collective-permute-start.4 = (f32[64,768]{1,0:T(8,128)S(1)}, f32[64,768]{1,0:T(8,128)S(1)}, u32[]{:S(2)}, u32[]{:S(2)}) collective-permute-start(f32[64,768]{1,0:T(8,128)S(1)} %slice_add_fusion.7), channel_id=1, source_target_pairs={{0,32},{32,64},{64,96},{96,128},{128,160},{160,192},{192,224},{224... | collective-permute-start | bytes 589832 | tf_op jit(solution)/shard_map/ppermute | solution.py:79
  85.2 4.6 %collective-permute-start.9 = (bf16[64,1536]{1,0:T(8,128)(2,1)S(1)}, bf16[64,1536]{1,0:T(8,128)(2,1)S(1)}, u32[]{:S(2)}, u32[]{:S(2)}) collective-permute-start(bf16[64,1536]{1,0:T(8,128)(2,1)S(1)} %pad_maximum_fusion.10), channel_id=1, source_target_pairs={{0,224},{32,0},{64,32},{96,64},{128,96},{160,128},{192,160},{224,1... | collective-permute-start | bytes 589832 | tf_op jit(solution)/shard_map/ppermute | solution.py:128
  85.3 5.8 %collective-permute-start.12 = (bf16[64,1536]{1,0:T(8,128)(2,1)S(1)}, bf16[64,1536]{1,0:T(8,128)(2,1)S(1)}, u32[]{:S(2)}, u32[]{:S(2)}) collective-permute-start(bf16[64,1536]{1,0:T(8,128)(2,1)S(1)} %pad_maximum_fusion.10), channel_id=1, source_target_pairs={{0,32},{32,64},{64,96},{96,128},{128,160},{160,192},{192,224},{224... | collective-permute-start | bytes 589832 | tf_op jit(solution)/shard_map/ppermute | solution.py:127
  89.8 6.9 %collective-permute-start.10 = (bf16[64,1536]{1,0:T(8,128)(2,1)S(1)}, bf16[64,1536]{1,0:T(8,128)(2,1)S(1)}, u32[]{:S(2)}, u32[]{:S(2)}) collective-permute-start(bf16[64,1536]{1,0:T(8,128)(2,1)S(1)} %collective-permute-done.9), channel_id=1, source_target_pairs={{0,224},{32,0},{64,32},{96,64},{128,96},{160,128},{192,160},{224,1... | collective-permute-start | bytes 589832 | tf_op jit(solution)/shard_map/ppermute | solution.py:128
  91.1 6.6 %collective-permute-start.13 = (bf16[64,1536]{1,0:T(8,128)(2,1)S(1)}, bf16[64,1536]{1,0:T(8,128)(2,1)S(1)}, u32[]{:S(2)}, u32[]{:S(2)}) collective-permute-start(bf16[64,1536]{1,0:T(8,128)(2,1)S(1)} %collective-permute-done.12), channel_id=1, source_target_pairs={{0,32},{32,64},{64,96},{96,128},{128,160},{160,192},{192,224},{224... | collective-permute-start | bytes 589832 | tf_op jit(solution)/shard_map/ppermute | solution.py:127
  96.6 9.0 %collective-permute-start.11 = (bf16[64,1536]{1,0:T(8,128)(2,1)S(1)}, bf16[64,1536]{1,0:T(8,128)(2,1)S(1)}, u32[]{:S(2)}, u32[]{:S(2)}) collective-permute-start(bf16[64,1536]{1,0:T(8,128)(2,1)S(1)} %collective-permute-done.10), channel_id=1, source_target_pairs={{0,224},{32,0},{64,32},{96,64},{128,96},{160,128},{192,160},{224,1... | collective-permute-start | bytes 589832 | tf_op jit(solution)/shard_map/ppermute | solution.py:128
  97.6 7.9 %collective-permute-start.14 = (bf16[64,1536]{1,0:T(8,128)(2,1)S(1)}, bf16[64,1536]{1,0:T(8,128)(2,1)S(1)}, u32[]{:S(2)}, u32[]{:S(2)}) collective-permute-start(bf16[64,1536]{1,0:T(8,128)(2,1)S(1)} %collective-permute-done.13), channel_id=1, source_target_pairs={{0,32},{32,64},{64,96},{96,128},{128,160},{160,192},{192,224},{224... | collective-permute-start | bytes 589832 | tf_op jit(solution)/shard_map/ppermute | solution.py:127
  105.5 5.3 %collective-permute-start.15 = (bf16[64,768]{1,0:T(8,128)(2,1)S(1)}, bf16[64,768]{1,0:T(8,128)(2,1)S(1)}, u32[]{:S(2)}, u32[]{:S(2)}) collective-permute-start(bf16[64,768]{1,0:T(8,128)(2,1)S(1)} %slice.238), channel_id=1, source_target_pairs={{0,32},{32,64},{64,96},{96,128},{128,160},{160,192},{192,224},{224... | collective-permute-start | bytes 294920 | tf_op jit(solution)/shard_map/ppermute | solution.py:134
  105.6 5.2 %collective-permute-start.16 = (bf16[64,768]{1,0:T(8,128)(2,1)S(1)}, bf16[64,768]{1,0:T(8,128)(2,1)S(1)}, u32[]{:S(2)}, u32[]{:S(2)}) collective-permute-start(bf16[64,768]{1,0:T(8,128)(2,1)S(1)} %slice.239), channel_id=1, source_target_pairs={{0,224},{32,0},{64,32},{96,64},{128,96},{160,128},{192,160},{224,1... | collective-permute-start | bytes 294920 | tf_op jit(solution)/shard_map/ppermute | solution.py:135
  114.1 12.0 %collective-permute-start.17 = (f32[16,16,2048]{2,1,0:T(8,128)S(1)}, f32[16,16,2048]{2,1,0:T(8,128)S(1)}, u32[]{:S(2)}, u32[]{:S(2)}) collective-permute-start(f32[16,16,2048]{2,1,0:T(8,128)S(1)} %bitcast.85), channel_id=1, source_target_pairs={{0,1},{1,0},{2,3},{3,2},{4,5},{5,4},{6,7},{7,6},{8,9},{9,8},{10,11... | collective-permute-start | bytes 6291464 | tf_op jit(solution)/shard_map/ppermute | solution.py:161
  127.7 5.4 %copy-start.4 = (pred[64,8,4,256]{3,1,2,0:T(8,128)(4,1)S(1)}, pred[64,8,4,256]{3,1,2,0:T(8,128)(4,1)}, u32[]{:S(2)}) copy-start(pred[64,8,4,256]{3,1,2,0:T(8,128)(4,1)} %copy-done.2) | copy-start | bytes 1572868
  127.7 37.6 %all-to-all-start.1 = ((f32[16,16,2048]{2,1,0:T(8,128)}), f32[16,16,2048]{2,1,0:T(8,128)}, u32[]{:S(2)}, u32[]{:S(2)}) async-start(f32[16,16,2048]{2,1,0:T(8,128)} %add.301), calls=%async_computation.1 | async-start | bytes 4194304 | tf_op jit(solution)/shard_map/all_to_all | solution.py:163
  (10 other events, 20.5 us)

commit v12 on v11

--- a/solution.py
+++ b/solution.py
@@ -150,9 +150,7 @@
     spread = jnp.broadcast_to(block[None], (chips,) + block.shape)
     mine = lax.all_to_all(spread, "chip", 0, 0, tiled=True)
     other = lax.ppermute(mine, "core", [(0, 1), (1, 0)])
-    grouped = (groups, chips // groups) + block.shape
-    paired = jnp.stack([mine.reshape(grouped), other.reshape(grouped)], axis=1)
-    return paired.reshape((chips * 2 * block.shape[0],) + block.shape[1:])
+    return mine, other
 
 
 def col_scatter_sum(mine_part, other_part):
@@ -176,13 +174,25 @@
     keep_down = kept_table(order_down, col_start, row_start, cols_here, rows_here, width_blocks)
     width_here = tokens.shape[1]
     groups = lax.axis_size("row")
-    inputs_all = col_gather(jnp.concatenate([tokens, cotangent], axis=1), groups)
+    halves = col_gather(jnp.concatenate([tokens, cotangent], axis=1), groups)
+    grouped = (groups, 1, -1) + halves[0].shape[2:]
+    inputs_all = jnp.concatenate([h.reshape(grouped) for h in halves], axis=1)
+    inputs_all = inputs_all.reshape((-1,) + halves[0].shape[2:])
     tokens_all, cotangent_all = inputs_all[:, :width_here], inputs_all[:, width_here:]
-    gate_term = apply_blocks(tokens_all, w_gate, keep_gate, "forward")
-    up_term = apply_blocks(tokens_all, w_up, keep_up, "forward")
-    hidden_term = apply_blocks(cotangent_all, w_down, keep_down, "transposed")
     row_major = Layout(major_to_minor=(0, 1))
-    partials = [with_layout_constraint(t, row_major) for t in (gate_term, up_term, hidden_term)]
+
+    def partial_terms(half):
+        rows = half.reshape((-1,) + half.shape[2:])
+        terms = (
+            apply_blocks(rows[:, :width_here], w_gate, keep_gate, "forward"),
+            apply_blocks(rows[:, :width_here], w_up, keep_up, "forward"),
+            apply_blocks(rows[:, width_here:], w_down, keep_down, "transposed"),
+        )
+        joined = jnp.concatenate([with_layout_constraint(t, row_major) for t in terms], axis=1)
+        return joined.reshape((groups, 1, -1) + joined.shape[1:])
+
+    partial = jnp.concatenate([partial_terms(h) for h in halves], axis=1)
+    partials = [partial.reshape((-1,) + partial.shape[3:])]
     sums = relay_scatter_sum(jnp.concatenate(partials, axis=1), "row")
     gate = sums[:, :hidden_here]
     up = sums[:, hidden_here : 2 * hidden_here]

time: 168 us -> 162 us (0.964)
  blocking collectives: 23.4 us -> 0 us
  waiting for transfers between devices: 72.6 us -> 81.4 us
  starting transfers between devices: 39 us -> 47.4 us
    all_to_all x1 -> x0, blocking collectives: 23.4 us -> none  [col_gather(): mine = lax.all_to_all(spread, 'chip', 0, 0, tiled=True)]
    all_to_all x0 -> x1, waiting for transfers between devices: none -> 8.66 us  [col_gather(): mine = lax.all_to_all(spread, 'chip', 0, 0, tiled=True)]
    all_to_all x0 -> x1, starting transfers between devices: none -> 7.57 us  [col_gather(): mine = lax.all_to_all(spread, 'chip', 0, 0, tiled=True)]
    unnamed x40 -> x44, local copies, waits for them, and re-layouts: 8.02 us -> 8.07 us
  transfers between devices with their start and end apart: 19 -> 20, of which waited for: 13 -> 14; matrix products, arithmetic and copies ran while one was open for 11% -> 11% of each run, Pallas kernels for 0% -> 0%
where the time goes in v12:
time: 162 us; the launch traced here: 161 us
  waiting for transfers between devices  81.4 us (50%)
  starting transfers between devices  47.4 us (29%)
  local copies, waits for them, and re-layouts  12.6 us (8%)
  matrix products  11.9 us (7%)
  other arithmetic  6.31 us (4%)
    all_to_all x1, waiting for transfers between devices, col_scatter_sum(): return lax.all_to_all(pair_sum, 'chip', 0, 0, tiled=True).sum(axis=0)  24.9 us
    ppermute x6, waiting for transfers between devices, joint_permute(): moved = lax.ppermute(jnp.concatenate(values, axis=1), axis_name, pairs)  21.5 us
    ppermute x6, starting transfers between devices, joint_permute(): moved = lax.ppermute(jnp.concatenate(values, axis=1), axis_name, pairs)  12.9 us
    all_to_all x1, waiting for transfers between devices, col_gather(): mine = lax.all_to_all(spread, 'chip', 0, 0, tiled=True)  8.66 us
    ppermute x1, starting transfers between devices, col_scatter_sum(): swapped = lax.ppermute(other_part.reshape(shape), 'core', [(0, 1), (1, 0)])  8.36 us
    unnamed x44, local copies, waits for them, and re-layouts  8.07 us
    ppermute x3, waiting for transfers between devices, relay_gather(): carry_ahead = lax.ppermute(carry_ahead, axis_name, forward)  8.07 us
    ppermute x3, waiting for transfers between devices, relay_gather(): carry_behind = lax.ppermute(carry_behind, axis_name, backward)  7.97 us
  transfers between devices with their start and end apart: 20, of which 14 were waited for; matrix products, arithmetic and copies ran while one was open for 11% of the time, Pallas kernels for 0%

profile of v12, /device:TPU:1, one launch (start us, length us, event | category | flops | bytes accessed | tf_op | source)
XLA Modules:
  0.0 161.1 jit_solution(11189638655286781078)
XLA Ops:
  2.5 7.6 %all-to-all-start = ((bf16[16,16,2048]{2,1,0:T(8,128)(2,1)}), bf16[16,16,2048]{2,1,0:T(8,128)(2,1)S(1)}, u32[]{:S(2)}, u32[]{:S(2)}) async-start(bf16[16,16,2048]{2,1,0:T(8,128)(2,1)} %broadcast_in_dim.8), calls=%async_computation | async-start | bytes 2097152 | tf_op jit(solution)/shard_map/all_to_all | solution.py:151
  13.3 2.5 %copy.19 = bf16[1024,512]{0,1:T(8,128)(2,1)} copy(bf16[1024,512]{1,0:T(8,128)(2,1)} %param.10) | data formatting | bytes 2097152 | tf_op args[2]
  17.5 8.7 %all-to-all-done = bf16[16,16,2048]{2,1,0:T(8,128)(2,1)S(1)} async-done(((bf16[16,16,2048]{2,1,0:T(8,128)(2,1)}), bf16[16,16,2048]{2,1,0:T(8,128)(2,1)S(1)}, u32[]{:S(2)}, u32[]{:S(2)}) %all-to-all-start) | async-done | bytes 1048608 | tf_op jit(solution)/shard_map/all_to_all | solution.py:151
  26.2 2.6 %collective-permute-start = (bf16[16,16,2048]{2,1,0:T(8,128)(2,1)S(1)}, bf16[16,16,2048]{2,1,0:T(8,128)(2,1)S(1)}, u32[]{:S(2)}, u32[]{:S(2)}) collective-permute-start(bf16[16,16,2048]{2,1,0:T(8,128)(2,1)S(1)} %all-to-all-done), channel_id=1, source_target_pairs={{0,1},{1,0},{2,3},{3,2},{4,5},{5,4},{6,7},{7,6},{8,9},{9,8},{10,11... | collective-permute-start | bytes 3145736 | tf_op jit(solution)/shard_map/ppermute | solution.py:152
  33.5 5.7 %collective-permute-start.5 = (f32[64,1536]{1,0:T(8,128)S(1)}, f32[64,1536]{1,0:T(8,128)S(1)}, u32[]{:S(2)}, u32[]{:S(2)}) collective-permute-start(f32[64,1536]{1,0:T(8,128)S(1)} %pad_maximum_fusion.9), channel_id=1, source_target_pairs={{0,224},{32,0},{64,32},{96,64},{128,96},{160,128},{192,160},{224,1... | collective-permute-start | bytes 1179656 | tf_op jit(solution)/shard_map/ppermute | solution.py:81
  39.4 8.0 %collective-permute-done.5 = f32[64,1536]{1,0:T(8,128)S(1)} collective-permute-done((f32[64,1536]{1,0:T(8,128)S(1)}, f32[64,1536]{1,0:T(8,128)S(1)}, u32[]{:S(2)}, u32[]{:S(2)}) %collective-permute-start.5) | collective-permute-done | bytes 393248 | tf_op jit(solution)/shard_map/ppermute | solution.py:81
  47.5 3.5 %collective-permute-start.6 = (f32[64,1536]{1,0:T(8,128)S(1)}, f32[64,1536]{1,0:T(8,128)S(1)}, u32[]{:S(2)}, u32[]{:S(2)}) collective-permute-start(f32[64,1536]{1,0:T(8,128)S(1)} %pad_maximum_fusion.10), channel_id=1, source_target_pairs={{0,224},{32,0},{64,32},{96,64},{128,96},{160,128},{192,160},{224,1... | collective-permute-start | bytes 1179656 | tf_op jit(solution)/shard_map/ppermute | solution.py:81
  51.1 7.2 %collective-permute-done.6 = f32[64,1536]{1,0:T(8,128)S(1)} collective-permute-done((f32[64,1536]{1,0:T(8,128)S(1)}, f32[64,1536]{1,0:T(8,128)S(1)}, u32[]{:S(2)}, u32[]{:S(2)}) %collective-permute-start.6) | collective-permute-done | bytes 393248 | tf_op jit(solution)/shard_map/ppermute | solution.py:81
  58.4 3.5 %collective-permute-start.7 = (f32[64,1536]{1,0:T(8,128)S(1)}, f32[64,1536]{1,0:T(8,128)S(1)}, u32[]{:S(2)}, u32[]{:S(2)}) collective-permute-start(f32[64,1536]{1,0:T(8,128)S(1)} %pad_maximum_fusion.11), channel_id=1, source_target_pairs={{0,224},{32,0},{64,32},{96,64},{128,96},{160,128},{192,160},{224,1... | collective-permute-start | bytes 1179656 | tf_op jit(solution)/shard_map/ppermute | solution.py:81
  62.1 6.3 %collective-permute-done.7 = f32[64,1536]{1,0:T(8,128)S(1)} collective-permute-done((f32[64,1536]{1,0:T(8,128)S(1)}, f32[64,1536]{1,0:T(8,128)S(1)}, u32[]{:S(2)}, u32[]{:S(2)}) %collective-permute-start.7) | collective-permute-done | bytes 393248 | tf_op jit(solution)/shard_map/ppermute | solution.py:81
  68.4 3.7 %collective-permute-start.8 = (f32[64,768]{1,0:T(8,128)S(1)}, f32[64,768]{1,0:T(8,128)S(1)}, u32[]{:S(2)}, u32[]{:S(2)}) collective-permute-start(f32[64,768]{1,0:T(8,128)S(1)} %slice_add_fusion), channel_id=1, source_target_pairs={{0,224},{32,0},{64,32},{96,64},{128,96},{160,128},{192,160},{224,1... | collective-permute-start | bytes 589832 | tf_op jit(solution)/shard_map/ppermute | solution.py:79
  72.2 2.5 %collective-permute-done.8 = f32[64,768]{1,0:T(8,128)S(1)} collective-permute-done((f32[64,768]{1,0:T(8,128)S(1)}, f32[64,768]{1,0:T(8,128)S(1)}, u32[]{:S(2)}, u32[]{:S(2)}) %collective-permute-start.8) | collective-permute-done | bytes 196640 | tf_op jit(solution)/shard_map/ppermute | solution.py:79
  74.7 3.2 %collective-permute-done.4 = f32[64,768]{1,0:T(8,128)S(1)} collective-permute-done((f32[64,768]{1,0:T(8,128)S(1)}, f32[64,768]{1,0:T(8,128)S(1)}, u32[]{:S(2)}, u32[]{:S(2)}) %collective-permute-start.4) | collective-permute-done | bytes 196640 | tf_op jit(solution)/shard_map/ppermute | solution.py:79
  79.7 3.0 %collective-permute-done.9 = bf16[64,1536]{1,0:T(8,128)(2,1)S(1)} collective-permute-done((bf16[64,1536]{1,0:T(8,128)(2,1)S(1)}, bf16[64,1536]{1,0:T(8,128)(2,1)S(1)}, u32[]{:S(2)}, u32[]{:S(2)}) %collective-permute-start.9) | collective-permute-done | bytes 196640 | tf_op jit(solution)/shard_map/ppermute | solution.py:128
  84.5 4.9 %collective-permute-done.10 = bf16[64,1536]{1,0:T(8,128)(2,1)S(1)} collective-permute-done((bf16[64,1536]{1,0:T(8,128)(2,1)S(1)}, bf16[64,1536]{1,0:T(8,128)(2,1)S(1)}, u32[]{:S(2)}, u32[]{:S(2)}) %collective-permute-start.10) | collective-permute-done | bytes 196640 | tf_op jit(solution)/shard_map/ppermute | solution.py:128
  91.2 7.6 %collective-permute-done.14 = bf16[64,1536]{1,0:T(8,128)(2,1)S(1)} collective-permute-done((bf16[64,1536]{1,0:T(8,128)(2,1)S(1)}, bf16[64,1536]{1,0:T(8,128)(2,1)S(1)}, u32[]{:S(2)}, u32[]{:S(2)}) %collective-permute-start.14) | collective-permute-done | bytes 196640 | tf_op jit(solution)/shard_map/ppermute | solution.py:127
  99.0 2.7 %collective-permute-start.16 = (bf16[64,768]{1,0:T(8,128)(2,1)S(1)}, bf16[64,768]{1,0:T(8,128)(2,1)S(1)}, u32[]{:S(2)}, u32[]{:S(2)}) collective-permute-start(bf16[64,768]{1,0:T(8,128)(2,1)S(1)} %slice.259), channel_id=1, source_target_pairs={{0,224},{32,0},{64,32},{96,64},{128,96},{160,128},{192,160},{224,1... | collective-permute-start | bytes 294920 | tf_op jit(solution)/shard_map/ppermute | solution.py:135
  101.7 2.3 %collective-permute-done.15 = bf16[64,768]{1,0:T(8,128)(2,1)S(1)} collective-permute-done((bf16[64,768]{1,0:T(8,128)(2,1)S(1)}, bf16[64,768]{1,0:T(8,128)(2,1)S(1)}, u32[]{:S(2)}, u32[]{:S(2)}) %collective-permute-start.15) | collective-permute-done | bytes 98336 | tf_op jit(solution)/shard_map/ppermute | solution.py:134
  107.4 8.4 %collective-permute-start.17 = (f32[16,16,2048]{2,1,0:T(8,128)S(1)}, f32[16,16,2048]{2,1,0:T(8,128)S(1)}, u32[]{:S(2)}, u32[]{:S(2)}) collective-permute-start(f32[16,16,2048]{2,1,0:T(8,128)S(1)} %bitcast.93), channel_id=1, source_target_pairs={{0,1},{1,0},{2,3},{3,2},{4,5},{5,4},{6,7},{7,6},{8,9},{9,8},{10,11... | collective-permute-start | bytes 6291464 | tf_op jit(solution)/shard_map/ppermute | solution.py:159
  117.4 2.2 %collective-permute-done.17 = f32[16,16,2048]{2,1,0:T(8,128)S(1)} collective-permute-done((f32[16,16,2048]{2,1,0:T(8,128)S(1)}, f32[16,16,2048]{2,1,0:T(8,128)S(1)}, u32[]{:S(2)}, u32[]{:S(2)}) %collective-permute-start.17) | collective-permute-done | bytes 2097184 | tf_op jit(solution)/shard_map/ppermute | solution.py:159
  121.2 4.8 %all-to-all-start.1 = ((f32[16,16,2048]{2,1,0:T(8,128)}), f32[16,16,2048]{2,1,0:T(8,128)}, u32[]{:S(2)}, u32[]{:S(2)}) async-start(f32[16,16,2048]{2,1,0:T(8,128)} %add.301), calls=%async_computation.1 | async-start | bytes 4194304 | tf_op jit(solution)/shard_map/all_to_all | solution.py:161
  127.7 2.1 %convolution_select_fusion.1 = f32[1024,512]{1,0:T(8,128)} fusion(pred[1024,512]{1,0:T(32,128)(4,1)S(1)} %copy.24, bf16[512,2048]{1,0:T(8,128)(2,1)S(1)} %bitcast.94, bf16[512,1536]{1,0:T(8,128)(2,1)S(1)} %bitcast.84), kind=kOutput, calls=%fused_computation.5 | convolution fusion | flops 537395200 | bytes 4194304 | tf_op jit(solution)/shard_map/dot_general | solution.py:34
  129.8 2.1 %convolution_select_fusion.2 = f32[1024,512]{1,0:T(8,128)} fusion(pred[1024,512]{1,0:T(32,128)(4,1)S(1)} %copy.23, bf16[512,2048]{1,0:T(8,128)(2,1)S(1)} %bitcast.95, bf16[512,1536]{1,0:T(8,128)(2,1)S(1)} %bitcast.85), kind=kOutput, calls=%fused_computation.6 | convolution fusion | flops 537395200 | bytes 4194304 | tf_op jit(solution)/shard_map/dot_general | solution.py:34
  133.9 24.9 %all-to-all-done.1 = f32[16,16,2048]{2,1,0:T(8,128)} async-done(((f32[16,16,2048]{2,1,0:T(8,128)}), f32[16,16,2048]{2,1,0:T(8,128)}, u32[]{:S(2)}, u32[]{:S(2)}) %all-to-all-start.1) | async-done | bytes 2097184 | tf_op jit(solution)/shard_map/all_to_all | solution.py:161
  (132 shorter events, 29.8 us)
Async XLA Ops:
  0.6 9.7 %slice-start = ((s32[2048]{0:T(1024)}), s32[1024]{0:T(1024)S(1)}, s32[]{:S(2)}) async-start(s32[2048]{0:T(1024)} %param.13), calls=%async_computation.2 | async-start | bytes 8192 | tf_op jit(solution)/shard_map/slice | solution.py:15
  0.6 9.7 %slice-start.1 = ((s32[2048]{0:T(1024)}), s32[1024]{0:T(1024)S(1)}, s32[]{:S(2)}) async-start(s32[2048]{0:T(1024)} %param.14), calls=%async_computation.3 | async-start | bytes 8192 | tf_op jit(solution)/shard_map/slice | solution.py:15
  2.5 23.6 %all-to-all-start = ((bf16[16,16,2048]{2,1,0:T(8,128)(2,1)}), bf16[16,16,2048]{2,1,0:T(8,128)(2,1)S(1)}, u32[]{:S(2)}, u32[]{:S(2)}) async-start(bf16[16,16,2048]{2,1,0:T(8,128)(2,1)} %broadcast_in_dim.8), calls=%async_computation | async-start | bytes 2097152 | tf_op jit(solution)/shard_map/all_to_all | solution.py:151
  13.3 18.4 %copy-start.2 = (pred[64,8,4,256]{3,1,2,0:T(8,128)(4,1)}, pred[64,8,4,256]{3,1,2,0:T(8,128)(4,1)S(1)}, u32[]{:S(2)}) copy-start(pred[64,8,4,256]{3,1,2,0:T(8,128)(4,1)S(1)} %copy.25) | copy-start | bytes 1572868
  26.2 5.1 %collective-permute-start = (bf16[16,16,2048]{2,1,0:T(8,128)(2,1)S(1)}, bf16[16,16,2048]{2,1,0:T(8,128)(2,1)S(1)}, u32[]{:S(2)}, u32[]{:S(2)}) collective-permute-start(bf16[16,16,2048]{2,1,0:T(8,128)(2,1)S(1)} %all-to-all-done), channel_id=1, source_target_pairs={{0,1},{1,0},{2,3},{3,2},{4,5},{5,4},{6,7},{7,6},{8,9},{9,8},{10,11... | collective-permute-start | bytes 3145736 | tf_op jit(solution)/shard_map/ppermute | solution.py:152
  33.5 13.9 %collective-permute-start.5 = (f32[64,1536]{1,0:T(8,128)S(1)}, f32[64,1536]{1,0:T(8,128)S(1)}, u32[]{:S(2)}, u32[]{:S(2)}) collective-permute-start(f32[64,1536]{1,0:T(8,128)S(1)} %pad_maximum_fusion.9), channel_id=1, source_target_pairs={{0,224},{32,0},{64,32},{96,64},{128,96},{160,128},{192,160},{224,1... | collective-permute-start | bytes 1179656 | tf_op jit(solution)/shard_map/ppermute | solution.py:81
  39.3 11.7 %collective-permute-start.1 = (f32[64,1536]{1,0:T(8,128)S(1)}, f32[64,1536]{1,0:T(8,128)S(1)}, u32[]{:S(2)}, u32[]{:S(2)}) collective-permute-start(f32[64,1536]{1,0:T(8,128)S(1)} %pad_maximum_fusion.6), channel_id=1, source_target_pairs={{0,32},{32,64},{64,96},{96,128},{128,160},{160,192},{192,224},{224... | collective-permute-start | bytes 1179656 | tf_op jit(solution)/shard_map/ppermute | solution.py:81
  47.5 10.8 %collective-permute-start.6 = (f32[64,1536]{1,0:T(8,128)S(1)}, f32[64,1536]{1,0:T(8,128)S(1)}, u32[]{:S(2)}, u32[]{:S(2)}) collective-permute-start(f32[64,1536]{1,0:T(8,128)S(1)} %pad_maximum_fusion.10), channel_id=1, source_target_pairs={{0,224},{32,0},{64,32},{96,64},{128,96},{160,128},{192,160},{224,1... | collective-permute-start | bytes 1179656 | tf_op jit(solution)/shard_map/ppermute | solution.py:81
  51.1 10.8 %collective-permute-start.2 = (f32[64,1536]{1,0:T(8,128)S(1)}, f32[64,1536]{1,0:T(8,128)S(1)}, u32[]{:S(2)}, u32[]{:S(2)}) collective-permute-start(f32[64,1536]{1,0:T(8,128)S(1)} %pad_maximum_fusion.7), channel_id=1, source_target_pairs={{0,32},{32,64},{64,96},{96,128},{128,160},{160,192},{192,224},{224... | collective-permute-start | bytes 1179656 | tf_op jit(solution)/shard_map/ppermute | solution.py:81
  58.4 10.0 %collective-permute-start.7 = (f32[64,1536]{1,0:T(8,128)S(1)}, f32[64,1536]{1,0:T(8,128)S(1)}, u32[]{:S(2)}, u32[]{:S(2)}) collective-permute-start(f32[64,1536]{1,0:T(8,128)S(1)} %pad_maximum_fusion.11), channel_id=1, source_target_pairs={{0,224},{32,0},{64,32},{96,64},{128,96},{160,128},{192,160},{224,1... | collective-permute-start | bytes 1179656 | tf_op jit(solution)/shard_map/ppermute | solution.py:81
  62.0 10.1 %collective-permute-start.3 = (f32[64,1536]{1,0:T(8,128)S(1)}, f32[64,1536]{1,0:T(8,128)S(1)}, u32[]{:S(2)}, u32[]{:S(2)}) collective-permute-start(f32[64,1536]{1,0:T(8,128)S(1)} %pad_maximum_fusion.8), channel_id=1, source_target_pairs={{0,32},{32,64},{64,96},{96,128},{128,160},{160,192},{192,224},{224... | collective-permute-start | bytes 1179656 | tf_op jit(solution)/shard_map/ppermute | solution.py:81
  68.4 6.3 %collective-permute-start.8 = (f32[64,768]{1,0:T(8,128)S(1)}, f32[64,768]{1,0:T(8,128)S(1)}, u32[]{:S(2)}, u32[]{:S(2)}) collective-permute-start(f32[64,768]{1,0:T(8,128)S(1)} %slice_add_fusion), channel_id=1, source_target_pairs={{0,224},{32,0},{64,32},{96,64},{128,96},{160,128},{192,160},{224,1... | collective-permute-start | bytes 589832 | tf_op jit(solution)/shard_map/ppermute | solution.py:79
  72.1 5.8 %collective-permute-start.4 = (f32[64,768]{1,0:T(8,128)S(1)}, f32[64,768]{1,0:T(8,128)S(1)}, u32[]{:S(2)}, u32[]{:S(2)}) collective-permute-start(f32[64,768]{1,0:T(8,128)S(1)} %slice_add_fusion.7), channel_id=1, source_target_pairs={{0,32},{32,64},{64,96},{96,128},{128,160},{160,192},{192,224},{224... | collective-permute-start | bytes 589832 | tf_op jit(solution)/shard_map/ppermute | solution.py:79
  78.1 4.6 %collective-permute-start.9 = (bf16[64,1536]{1,0:T(8,128)(2,1)S(1)}, bf16[64,1536]{1,0:T(8,128)(2,1)S(1)}, u32[]{:S(2)}, u32[]{:S(2)}) collective-permute-start(bf16[64,1536]{1,0:T(8,128)(2,1)S(1)} %pad_maximum_fusion.12), channel_id=1, source_target_pairs={{0,224},{32,0},{64,32},{96,64},{128,96},{160,128},{192,160},{224,1... | collective-permute-start | bytes 589832 | tf_op jit(solution)/shard_map/ppermute | solution.py:128
  78.2 5.8 %collective-permute-start.12 = (bf16[64,1536]{1,0:T(8,128)(2,1)S(1)}, bf16[64,1536]{1,0:T(8,128)(2,1)S(1)}, u32[]{:S(2)}, u32[]{:S(2)}) collective-permute-start(bf16[64,1536]{1,0:T(8,128)(2,1)S(1)} %pad_maximum_fusion.12), channel_id=1, source_target_pairs={{0,32},{32,64},{64,96},{96,128},{128,160},{160,192},{192,224},{224... | collective-permute-start | bytes 589832 | tf_op jit(solution)/shard_map/ppermute | solution.py:127
  82.7 6.7 %collective-permute-start.10 = (bf16[64,1536]{1,0:T(8,128)(2,1)S(1)}, bf16[64,1536]{1,0:T(8,128)(2,1)S(1)}, u32[]{:S(2)}, u32[]{:S(2)}) collective-permute-start(bf16[64,1536]{1,0:T(8,128)(2,1)S(1)} %collective-permute-done.9), channel_id=1, source_target_pairs={{0,224},{32,0},{64,32},{96,64},{128,96},{160,128},{192,160},{224,1... | collective-permute-start | bytes 589832 | tf_op jit(solution)/shard_map/ppermute | solution.py:128
  84.0 6.8 %collective-permute-start.13 = (bf16[64,1536]{1,0:T(8,128)(2,1)S(1)}, bf16[64,1536]{1,0:T(8,128)(2,1)S(1)}, u32[]{:S(2)}, u32[]{:S(2)}) collective-permute-start(bf16[64,1536]{1,0:T(8,128)(2,1)S(1)} %collective-permute-done.12), channel_id=1, source_target_pairs={{0,32},{32,64},{64,96},{96,128},{128,160},{160,192},{192,224},{224... | collective-permute-start | bytes 589832 | tf_op jit(solution)/shard_map/ppermute | solution.py:127
  89.4 9.5 %collective-permute-start.11 = (bf16[64,1536]{1,0:T(8,128)(2,1)S(1)}, bf16[64,1536]{1,0:T(8,128)(2,1)S(1)}, u32[]{:S(2)}, u32[]{:S(2)}) collective-permute-start(bf16[64,1536]{1,0:T(8,128)(2,1)S(1)} %collective-permute-done.10), channel_id=1, source_target_pairs={{0,224},{32,0},{64,32},{96,64},{128,96},{160,128},{192,160},{224,1... | collective-permute-start | bytes 589832 | tf_op jit(solution)/shard_map/ppermute | solution.py:128
  90.8 8.0 %collective-permute-start.14 = (bf16[64,1536]{1,0:T(8,128)(2,1)S(1)}, bf16[64,1536]{1,0:T(8,128)(2,1)S(1)}, u32[]{:S(2)}, u32[]{:S(2)}) collective-permute-start(bf16[64,1536]{1,0:T(8,128)(2,1)S(1)} %collective-permute-done.13), channel_id=1, source_target_pairs={{0,32},{32,64},{64,96},{96,128},{128,160},{160,192},{192,224},{224... | collective-permute-start | bytes 589832 | tf_op jit(solution)/shard_map/ppermute | solution.py:127
  98.8 5.2 %collective-permute-start.15 = (bf16[64,768]{1,0:T(8,128)(2,1)S(1)}, bf16[64,768]{1,0:T(8,128)(2,1)S(1)}, u32[]{:S(2)}, u32[]{:S(2)}) collective-permute-start(bf16[64,768]{1,0:T(8,128)(2,1)S(1)} %slice.258), channel_id=1, source_target_pairs={{0,32},{32,64},{64,96},{96,128},{128,160},{160,192},{192,224},{224... | collective-permute-start | bytes 294920 | tf_op jit(solution)/shard_map/ppermute | solution.py:134
  99.0 5.1 %collective-permute-start.16 = (bf16[64,768]{1,0:T(8,128)(2,1)S(1)}, bf16[64,768]{1,0:T(8,128)(2,1)S(1)}, u32[]{:S(2)}, u32[]{:S(2)}) collective-permute-start(bf16[64,768]{1,0:T(8,128)(2,1)S(1)} %slice.259), channel_id=1, source_target_pairs={{0,224},{32,0},{64,32},{96,64},{128,96},{160,128},{192,160},{224,1... | collective-permute-start | bytes 294920 | tf_op jit(solution)/shard_map/ppermute | solution.py:135
  107.4 12.1 %collective-permute-start.17 = (f32[16,16,2048]{2,1,0:T(8,128)S(1)}, f32[16,16,2048]{2,1,0:T(8,128)S(1)}, u32[]{:S(2)}, u32[]{:S(2)}) collective-permute-start(f32[16,16,2048]{2,1,0:T(8,128)S(1)} %bitcast.93), channel_id=1, source_target_pairs={{0,1},{1,0},{2,3},{3,2},{4,5},{5,4},{6,7},{7,6},{8,9},{9,8},{10,11... | collective-permute-start | bytes 6291464 | tf_op jit(solution)/shard_map/ppermute | solution.py:159
  121.2 5.4 %copy-start.4 = (pred[64,8,4,256]{3,1,2,0:T(8,128)(4,1)S(1)}, pred[64,8,4,256]{3,1,2,0:T(8,128)(4,1)}, u32[]{:S(2)}) copy-start(pred[64,8,4,256]{3,1,2,0:T(8,128)(4,1)} %copy-done.2) | copy-start | bytes 1572868
  121.2 37.6 %all-to-all-start.1 = ((f32[16,16,2048]{2,1,0:T(8,128)}), f32[16,16,2048]{2,1,0:T(8,128)}, u32[]{:S(2)}, u32[]{:S(2)}) async-start(f32[16,16,2048]{2,1,0:T(8,128)} %add.301), calls=%async_computation.1 | async-start | bytes 4194304 | tf_op jit(solution)/shard_map/all_to_all | solution.py:161
  (13 other events, 24.1 us)
